TPU v7x, 128 devices: a whole 4x4x4 slice. The times are simulated.
128 devices in a mesh: blk: 32 (over y, x, core), grp: 4 (over z).
Axes of the slice: x: 4, y: 4, z: 4, core: 2. Of those that a mesh axis runs over, the one named last changes fastest.
Arguments:
- sky_map: bfloat16 [256, 1048576], P(None, ('blk', 'grp')), may hold values from -128 to 128
- fg_templates: bfloat16 [256, 16], replicated, may hold values from -0.375 to 0.375
- cycle_len: int32 [512], P(('blk', 'grp')), may hold values from 512 to 2048, as said below
- beam_profile: float32 [8, 1024], replicated, may hold values from 0.2 to 2
- beam_index: int32 [256], P('blk'), may hold values from 0 to 7
Outputs:
- filtered: float32 [1024, 256, 2, 1024], P(None, 'blk', None, 'grp')
Inputs may be any that keep to these rules, and one draw needn't show every extreme that they name: `cycle_len`: some cycle has exactly 2048 pixels.
All inputs are finite; a program needn't handle non-finite values.
Results may differ from a plain program's by a relative error of at most 0.0064.
Values may be sent and summed in bfloat16 or wider, within the bound.
No kernel may reach another device: no remote copies, remote signals or barrier semaphores. Data moves between devices by JAX's collectives and lax.ppermute only.
A program may use at most 192 MiB of HBM per device.

v0:
```python
import jax
import jax.numpy as jnp
from jax import lax
from jax.sharding import PartitionSpec as P
from jax.experimental import pallas as pl
from jax.experimental.pallas import tpu as pltpu

RPIX = 2048
L = 1024
M_DEV = 256
J_LO = 128


def cos_sin_of_phase(phase, length):
    angle = jnp.pi * phase.astype(jnp.float32) / length.astype(jnp.float32)
    return jnp.cos(angle), jnp.sin(angle)


def add_angles(ca, sa, cb, sb):
    return ca * cb - sa * sb, sa * cb + ca * sb


def small_tables(cycle_len, m_width):
    length = cycle_len[:, None, None]
    period = 2 * length
    orders = jnp.arange(m_width, dtype=jnp.int32)[None, None, :]
    j_hi = jnp.arange(RPIX // J_LO, dtype=jnp.int32)[None, :, None]
    j_mid = jnp.arange(J_LO // 16, dtype=jnp.int32)[None, :, None]
    j_q = jnp.arange(16, dtype=jnp.int32)[None, :, None]
    ca, sa = cos_sin_of_phase((2 * J_LO * j_hi) % period * orders % period, length)
    cm, sm = cos_sin_of_phase((32 * j_mid) % period * orders % period, length)
    cq, sq = cos_sin_of_phase(orders * (2 * j_q + 1) % period, length)
    cb, sb = add_angles(cm[:, :, None, :], sm[:, :, None, :], cq[:, None, :, :], sq[:, None, :, :])
    n_cyc = cycle_len.shape[0]
    cb = cb.reshape(n_cyc, J_LO, m_width)
    sb = sb.reshape(n_cyc, J_LO, m_width)
    return ca, sa, cb, sb


def fourier_kernel(ca_ref, sa_ref, cb_ref, sb_ref, inv_ref, len_ref, x_ref, o_ref, tab_ref):
    m_width = cb_ref.shape[2]
    inv = inv_ref[0][:, 0:1]
    length = len_ref[0][:, 0:1]

    def build(t, carry):
        ca = ca_ref[0, pl.ds(t, 1), :]
        sa = sa_ref[0, pl.ds(t, 1), :]
        cb = cb_ref[0]
        sb = sb_ref[0]
        rows = t * J_LO + lax.broadcasted_iota(jnp.int32, (J_LO, 1), 0)
        weight = jnp.where(rows < length, inv, 0.0)
        cos_t, sin_t = add_angles(ca, sa, cb, sb)
        r0 = pl.multiple_of(t * J_LO, J_LO)
        tab_ref[pl.ds(r0, J_LO), 0:m_width] = (cos_t * weight).astype(jnp.bfloat16)
        tab_ref[pl.ds(r0, J_LO), m_width : 2 * m_width] = (-sin_t * weight).astype(jnp.bfloat16)
        return carry

    lax.fori_loop(0, RPIX // J_LO, build, 0)
    width = 2 * m_width
    step = 512
    for q in range(width // step):
        o_ref[0, :, q * step : (q + 1) * step] = jnp.dot(
            x_ref[...], tab_ref[:, q * step : (q + 1) * step], preferred_element_type=jnp.float32
        ).astype(jnp.bfloat16)


def cycle_fourier(cleaned, cycle_len, m_width):
    n_cyc = cycle_len.shape[0]
    n_chan = cleaned.shape[0]
    ca, sa, cb, sb = small_tables(cycle_len, m_width)
    inv = jnp.broadcast_to(lax.rsqrt(cycle_len.astype(jnp.float32))[:, None, None], (n_cyc, 1, 128))
    lens = jnp.broadcast_to(cycle_len[:, None, None], (n_cyc, 1, 128))
    n_hi = RPIX // J_LO
    return pl.pallas_call(
        fourier_kernel,
        grid=(n_cyc,),
        in_specs=[
            pl.BlockSpec((1, n_hi, m_width), lambda k: (k, 0, 0)),
            pl.BlockSpec((1, n_hi, m_width), lambda k: (k, 0, 0)),
            pl.BlockSpec((1, J_LO, m_width), lambda k: (k, 0, 0)),
            pl.BlockSpec((1, J_LO, m_width), lambda k: (k, 0, 0)),
            pl.BlockSpec((1, 1, 128), lambda k: (k, 0, 0)),
            pl.BlockSpec((1, 1, 128), lambda k: (k, 0, 0)),
            pl.BlockSpec((n_chan, RPIX), lambda k: (0, k)),
        ],
        out_specs=pl.BlockSpec((1, n_chan, 2 * m_width), lambda k: (k, 0, 0)),
        out_shape=jax.ShapeDtypeStruct((n_cyc, n_chan, 2 * m_width), jnp.bfloat16),
        scratch_shapes=[pltpu.VMEM((RPIX, 2 * m_width), jnp.bfloat16)],
        compiler_params=pltpu.CompilerParams(vmem_limit_bytes=48 * 1024 * 1024),
    )(ca, sa, cb, sb, inv, lens, cleaned)


def theta_table(cycle_ids, n_cycle):
    degrees = jnp.arange(L, dtype=jnp.int32)
    odd = 2 * cycle_ids + 1
    phase = degrees[:, None] * odd[None, :] % (4 * n_cycle)
    angle = jnp.pi * phase.astype(jnp.float32) / (2.0 * n_cycle)
    weight = jnp.sin(jnp.pi * odd.astype(jnp.float32) / (2.0 * n_cycle)) * (
        2.0 / jnp.sqrt(jnp.float32(n_cycle))
    )
    return (jnp.cos(angle) * weight[None, :]).astype(jnp.bfloat16)


def sub_axes(n_blk, n_grp):
    return [
        ("blk", 2, 1, n_blk),
        ("blk", 4, 2, n_blk),
        ("blk", n_blk // 8, 8, n_blk),
        ("grp", n_grp, 1, n_grp),
    ]


def shift_perm(size, stride, total, k):
    pairs = []
    for i in range(total):
        c = (i // stride) % size
        pairs.append((i, i + ((c + k) % size - c) * stride))
    return pairs


def ring_sum(v, subs):
    for axis, size, stride, total in subs:
        parts = [lax.ppermute(v, axis, shift_perm(size, stride, total, k)) for k in range(1, size)]
        for part in parts:
            v = v + part
    return v


def body(sky_map, fg_templates, cycle_len, beam_profile, beam_index):
    n_blk = lax.axis_size("blk")
    n_grp = lax.axis_size("grp")
    cycle_dev = cycle_len.shape[0]
    n_chan = sky_map.shape[0]
    n_mode = fg_templates.shape[1]
    chan_dev = n_chan // n_blk
    m_width = M_DEV * n_grp
    n_cycle = cycle_dev * n_blk * n_grp
    slots = jnp.arange(RPIX, dtype=jnp.int32)
    valid = (slots[None, :] < cycle_len[:, None]).reshape(-1)
    masked = jnp.where(valid[None, :], sky_map, jnp.zeros((), jnp.bfloat16))
    mode_amps = jnp.dot(fg_templates.T, masked, preferred_element_type=jnp.float32).astype(
        jnp.bfloat16
    )
    gram_part = jnp.dot(mode_amps, mode_amps.T, preferred_element_type=jnp.float32)
    cross_part = lax.dot_general(
        mode_amps, masked, (((1,), (1,)), ((), ())), preferred_element_type=jnp.float32
    )
    amps_wide = mode_amps.astype(jnp.float32)
    subs = sub_axes(n_blk, n_grp)
    sums = ring_sum(jnp.concatenate([gram_part, cross_part], axis=1), subs)
    gram_sum = sums[:, :n_mode]
    cross_sum = sums[:, n_mode:]
    lower = jnp.linalg.cholesky(gram_sum)
    basis = jax.scipy.linalg.solve_triangular(lower, amps_wide, lower=True)
    projected = jax.scipy.linalg.solve_triangular(lower, cross_sum, lower=True)
    correction = jnp.dot(projected.T, basis, precision=lax.Precision.HIGHEST)
    cleaned = (masked.astype(jnp.float32) - correction).astype(jnp.bfloat16)
    fourier = cycle_fourier(cleaned, cycle_len, m_width)
    fourier = fourier.reshape(cycle_dev, n_blk, chan_dev, 2, n_grp, M_DEV)
    sendbuf = fourier.transpose(1, 4, 0, 2, 3, 5).reshape(
        n_blk * n_grp, cycle_dev, chan_dev, 2, M_DEV
    )
    moved = lax.all_to_all(sendbuf, ("blk", "grp"), 0, 0, tiled=True)
    moved = moved.reshape(n_cycle, chan_dev * 2 * M_DEV)
    theta_tab = theta_table(jnp.arange(n_cycle, dtype=jnp.int32), n_cycle)
    harmonic = jnp.dot(theta_tab, moved, preferred_element_type=jnp.float32).reshape(
        L, chan_dev, 2, M_DEV
    )
    onehot = (
        beam_index[:, None] == jnp.arange(beam_profile.shape[0], dtype=jnp.int32)[None, :]
    ).astype(jnp.float32)
    profiles = jnp.dot(onehot, beam_profile, precision=lax.Precision.HIGHEST)
    shaped = harmonic * profiles.T[:, :, None, None]
    orders = lax.axis_index("grp") * M_DEV + jnp.arange(M_DEV, dtype=jnp.int32)
    mweight = 0.25 + orders.astype(jnp.float32) / m_width
    weighted = shaped * mweight[None, None, None, :]
    power_part = jnp.sum(weighted * weighted, axis=(0, 2, 3))
    power = ring_sum(power_part, subs[3:])
    return weighted * lax.rsqrt(power / (2.0 * L * m_width) + 1e-06)[None, :, None, None]


def solution(mesh):
    return jax.shard_map(
        body,
        mesh=mesh,
        in_specs=(P(None, ("blk", "grp")), P(), P(("blk", "grp")), P(), P("blk")),
        out_specs=P(None, "blk", None, "grp"),
        check_vma=False,
    )
```

profile of v0, /device:TPU:0, one launch (start us, length us, event | category | flops | bytes accessed | tf_op | source)
XLA Modules:
  0.0 232.3 jit_solution(13375940199783110813)
XLA Ops:
  0.9 3.1 %convolution_convert_fusion = bf16[8192,16]{0,1:T(8,128)(2,1)S(1)} fusion(bf16[256,16]{0,1:T(8,128)(2,1)} %param.6, bf16[256,8192]{1,0:T(8,128)(2,1)} %param.5, pred[8192]{0:T(1024)(128)(4,1)S(1)} %bitcast.46), kind=kOutput, calls=%fused_computation.5 | convolution fusion | flops 69337088 | bytes 4472832 | tf_op jit(solution)/shard_map/dot_general | solution.py:141
  6.1 7.0 %fusion.45 = (f32[4,16,1024]{2,1,0:T(8,128)S(1)}, f32[4,16,1024]{2,1,0:T(8,128)S(1)}, f32[4,16,1024]{2,1,0:T(8,128)S(1)}, f32[4,16,1024]{2,1,0:T(8,128)S(1)}) fusion(f32[4]{0:T(128)S(1)} %get-tuple-element.16, pred[4]{0:T(512)(128)(4,1)S(1)} %broadcast_compare_fusion, s32[4]{0:T(128)S(1)} %get-tuple-element.15, s32[16,1024]{1,0:T(8,128)S(1)} %iota_multiply_fusion, ...), kind=kLoop, calls=%fused_computation.66 | loop fusion | flops 1376256 | bytes 1114404 | tf_op jit(solution)/shard_map/cos | solution.py:16
  13.3 2.9 %collective-permute-start.3 = (f32[16,272]{0,1:T(8,128)S(1)}, f32[16,272]{0,1:T(8,128)S(1)}, u32[]{:S(2)}, u32[]{:S(2)}) collective-permute-start(f32[16,272]{0,1:T(8,128)S(1)} %add.196), channel_id=1, source_target_pairs={{0,24},{4,28},{8,0},{12,4},{16,8},{20,12},{24,16},{28,20},{32,56},... | collective-permute-start | bytes 52232 | tf_op jit(solution)/shard_map/ppermute | solution.py:123
  19.7 3.0 %collective-permute-done.3 = f32[16,272]{0,1:T(8,128)S(1)} collective-permute-done((f32[16,272]{0,1:T(8,128)S(1)}, f32[16,272]{0,1:T(8,128)S(1)}, u32[]{:S(2)}, u32[]{:S(2)}) %collective-permute-start.3) | collective-permute-done | bytes 17440 | tf_op jit(solution)/shard_map/ppermute | solution.py:123
  24.3 2.2 collective-permute-done.1
  26.5 3.1 %collective-permute-start.6 = (f32[16,272]{0,1:T(8,128)S(1)}, f32[16,272]{0,1:T(8,128)S(1)}, u32[]{:S(2)}, u32[]{:S(2)}) collective-permute-start(f32[16,272]{0,1:T(8,128)S(1)} %add_add_fusion.2), channel_id=1, source_target_pairs={{0,96},{4,100},{8,104},{12,108},{16,112},{20,116},{24,120},{28,124... | collective-permute-start | bytes 52232 | tf_op jit(solution)/shard_map/ppermute | solution.py:123
  31.2 2.0 multiply_add_fusion
  33.2 2.5 %collective-permute-done.6 = f32[16,272]{0,1:T(8,128)S(1)} collective-permute-done((f32[16,272]{0,1:T(8,128)S(1)}, f32[16,272]{0,1:T(8,128)S(1)}, u32[]{:S(2)}, u32[]{:S(2)}) %collective-permute-start.6) | collective-permute-done | bytes 17440 | tf_op jit(solution)/shard_map/ppermute | solution.py:123
  35.7 2.0 collective-permute-done.5
  39.4 4.1 %collective-permute-start.9 = (f32[16,272]{0,1:T(8,128)S(1)}, f32[16,272]{0,1:T(8,128)S(1)}, u32[]{:S(2)}, u32[]{:S(2)}) collective-permute-start(f32[16,272]{0,1:T(8,128)S(1)} %add_add_fusion.1), channel_id=1, source_target_pairs={{0,3},{1,0},{2,1},{3,2},{4,7},{5,4},{6,5},{7,6},{8,11},{9,8},{10,9... | collective-permute-start | bytes 52232 | tf_op jit(solution)/shard_map/ppermute | solution.py:123
  44.8 4.8 %collective-permute-done.9 = f32[16,272]{0,1:T(8,128)S(1)} collective-permute-done((f32[16,272]{0,1:T(8,128)S(1)}, f32[16,272]{0,1:T(8,128)S(1)}, u32[]{:S(2)}, u32[]{:S(2)}) %collective-permute-start.9) | collective-permute-done | bytes 17440 | tf_op jit(solution)/shard_map/ppermute | solution.py:123
  49.6 1.9 collective-permute-done.8
  57.9 10.3 %fusion.1.x_ref = bf16[256,8192]{1,0:T(8,128)(2,1)} fusion(f32[16,256]{1,0:T(8,128)S(1)} %fusion.38, f32[16,8192]{1,0:T(8,128)S(1)} %fusion.52, bf16[256,8192]{1,0:T(8,128)(2,1)} %param.5, pred[8192]{0:T(1024)(128)(4,1)S(1)} %bitcast.48), kind=kOutput, calls=%fused_computation.4 | convolution fusion | flops 411041792 | bytes 8937472 | tf_op jit(solution)/shard_map/dot_general | solution.py:156
  68.4 24.6 %shard_map.55 = bf16[4,256,2048]{2,1,0:T(8,128)(2,1)} custom-call(f32[4,16,1024]{2,1,0:T(8,128)S(1)} %get-tuple-element.13.ca_ref, f32[4,16,1024]{2,1,0:T(8,128)S(1)} %get-tuple-element.14.sa_ref, f32[4,128,1024]{2,1,0:T(8,128)S(1)} %bitcast.41, f32[4,128,1024]{2,1,0:T(8,128)S(1)} %bitcast.40, f32[4,1,128]{2,1,0:T(1,128)S(1)} %broadcast_in_dim.18.inv_ref, ...), custom_call_target="tpu_custom_call" | custom-call | tf_op jit(solution)/shard_map/pallas_call | solution.py:74
  92.9 4.8 %copy.20 = bf16[4,32,8,2,4,256]{5,2,3,0,4,1:T(8,128)(2,1)} copy(bf16[4,32,8,2,4,256]{5,2,4,3,1,0:T(8,128)(2,1)} %bitcast.43) | data formatting | bytes 8388608 | tf_op jit(solution)/shard_map/reshape | solution.py:159
  97.7 6.2 %all-to-all-start = ((bf16[128,4,8,2,256]{4,2,3,1,0:T(8,128)(2,1)}), bf16[128,4,8,2,256]{4,2,3,1,0:T(8,128)(2,1)}, u32[]{:S(2)}, u32[]{:S(2)}) async-start(bf16[128,4,8,2,256]{4,2,3,1,0:T(8,128)(2,1)} %bitcast.42), calls=%async_computation | async-start | bytes 8388608 | tf_op jit(solution)/shard_map/all_to_all | solution.py:163
  104.2 50.9 %all-to-all-done = bf16[128,4,8,2,256]{4,2,3,1,0:T(8,128)(2,1)} async-done(((bf16[128,4,8,2,256]{4,2,3,1,0:T(8,128)(2,1)}), bf16[128,4,8,2,256]{4,2,3,1,0:T(8,128)(2,1)}, u32[]{:S(2)}, u32[]{:S(2)}) %all-to-all-start) | async-done | bytes 4194336 | tf_op jit(solution)/shard_map/all_to_all | solution.py:163
  155.1 9.5 %copy.21 = bf16[128,4,8,2,256]{4,3,2,1,0:T(2,128)(2,1)} copy(bf16[128,4,8,2,256]{4,2,3,1,0:T(8,128)(2,1)} %all-to-all-done) | data formatting | bytes 8388608 | tf_op jit(solution)/shard_map/all_to_all | solution.py:163
  164.5 7.8 %reshape.305 = bf16[512,4096]{1,0:T(8,128)(2,1)} reshape(bf16[128,4,8,2,256]{4,3,2,1,0:T(2,128)(2,1)} %copy.21) | data formatting | bytes 8388608 | tf_op jit(solution)/shard_map/reshape | solution.py:164
  172.3 6.5 %copy.22 = bf16[4096,512]{1,0:T(8,128)(2,1)} copy(bf16[4096,512]{0,1:T(8,128)(2,1)} %bitcast.44) | data formatting | bytes 8388608 | tf_op jit(solution)/shard_map/dot_general | solution.py:166
  178.8 17.2 %multiply_reduce_fusion = (f32[8]{0:T(128)S(1)}, f32[1024,8,2,256]{3,0,2,1:T(8,128)}) fusion(f32[256]{0:T(256)S(1)} %multiply_add_fusion.2, f32[1024,8]{0,1:T(8,128)S(1)} %convolution_bitcast_fusion, bf16[8,2,256,512]{3,2,1,0:T(8,128)(2,1)} %bitcast.45, f32[512]{0:T(512)S(1)} %sine_multiply_fusion, s32[512]{0:T(512)S(1)} %multiply_add_fusion.1), kind=kOutput, calls=%fused_computation | convolution fusion | flops 4320133120 | bytes 21009440 | tf_op jit(solution)/shard_map/dot_general | solution.py:166
  199.6 3.4 %collective-permute-done.11 = f32[8]{0:T(128)S(1)} collective-permute-done((f32[8]{0:T(128)S(1)}, f32[8]{0:T(128)S(1)}, u32[]{:S(2)}, u32[]{:S(2)}) %collective-permute-start.11) | collective-permute-done | bytes 64 | tf_op jit(solution)/shard_map/ppermute | solution.py:123
  203.8 7.0 %fusion = f32[1024,8,2,256]{3,0,2,1:T(8,128)S(1)} fusion(f32[1024,8,2,256]{3,0,2,1:T(8,128)} %get-tuple-element.18, f32[8]{0:T(128)S(1)} %add_rsqrt_fusion, f32[256]{0:T(256)S(1)} %multiply_add_fusion.2, f32[1024,8]{0,1:T(8,128)S(1)} %convolution_bitcast_fusion), kind=kLoop, calls=%fused_computation.2 | loop fusion | flops 12582912 | bytes 33588256 | tf_op jit(solution)/shard_map/mul | solution.py:179
  210.8 21.5 %copy.23 = f32[1024,8,2,256]{3,2,1,0:T(2,128)} copy(f32[1024,8,2,256]{3,0,2,1:T(8,128)S(1)} %fusion) | data formatting | bytes 33554432 | tf_op jit(solution)/shard_map/mul | solution.py:179
  (65 shorter events, 23.8 us)
Async XLA Ops:
  0.0 104.0 %copy-start = (f32[8,1024]{1,0:T(8,128)S(1)}, f32[8,1024]{1,0:T(8,128)}, u32[]{:S(2)}) copy-start(f32[8,1024]{1,0:T(8,128)} %param.8) | copy-start | bytes 98308
  0.0 4.2 %copy-start.3 = (bf16[256,8192]{1,0:T(8,128)(2,1)S(1)}, bf16[256,8192]{1,0:T(8,128)(2,1)}, u32[]{:S(2)}) copy-start(bf16[256,8192]{1,0:T(8,128)(2,1)} %param.5) | copy-start | bytes 12582916
  4.0 1.7 copy-start.4
  5.6 7.6 %collective-permute-start = (f32[16,272]{0,1:T(8,128)S(1)}, f32[16,272]{0,1:T(8,128)S(1)}, u32[]{:S(2)}, u32[]{:S(2)}) collective-permute-start(f32[16,272]{0,1:T(8,128)S(1)} %copy.18), channel_id=1, source_target_pairs={{0,4},{4,0},{8,12},{12,8},{16,20},{20,16},{24,28},{28,24},{32,36},... | collective-permute-start | bytes 52232 | tf_op jit(solution)/shard_map/ppermute | solution.py:123
  13.3 9.5 %collective-permute-start.3 = (f32[16,272]{0,1:T(8,128)S(1)}, f32[16,272]{0,1:T(8,128)S(1)}, u32[]{:S(2)}, u32[]{:S(2)}) collective-permute-start(f32[16,272]{0,1:T(8,128)S(1)} %add.196), channel_id=1, source_target_pairs={{0,24},{4,28},{8,0},{12,4},{16,8},{20,12},{24,16},{28,20},{32,56},... | collective-permute-start | bytes 52232 | tf_op jit(solution)/shard_map/ppermute | solution.py:123
  16.2 8.1 %collective-permute-start.2 = (f32[16,272]{0,1:T(8,128)S(1)}, f32[16,272]{0,1:T(8,128)S(1)}, u32[]{:S(2)}, u32[]{:S(2)}) collective-permute-start(f32[16,272]{0,1:T(8,128)S(1)} %add.196), channel_id=1, source_target_pairs={{0,16},{4,20},{8,24},{12,28},{16,0},{20,4},{24,8},{28,12},{32,48},... | collective-permute-start | bytes 52232 | tf_op jit(solution)/shard_map/ppermute | solution.py:123
  17.0 9.5 %collective-permute-start.1 = (f32[16,272]{0,1:T(8,128)S(1)}, f32[16,272]{0,1:T(8,128)S(1)}, u32[]{:S(2)}, u32[]{:S(2)}) collective-permute-start(f32[16,272]{0,1:T(8,128)S(1)} %add.196), channel_id=1, source_target_pairs={{0,8},{4,12},{8,16},{12,20},{16,24},{20,28},{24,0},{28,4},{32,40},... | collective-permute-start | bytes 52232 | tf_op jit(solution)/shard_map/ppermute | solution.py:123
  26.5 9.2 %collective-permute-start.6 = (f32[16,272]{0,1:T(8,128)S(1)}, f32[16,272]{0,1:T(8,128)S(1)}, u32[]{:S(2)}, u32[]{:S(2)}) collective-permute-start(f32[16,272]{0,1:T(8,128)S(1)} %add_add_fusion.2), channel_id=1, source_target_pairs={{0,96},{4,100},{8,104},{12,108},{16,112},{20,116},{24,120},{28,124... | collective-permute-start | bytes 52232 | tf_op jit(solution)/shard_map/ppermute | solution.py:123
  29.6 8.1 %collective-permute-start.5 = (f32[16,272]{0,1:T(8,128)S(1)}, f32[16,272]{0,1:T(8,128)S(1)}, u32[]{:S(2)}, u32[]{:S(2)}) collective-permute-start(f32[16,272]{0,1:T(8,128)S(1)} %add_add_fusion.2), channel_id=1, source_target_pairs={{0,64},{4,68},{8,72},{12,76},{16,80},{20,84},{24,88},{28,92},{32,9... | collective-permute-start | bytes 52232 | tf_op jit(solution)/shard_map/ppermute | solution.py:123
  30.2 9.2 %collective-permute-start.4 = (f32[16,272]{0,1:T(8,128)S(1)}, f32[16,272]{0,1:T(8,128)S(1)}, u32[]{:S(2)}, u32[]{:S(2)}) collective-permute-start(f32[16,272]{0,1:T(8,128)S(1)} %add_add_fusion.2), channel_id=1, source_target_pairs={{0,32},{4,36},{8,40},{12,44},{16,48},{20,52},{24,56},{28,60},{32,6... | collective-permute-start | bytes 52232 | tf_op jit(solution)/shard_map/ppermute | solution.py:123
  39.4 10.2 %collective-permute-start.9 = (f32[16,272]{0,1:T(8,128)S(1)}, f32[16,272]{0,1:T(8,128)S(1)}, u32[]{:S(2)}, u32[]{:S(2)}) collective-permute-start(f32[16,272]{0,1:T(8,128)S(1)} %add_add_fusion.1), channel_id=1, source_target_pairs={{0,3},{1,0},{2,1},{3,2},{4,7},{5,4},{6,5},{7,6},{8,11},{9,8},{10,9... | collective-permute-start | bytes 52232 | tf_op jit(solution)/shard_map/ppermute | solution.py:123
  43.5 8.0 %collective-permute-start.8 = (f32[16,272]{0,1:T(8,128)S(1)}, f32[16,272]{0,1:T(8,128)S(1)}, u32[]{:S(2)}, u32[]{:S(2)}) collective-permute-start(f32[16,272]{0,1:T(8,128)S(1)} %add_add_fusion.1), channel_id=1, source_target_pairs={{0,2},{1,3},{2,0},{3,1},{4,6},{5,7},{6,4},{7,5},{8,10},{9,11},{10,... | collective-permute-start | bytes 52232 | tf_op jit(solution)/shard_map/ppermute | solution.py:123
  43.6 9.5 %collective-permute-start.7 = (f32[16,272]{0,1:T(8,128)S(1)}, f32[16,272]{0,1:T(8,128)S(1)}, u32[]{:S(2)}, u32[]{:S(2)}) collective-permute-start(f32[16,272]{0,1:T(8,128)S(1)} %add_add_fusion.1), channel_id=1, source_target_pairs={{0,1},{1,2},{2,3},{3,0},{4,5},{5,6},{6,7},{7,4},{8,9},{9,10},{10,1... | collective-permute-start | bytes 52232 | tf_op jit(solution)/shard_map/ppermute | solution.py:123
  57.9 10.5 %copy-start.2 = (f32[4,8,16,1024]{3,2,1,0:T(8,128)S(1)}, f32[4,8,16,1024]{3,2,1,0:T(8,128)}, u32[]{:S(2)}) copy-start(f32[4,8,16,1024]{3,2,1,0:T(8,128)} %get-tuple-element.6) | copy-start | bytes 6291460
  97.7 6.3 %copy-start.5 = (s32[8]{0:T(128)S(1)}, s32[8]{0:T(128)}, u32[]{:S(2)}) copy-start(s32[8]{0:T(128)} %param.9) | copy-start | bytes 100
  97.7 57.4 %all-to-all-start = ((bf16[128,4,8,2,256]{4,2,3,1,0:T(8,128)(2,1)}), bf16[128,4,8,2,256]{4,2,3,1,0:T(8,128)(2,1)}, u32[]{:S(2)}, u32[]{:S(2)}) async-start(bf16[128,4,8,2,256]{4,2,3,1,0:T(8,128)(2,1)} %bitcast.42), calls=%async_computation | async-start | bytes 8388608 | tf_op jit(solution)/shard_map/all_to_all | solution.py:163
  196.0 3.6 %collective-permute-start.12 = (f32[8]{0:T(128)S(1)}, f32[8]{0:T(128)S(1)}, u32[]{:S(2)}, u32[]{:S(2)}) collective-permute-start(f32[8]{0:T(128)S(1)} %get-tuple-element.17), channel_id=1, source_target_pairs={{0,3},{1,0},{2,1},{3,2},{4,7},{5,4},{6,5},{7,6},{8,11},{9,8},{10,9... | collective-permute-start | bytes 104 | tf_op jit(solution)/shard_map/ppermute | solution.py:123
  197.9 5.1 %collective-permute-start.11 = (f32[8]{0:T(128)S(1)}, f32[8]{0:T(128)S(1)}, u32[]{:S(2)}, u32[]{:S(2)}) collective-permute-start(f32[8]{0:T(128)S(1)} %get-tuple-element.17), channel_id=1, source_target_pairs={{0,2},{1,3},{2,0},{3,1},{4,6},{5,7},{6,4},{7,5},{8,10},{9,11},{10,... | collective-permute-start | bytes 104 | tf_op jit(solution)/shard_map/ppermute | solution.py:123
  199.0 4.8 %collective-permute-start.10 = (f32[8]{0:T(128)S(1)}, f32[8]{0:T(128)S(1)}, u32[]{:S(2)}, u32[]{:S(2)}) collective-permute-start(f32[8]{0:T(128)S(1)} %get-tuple-element.17), channel_id=1, source_target_pairs={{0,1},{1,2},{2,3},{3,0},{4,5},{5,6},{6,7},{7,4},{8,9},{9,10},{10,1... | collective-permute-start | bytes 104 | tf_op jit(solution)/shard_map/ppermute | solution.py:123
  210.8 21.5 %copy-start.1 = (f32[8,1024]{1,0:T(8,128)S(1)}, f32[8,1024]{1,0:T(8,128)}, u32[]{:S(2)}) copy-start(f32[8,1024]{1,0:T(8,128)} %param.8) | copy-start | bytes 98308
where the time goes:
time: 233 us; the launch traced here: 232 us
  waiting for transfers between devices  76.9 us (33%)
  local copies, waits for them, and re-layouts  50.3 us (22%)
  matrix products  32.9 us (14%)
  Pallas kernels  24.6 us (11%)
  starting transfers between devices  23.9 us (10%)
  other arithmetic  23.5 us (10%)
    all_to_all x1, waiting for transfers between devices, body(): moved = lax.all_to_all(sendbuf, ('blk', 'grp'), 0, 0, tiled=True)  50.9 us
    ppermute x13, waiting for transfers between devices, ring_sum(): lax.ppermute(v, axis, shift_perm(size, stride, total, k))  26 us
    pallas_call x1, Pallas kernels, cycle_fourier(): pl.pallas_call(fourier_kernel, grid=(n_cyc,), in_specs=[pl.BlockSpec((1,...  24.6 us
    mul x1, local copies, waits for them, and re-layouts, body(): weighted * lax.rsqrt(power / (2.0 * L * m_width) + 1e-06)[None, :, None,...  21.5 us
    ppermute x13, starting transfers between devices, ring_sum(): lax.ppermute(v, axis, shift_perm(size, stride, total, k))  17.7 us
    dot_general x1, matrix products, body(): jnp.dot(theta_tab, moved, preferred_element_type=jnp.float32)  17.2 us
    dot_general x1, matrix products, body(): correction = jnp.dot(projected.T, basis, precision=lax.Precision.HIGHEST)  10.3 us
    all_to_all x1, local copies, waits for them, and re-layouts, body(): moved = lax.all_to_all(sendbuf, ('blk', 'grp'), 0, 0, tiled=True)  9.46 us
  transfers between devices with their start and end apart: 14, of which 13 were waited for; matrix products, arithmetic and copies ran while one was open for 5% of the time, Pallas kernels for 0%

commit v1 on v0

--- a/solution.py
+++ b/solution.py
@@ -37,57 +37,66 @@
     return ca, sa, cb, sb
 
 
-def fourier_kernel(ca_ref, sa_ref, cb_ref, sb_ref, inv_ref, len_ref, x_ref, o_ref, tab_ref):
+def table_kernel(ca_ref, sa_ref, cb_ref, sb_ref, inv_ref, len_ref, tab_ref):
+    t = pl.program_id(1)
     m_width = cb_ref.shape[2]
     inv = inv_ref[0][:, 0:1]
     length = len_ref[0][:, 0:1]
-
-    def build(t, carry):
-        ca = ca_ref[0, pl.ds(t, 1), :]
-        sa = sa_ref[0, pl.ds(t, 1), :]
-        cb = cb_ref[0]
-        sb = sb_ref[0]
-        rows = t * J_LO + lax.broadcasted_iota(jnp.int32, (J_LO, 1), 0)
-        weight = jnp.where(rows < length, inv, 0.0)
-        cos_t, sin_t = add_angles(ca, sa, cb, sb)
-        r0 = pl.multiple_of(t * J_LO, J_LO)
-        tab_ref[pl.ds(r0, J_LO), 0:m_width] = (cos_t * weight).astype(jnp.bfloat16)
-        tab_ref[pl.ds(r0, J_LO), m_width : 2 * m_width] = (-sin_t * weight).astype(jnp.bfloat16)
-        return carry
-
-    lax.fori_loop(0, RPIX // J_LO, build, 0)
-    width = 2 * m_width
-    step = 512
-    for q in range(width // step):
-        o_ref[0, :, q * step : (q + 1) * step] = jnp.dot(
-            x_ref[...], tab_ref[:, q * step : (q + 1) * step], preferred_element_type=jnp.float32
-        ).astype(jnp.bfloat16)
+    ca = ca_ref[0, pl.ds(t, 1), :]
+    sa = sa_ref[0, pl.ds(t, 1), :]
+    cb = cb_ref[0]
+    sb = sb_ref[0]
+    rows = t * J_LO + lax.broadcasted_iota(jnp.int32, (J_LO, 1), 0)
+    weight = jnp.where(rows < length, inv, 0.0)
+    cos_t, sin_t = add_angles(ca, sa, cb, sb)
+    tab_ref[0, :, 0:m_width] = (cos_t * weight).astype(jnp.bfloat16)
+    tab_ref[0, :, m_width : 2 * m_width] = (-sin_t * weight).astype(jnp.bfloat16)
 
 
-def cycle_fourier(cleaned, cycle_len, m_width):
+def matmul_kernel(x_ref, tab_ref, o_ref):
+    o_ref[0] = jnp.dot(x_ref[...], tab_ref[0], preferred_element_type=jnp.float32).astype(
+        jnp.bfloat16
+    )
+
+
+def cycle_tables(cycle_len, m_width):
     n_cyc = cycle_len.shape[0]
-    n_chan = cleaned.shape[0]
     ca, sa, cb, sb = small_tables(cycle_len, m_width)
     inv = jnp.broadcast_to(lax.rsqrt(cycle_len.astype(jnp.float32))[:, None, None], (n_cyc, 1, 128))
     lens = jnp.broadcast_to(cycle_len[:, None, None], (n_cyc, 1, 128))
     n_hi = RPIX // J_LO
     return pl.pallas_call(
-        fourier_kernel,
-        grid=(n_cyc,),
+        table_kernel,
+        grid=(n_cyc, n_hi),
         in_specs=[
-            pl.BlockSpec((1, n_hi, m_width), lambda k: (k, 0, 0)),
-            pl.BlockSpec((1, n_hi, m_width), lambda k: (k, 0, 0)),
-            pl.BlockSpec((1, J_LO, m_width), lambda k: (k, 0, 0)),
-            pl.BlockSpec((1, J_LO, m_width), lambda k: (k, 0, 0)),
-            pl.BlockSpec((1, 1, 128), lambda k: (k, 0, 0)),
-            pl.BlockSpec((1, 1, 128), lambda k: (k, 0, 0)),
-            pl.BlockSpec((n_chan, RPIX), lambda k: (0, k)),
+            pl.BlockSpec((1, n_hi, m_width), lambda k, t: (k, 0, 0)),
+            pl.BlockSpec((1, n_hi, m_width), lambda k, t: (k, 0, 0)),
+            pl.BlockSpec((1, J_LO, m_width), lambda k, t: (k, 0, 0)),
+            pl.BlockSpec((1, J_LO, m_width), lambda k, t: (k, 0, 0)),
+            pl.BlockSpec((1, 1, 128), lambda k, t: (k, 0, 0)),
+            pl.BlockSpec((1, 1, 128), lambda k, t: (k, 0, 0)),
         ],
-        out_specs=pl.BlockSpec((1, n_chan, 2 * m_width), lambda k: (k, 0, 0)),
-        out_shape=jax.ShapeDtypeStruct((n_cyc, n_chan, 2 * m_width), jnp.bfloat16),
-        scratch_shapes=[pltpu.VMEM((RPIX, 2 * m_width), jnp.bfloat16)],
-        compiler_params=pltpu.CompilerParams(vmem_limit_bytes=48 * 1024 * 1024),
-    )(ca, sa, cb, sb, inv, lens, cleaned)
+        out_specs=pl.BlockSpec((1, J_LO, 2 * m_width), lambda k, t: (k, t, 0)),
+        out_shape=jax.ShapeDtypeStruct((n_cyc, RPIX, 2 * m_width), jnp.bfloat16),
+    )(ca, sa, cb, sb, inv, lens)
+
+
+def cycle_fourier(cleaned, tables):
+    n_cyc = tables.shape[0]
+    n_chan = cleaned.shape[0]
+    width = tables.shape[2]
+    step = 512
+    return pl.pallas_call(
+        matmul_kernel,
+        grid=(n_cyc, width // step),
+        in_specs=[
+            pl.BlockSpec((n_chan, RPIX), lambda k, q: (0, k)),
+            pl.BlockSpec((1, RPIX, step), lambda k, q: (k, 0, q)),
+        ],
+        out_specs=pl.BlockSpec((1, n_chan, step), lambda k, q: (k, 0, q)),
+        out_shape=jax.ShapeDtypeStruct((n_cyc, n_chan, width), jnp.bfloat16),
+        compiler_params=pltpu.CompilerParams(vmem_limit_bytes=32 * 1024 * 1024),
+    )(cleaned, tables)
 
 
 def theta_table(cycle_ids, n_cycle):
@@ -146,6 +155,7 @@
         mode_amps, masked, (((1,), (1,)), ((), ())), preferred_element_type=jnp.float32
     )
     amps_wide = mode_amps.astype(jnp.float32)
+    tables = cycle_tables(cycle_len, m_width)
     subs = sub_axes(n_blk, n_grp)
     sums = ring_sum(jnp.concatenate([gram_part, cross_part], axis=1), subs)
     gram_sum = sums[:, :n_mode]
@@ -155,7 +165,7 @@
     projected = jax.scipy.linalg.solve_triangular(lower, cross_sum, lower=True)
     correction = jnp.dot(projected.T, basis, precision=lax.Precision.HIGHEST)
     cleaned = (masked.astype(jnp.float32) - correction).astype(jnp.bfloat16)
-    fourier = cycle_fourier(cleaned, cycle_len, m_width)
+    fourier = cycle_fourier(cleaned, tables)
     fourier = fourier.reshape(cycle_dev, n_blk, chan_dev, 2, n_grp, M_DEV)
     sendbuf = fourier.transpose(1, 4, 0, 2, 3, 5).reshape(
         n_blk * n_grp, cycle_dev, chan_dev, 2, M_DEV

time: 233 us -> 253 us (1.086)
  Pallas kernels: 24.6 us -> 56.8 us
  waiting for transfers between devices: 76.9 us -> 60.3 us
  starting transfers between devices: 23.9 us -> 29.4 us
    pallas_call x1 -> x2, Pallas kernels: 24.6 us -> 56.8 us  [the longest x1 36.3 us: cycle_tables(): pl.pallas_call(table_kernel, grid=(n_cyc, n_hi), in_specs=[pl.BlockSpec((...]
    ppermute x13, waiting for transfers between devices: 26 us -> 9.21 us  [ring_sum(): lax.ppermute(v, axis, shift_perm(size, stride, total, k))]
    ppermute x13, starting transfers between devices: 17.7 us -> 22 us  [ring_sum(): lax.ppermute(v, axis, shift_perm(size, stride, total, k))]
  transfers between devices with their start and end apart: 14 -> 14, of which waited for: 13 -> 6; matrix products, arithmetic and copies ran while one was open for 5% -> 6% of each run, Pallas kernels for 0% -> 14%
where the time goes in v1:
time: 253 us
  waiting for transfers between devices  60.3 us (24%)
  Pallas kernels  56.8 us (22%)
  local copies, waits for them, and re-layouts  49.4 us (20%)
  matrix products  31.5 us (12%)
  starting transfers between devices  29.4 us (12%)
  other arithmetic  25 us (10%)
    all_to_all x1, waiting for transfers between devices, body(): moved = lax.all_to_all(sendbuf, ('blk', 'grp'), 0, 0, tiled=True)  51.1 us
    pallas_call x1, Pallas kernels, cycle_tables(): pl.pallas_call(table_kernel, grid=(n_cyc, n_hi), in_specs=[pl.BlockSpec((...  36.3 us
    ppermute x13, starting transfers between devices, ring_sum(): lax.ppermute(v, axis, shift_perm(size, stride, total, k))  22 us
    mul x1, local copies, waits for them, and re-layouts, body(): weighted * lax.rsqrt(power / (2.0 * L * m_width) + 1e-06)[None, :, None,...  21.5 us
    pallas_call x1, Pallas kernels, cycle_fourier(): pl.pallas_call(matmul_kernel, grid=(n_cyc, width // step), in_specs=[pl.B...  20.4 us
    dot_general x1, matrix products, body(): jnp.dot(theta_tab, moved, preferred_element_type=jnp.float32)  17.2 us
    cos x2, other arithmetic, cos_sin_of_phase(): return (jnp.cos(angle), jnp.sin(angle))  9.68 us
    all_to_all x1, local copies, waits for them, and re-layouts, body(): moved = lax.all_to_all(sendbuf, ('blk', 'grp'), 0, 0, tiled=True)  9.46 us
  transfers between devices with their start and end apart: 14, of which 6 were waited for; matrix products, arithmetic and copies ran while one was open for 6% of the time, Pallas kernels for 14%

profile of v1, /device:TPU:0, one launch (start us, length us, event | category | flops | bytes accessed | tf_op | source)
XLA Modules:
  0.0 252.5 jit_solution(3690235838937340254)
XLA Ops:
  0.9 3.1 %convolution_convert_fusion = bf16[8192,16]{0,1:T(8,128)(2,1)S(1)} fusion(bf16[256,16]{0,1:T(8,128)(2,1)} %param.6, bf16[256,8192]{1,0:T(8,128)(2,1)} %param.5, pred[8192]{0:T(1024)(128)(4,1)S(1)} %bitcast.46), kind=kOutput, calls=%fused_computation.5 | convolution fusion | flops 69337088 | bytes 4472832 | tf_op jit(solution)/shard_map/dot_general | solution.py:150
  6.1 7.8 %fusion.45 = (f32[4,16,1024]{2,1,0:T(8,128)S(1)}, f32[4,16,1024]{2,1,0:T(8,128)S(1)}, f32[4,16,1024]{2,1,0:T(8,128)}, f32[4,16,1024]{2,1,0:T(8,128)}) fusion(f32[4]{0:T(128)S(1)} %get-tuple-element.16, pred[4]{0:T(512)(128)(4,1)S(1)} %broadcast_compare_fusion, s32[4]{0:T(128)S(1)} %get-tuple-element.15, s32[16,1024]{1,0:T(8,128)S(1)} %iota_multiply_fusion, ...), kind=kLoop, calls=%fused_computation.66 | loop fusion | flops 1376256 | bytes 1114404 | tf_op jit(solution)/shard_map/cos | solution.py:16
  14.1 1.7 collective-permute-start.1
  15.8 2.7 %collective-permute-start.2 = (f32[16,272]{0,1:T(8,128)S(1)}, f32[16,272]{0,1:T(8,128)S(1)}, u32[]{:S(2)}, u32[]{:S(2)}) collective-permute-start(f32[16,272]{0,1:T(8,128)S(1)} %add.188), channel_id=1, source_target_pairs={{0,16},{4,20},{8,24},{12,28},{16,0},{20,4},{24,8},{28,12},{32,48},... | collective-permute-start | bytes 52232 | tf_op jit(solution)/shard_map/ppermute | solution.py:132
  20.0 1.8 fusion.49
  21.8 3.7 %collective-permute-done.2 = f32[16,272]{0,1:T(8,128)S(1)} collective-permute-done((f32[16,272]{0,1:T(8,128)S(1)}, f32[16,272]{0,1:T(8,128)S(1)}, u32[]{:S(2)}, u32[]{:S(2)}) %collective-permute-start.2) | collective-permute-done | bytes 17440 | tf_op jit(solution)/shard_map/ppermute | solution.py:132
  27.2 2.9 %collective-permute-start.5 = (f32[16,272]{0,1:T(8,128)S(1)}, f32[16,272]{0,1:T(8,128)S(1)}, u32[]{:S(2)}, u32[]{:S(2)}) collective-permute-start(f32[16,272]{0,1:T(8,128)S(1)} %add_add_fusion.2), channel_id=1, source_target_pairs={{0,64},{4,68},{8,72},{12,76},{16,80},{20,84},{24,88},{28,92},{32,9... | collective-permute-start | bytes 52232 | tf_op jit(solution)/shard_map/ppermute | solution.py:132
  31.5 2.6 %multiply_add_fusion = (f32[4,8,16,1024]{3,2,1,0:T(8,128)}, f32[4,8,16,1024]{3,2,1,0:T(8,128)}) fusion(f32[4,16,1024]{2,1,0:T(8,128)S(1)} %get-tuple-element.8, f32[4,8,1024]{2,1,0:T(8,128)S(1)} %get-tuple-element.10, f32[4,16,1024]{2,1,0:T(8,128)S(1)} %get-tuple-element.7, f32[4,8,1024]{2,1,0:T(8,128)S(1)} %get-tuple-element.9), kind=kLoop, calls=%fused_computation.17 | loop fusion | flops 3145728 | bytes 4980736 | tf_op jit(solution)/shard_map/add | solution.py:20
  34.1 2.2 collective-permute-done.5
  36.3 2.0 collective-permute-start.7
  38.3 3.6 %collective-permute-start.8 = (f32[16,272]{0,1:T(8,128)S(1)}, f32[16,272]{0,1:T(8,128)S(1)}, u32[]{:S(2)}, u32[]{:S(2)}) collective-permute-start(f32[16,272]{0,1:T(8,128)S(1)} %add_add_fusion.1), channel_id=1, source_target_pairs={{0,2},{1,3},{2,0},{3,1},{4,6},{5,7},{6,4},{7,5},{8,10},{9,11},{10,... | collective-permute-start | bytes 52232 | tf_op jit(solution)/shard_map/ppermute | solution.py:132
  44.2 36.3 %shard_map.55.tab_ref = bf16[4,2048,2048]{2,1,0:T(8,128)(2,1)} custom-call(f32[4,16,1024]{2,1,0:T(8,128)} %get-tuple-element.13.ca_ref, f32[4,16,1024]{2,1,0:T(8,128)} %get-tuple-element.14.sa_ref, f32[4,128,1024]{2,1,0:T(8,128)} %bitcast.44, f32[4,128,1024]{2,1,0:T(8,128)} %bitcast.43, f32[4,1,128]{2,1,0:T(1,128)} %broadcast_in_dim.19.inv_ref, ...), custom_call_target="tpu_custom_call" | custom-call | tf_op jit(solution)/shard_map/pallas_call | solution.py:68
  85.4 8.9 %fusion.1.x_ref = bf16[256,8192]{1,0:T(8,128)(2,1)S(1)} fusion(f32[16,256]{1,0:T(8,128)S(1)} %fusion.38, f32[16,8192]{1,0:T(8,128)S(1)} %fusion.52, bf16[256,8192]{1,0:T(8,128)(2,1)} %param.5, pred[8192]{0:T(1024)(128)(4,1)S(1)} %bitcast.48), kind=kOutput, calls=%fused_computation.4 | convolution fusion | flops 411041792 | bytes 8937472 | tf_op jit(solution)/shard_map/dot_general | solution.py:166
  94.3 20.4 %shard_map.56 = bf16[4,256,2048]{2,1,0:T(8,128)(2,1)S(1)} custom-call(bf16[256,8192]{1,0:T(8,128)(2,1)S(1)} %fusion.1.x_ref, bf16[4,2048,2048]{2,1,0:T(8,128)(2,1)} %shard_map.55.tab_ref), custom_call_target="tpu_custom_call" | custom-call | tf_op jit(solution)/shard_map/pallas_call | solution.py:89
  114.7 2.6 %copy.20 = bf16[4,32,8,2,4,256]{5,2,3,0,4,1:T(8,128)(2,1)} copy(bf16[4,32,8,2,4,256]{5,2,4,3,1,0:T(8,128)(2,1)S(1)} %bitcast.40) | data formatting | bytes 8388608 | tf_op jit(solution)/shard_map/reshape | solution.py:169
  117.3 7.3 %all-to-all-start = ((bf16[128,4,8,2,256]{4,2,3,1,0:T(8,128)(2,1)}), bf16[128,4,8,2,256]{4,2,3,1,0:T(8,128)(2,1)}, u32[]{:S(2)}, u32[]{:S(2)}) async-start(bf16[128,4,8,2,256]{4,2,3,1,0:T(8,128)(2,1)} %bitcast.41), calls=%async_computation | async-start | bytes 8388608 | tf_op jit(solution)/shard_map/all_to_all | solution.py:173
  125.0 51.1 %all-to-all-done = bf16[128,4,8,2,256]{4,2,3,1,0:T(8,128)(2,1)} async-done(((bf16[128,4,8,2,256]{4,2,3,1,0:T(8,128)(2,1)}), bf16[128,4,8,2,256]{4,2,3,1,0:T(8,128)(2,1)}, u32[]{:S(2)}, u32[]{:S(2)}) %all-to-all-start) | async-done | bytes 4194336 | tf_op jit(solution)/shard_map/all_to_all | solution.py:173
  176.1 9.5 %copy.21 = bf16[128,4,8,2,256]{4,3,2,1,0:T(2,128)(2,1)} copy(bf16[128,4,8,2,256]{4,2,3,1,0:T(8,128)(2,1)} %all-to-all-done) | data formatting | bytes 8388608 | tf_op jit(solution)/shard_map/all_to_all | solution.py:173
  185.5 7.8 %reshape.305 = bf16[512,4096]{1,0:T(8,128)(2,1)} reshape(bf16[128,4,8,2,256]{4,3,2,1,0:T(2,128)(2,1)} %copy.21) | data formatting | bytes 8388608 | tf_op jit(solution)/shard_map/reshape | solution.py:174
  193.3 6.5 %copy.22 = bf16[4096,512]{1,0:T(8,128)(2,1)} copy(bf16[4096,512]{0,1:T(8,128)(2,1)} %bitcast.42) | data formatting | bytes 8388608 | tf_op jit(solution)/shard_map/dot_general | solution.py:176
  199.8 17.2 %multiply_reduce_fusion = (f32[8]{0:T(128)S(1)}, f32[1024,8,2,256]{3,0,2,1:T(8,128)}) fusion(f32[256]{0:T(256)S(1)} %multiply_add_fusion.2, f32[1024,8]{0,1:T(8,128)S(1)} %convolution_bitcast_fusion, bf16[8,2,256,512]{3,2,1,0:T(8,128)(2,1)} %bitcast.45, f32[512]{0:T(512)S(1)} %sine_multiply_fusion, s32[512]{0:T(512)S(1)} %multiply_add_fusion.1), kind=kOutput, calls=%fused_computation | convolution fusion | flops 4320133120 | bytes 21009440 | tf_op jit(solution)/shard_map/dot_general | solution.py:176
  217.9 2.5 %collective-permute-start.11 = (f32[8]{0:T(128)S(1)}, f32[8]{0:T(128)S(1)}, u32[]{:S(2)}, u32[]{:S(2)}) collective-permute-start(f32[8]{0:T(128)S(1)} %get-tuple-element.17), channel_id=1, source_target_pairs={{0,2},{1,3},{2,0},{3,1},{4,6},{5,7},{6,4},{7,5},{8,10},{9,11},{10,... | collective-permute-start | bytes 104 | tf_op jit(solution)/shard_map/ppermute | solution.py:132
  224.0 7.0 %fusion = f32[1024,8,2,256]{3,0,2,1:T(8,128)S(1)} fusion(f32[1024,8,2,256]{3,0,2,1:T(8,128)} %get-tuple-element.18, f32[8]{0:T(128)S(1)} %add_rsqrt_fusion, f32[256]{0:T(256)S(1)} %multiply_add_fusion.2, f32[1024,8]{0,1:T(8,128)S(1)} %convolution_bitcast_fusion), kind=kLoop, calls=%fused_computation.2 | loop fusion | flops 12582912 | bytes 33588256 | tf_op jit(solution)/shard_map/mul | solution.py:189
  231.0 21.5 %copy.23 = f32[1024,8,2,256]{3,2,1,0:T(2,128)} copy(f32[1024,8,2,256]{3,0,2,1:T(8,128)S(1)} %fusion) | data formatting | bytes 33554432 | tf_op jit(solution)/shard_map/mul | solution.py:189
  (64 shorter events, 19.4 us)
Async XLA Ops:
  0.0 124.8 %copy-start = (f32[8,1024]{1,0:T(8,128)S(1)}, f32[8,1024]{1,0:T(8,128)}, u32[]{:S(2)}) copy-start(f32[8,1024]{1,0:T(8,128)} %param.8) | copy-start | bytes 98308
  0.0 4.0 %copy-start.2 = (bf16[256,8192]{1,0:T(8,128)(2,1)S(1)}, bf16[256,8192]{1,0:T(8,128)(2,1)}, u32[]{:S(2)}) copy-start(bf16[256,8192]{1,0:T(8,128)(2,1)} %param.5) | copy-start | bytes 12582916
  4.0 1.7 copy-start.3
  5.6 8.5 %collective-permute-start = (f32[16,272]{0,1:T(8,128)S(1)}, f32[16,272]{0,1:T(8,128)S(1)}, u32[]{:S(2)}, u32[]{:S(2)}) collective-permute-start(f32[16,272]{0,1:T(8,128)S(1)} %copy.18), channel_id=1, source_target_pairs={{0,4},{4,0},{8,12},{12,8},{16,20},{20,16},{24,28},{28,24},{32,36},... | collective-permute-start | bytes 52232 | tf_op jit(solution)/shard_map/ppermute | solution.py:132
  14.1 7.7 %collective-permute-start.1 = (f32[16,272]{0,1:T(8,128)S(1)}, f32[16,272]{0,1:T(8,128)S(1)}, u32[]{:S(2)}, u32[]{:S(2)}) collective-permute-start(f32[16,272]{0,1:T(8,128)S(1)} %add.188), channel_id=1, source_target_pairs={{0,8},{4,12},{8,16},{12,20},{16,24},{20,28},{24,0},{28,4},{32,40},... | collective-permute-start | bytes 52232 | tf_op jit(solution)/shard_map/ppermute | solution.py:132
  15.8 9.7 %collective-permute-start.2 = (f32[16,272]{0,1:T(8,128)S(1)}, f32[16,272]{0,1:T(8,128)S(1)}, u32[]{:S(2)}, u32[]{:S(2)}) collective-permute-start(f32[16,272]{0,1:T(8,128)S(1)} %add.188), channel_id=1, source_target_pairs={{0,16},{4,20},{8,24},{12,28},{16,0},{20,4},{24,8},{28,12},{32,48},... | collective-permute-start | bytes 52232 | tf_op jit(solution)/shard_map/ppermute | solution.py:132
  18.5 7.0 %collective-permute-start.3 = (f32[16,272]{0,1:T(8,128)S(1)}, f32[16,272]{0,1:T(8,128)S(1)}, u32[]{:S(2)}, u32[]{:S(2)}) collective-permute-start(f32[16,272]{0,1:T(8,128)S(1)} %add.188), channel_id=1, source_target_pairs={{0,24},{4,28},{8,0},{12,4},{16,8},{20,12},{24,16},{28,20},{32,56},... | collective-permute-start | bytes 52232 | tf_op jit(solution)/shard_map/ppermute | solution.py:132
  25.6 8.5 %collective-permute-start.4 = (f32[16,272]{0,1:T(8,128)S(1)}, f32[16,272]{0,1:T(8,128)S(1)}, u32[]{:S(2)}, u32[]{:S(2)}) collective-permute-start(f32[16,272]{0,1:T(8,128)S(1)} %add_add_fusion.2), channel_id=1, source_target_pairs={{0,32},{4,36},{8,40},{12,44},{16,48},{20,52},{24,56},{28,60},{32,6... | collective-permute-start | bytes 52232 | tf_op jit(solution)/shard_map/ppermute | solution.py:132
  27.2 9.0 %collective-permute-start.5 = (f32[16,272]{0,1:T(8,128)S(1)}, f32[16,272]{0,1:T(8,128)S(1)}, u32[]{:S(2)}, u32[]{:S(2)}) collective-permute-start(f32[16,272]{0,1:T(8,128)S(1)} %add_add_fusion.2), channel_id=1, source_target_pairs={{0,64},{4,68},{8,72},{12,76},{16,80},{20,84},{24,88},{28,92},{32,9... | collective-permute-start | bytes 52232 | tf_op jit(solution)/shard_map/ppermute | solution.py:132
  30.1 6.2 %collective-permute-start.6 = (f32[16,272]{0,1:T(8,128)S(1)}, f32[16,272]{0,1:T(8,128)S(1)}, u32[]{:S(2)}, u32[]{:S(2)}) collective-permute-start(f32[16,272]{0,1:T(8,128)S(1)} %add_add_fusion.2), channel_id=1, source_target_pairs={{0,96},{4,100},{8,104},{12,108},{16,112},{20,116},{24,120},{28,124... | collective-permute-start | bytes 52232 | tf_op jit(solution)/shard_map/ppermute | solution.py:132
  36.3 44.2 %collective-permute-start.7 = (f32[16,272]{0,1:T(8,128)S(1)}, f32[16,272]{0,1:T(8,128)S(1)}, u32[]{:S(2)}, u32[]{:S(2)}) collective-permute-start(f32[16,272]{0,1:T(8,128)S(1)} %add_add_fusion.1), channel_id=1, source_target_pairs={{0,1},{1,2},{2,3},{3,0},{4,5},{5,6},{6,7},{7,4},{8,9},{9,10},{10,1... | collective-permute-start | bytes 52232 | tf_op jit(solution)/shard_map/ppermute | solution.py:132
  38.3 42.2 %collective-permute-start.8 = (f32[16,272]{0,1:T(8,128)S(1)}, f32[16,272]{0,1:T(8,128)S(1)}, u32[]{:S(2)}, u32[]{:S(2)}) collective-permute-start(f32[16,272]{0,1:T(8,128)S(1)} %add_add_fusion.1), channel_id=1, source_target_pairs={{0,2},{1,3},{2,0},{3,1},{4,6},{5,7},{6,4},{7,5},{8,10},{9,11},{10,... | collective-permute-start | bytes 52232 | tf_op jit(solution)/shard_map/ppermute | solution.py:132
  41.9 38.7 %collective-permute-start.9 = (f32[16,272]{0,1:T(8,128)S(1)}, f32[16,272]{0,1:T(8,128)S(1)}, u32[]{:S(2)}, u32[]{:S(2)}) collective-permute-start(f32[16,272]{0,1:T(8,128)S(1)} %add_add_fusion.1), channel_id=1, source_target_pairs={{0,3},{1,0},{2,1},{3,2},{4,7},{5,4},{6,5},{7,6},{8,11},{9,8},{10,9... | collective-permute-start | bytes 52232 | tf_op jit(solution)/shard_map/ppermute | solution.py:132
  117.3 7.4 %copy-start.4 = (s32[8]{0:T(128)S(1)}, s32[8]{0:T(128)}, u32[]{:S(2)}) copy-start(s32[8]{0:T(128)} %param.9) | copy-start | bytes 100
  117.3 58.7 %all-to-all-start = ((bf16[128,4,8,2,256]{4,2,3,1,0:T(8,128)(2,1)}), bf16[128,4,8,2,256]{4,2,3,1,0:T(8,128)(2,1)}, u32[]{:S(2)}, u32[]{:S(2)}) async-start(bf16[128,4,8,2,256]{4,2,3,1,0:T(8,128)(2,1)} %bitcast.41), calls=%async_computation | async-start | bytes 8388608 | tf_op jit(solution)/shard_map/all_to_all | solution.py:173
  217.0 4.8 %collective-permute-start.10 = (f32[8]{0:T(128)S(1)}, f32[8]{0:T(128)S(1)}, u32[]{:S(2)}, u32[]{:S(2)}) collective-permute-start(f32[8]{0:T(128)S(1)} %get-tuple-element.17), channel_id=1, source_target_pairs={{0,1},{1,2},{2,3},{3,0},{4,5},{5,6},{6,7},{7,4},{8,9},{9,10},{10,1... | collective-permute-start | bytes 104 | tf_op jit(solution)/shard_map/ppermute | solution.py:132
  217.9 5.1 %collective-permute-start.11 = (f32[8]{0:T(128)S(1)}, f32[8]{0:T(128)S(1)}, u32[]{:S(2)}, u32[]{:S(2)}) collective-permute-start(f32[8]{0:T(128)S(1)} %get-tuple-element.17), channel_id=1, source_target_pairs={{0,2},{1,3},{2,0},{3,1},{4,6},{5,7},{6,4},{7,5},{8,10},{9,11},{10,... | collective-permute-start | bytes 104 | tf_op jit(solution)/shard_map/ppermute | solution.py:132
  220.4 3.6 %collective-permute-start.12 = (f32[8]{0:T(128)S(1)}, f32[8]{0:T(128)S(1)}, u32[]{:S(2)}, u32[]{:S(2)}) collective-permute-start(f32[8]{0:T(128)S(1)} %get-tuple-element.17), channel_id=1, source_target_pairs={{0,3},{1,0},{2,1},{3,2},{4,7},{5,4},{6,5},{7,6},{8,11},{9,8},{10,9... | collective-permute-start | bytes 104 | tf_op jit(solution)/shard_map/ppermute | solution.py:132
  231.0 21.5 %copy-start.1 = (f32[8,1024]{1,0:T(8,128)S(1)}, f32[8,1024]{1,0:T(8,128)}, u32[]{:S(2)}) copy-start(f32[8,1024]{1,0:T(8,128)} %param.8) | copy-start | bytes 98308

commit v2 on v0

--- a/solution.py
+++ b/solution.py
@@ -90,6 +90,38 @@
     )(ca, sa, cb, sb, inv, lens, cleaned)
 
 
+def harmonic_tile(theta_ref, mv_ref, prof_ref, mw_ref, lc):
+    rows = pl.ds(lc * 256, 256)
+    h = jnp.dot(theta_ref[rows, :], mv_ref[...], preferred_element_type=jnp.float32)
+    return h * prof_ref[0, rows, :] * mw_ref[...]
+
+
+def power_kernel(theta_ref, mv_ref, prof_ref, mw_ref, o_ref):
+    total = jnp.zeros((1, 1), jnp.float32)
+    for lc in range(theta_ref.shape[0] // 256):
+        w = harmonic_tile(theta_ref, mv_ref, prof_ref, mw_ref, lc)
+        total = total + jnp.sum(w * w, keepdims=True)
+    o_ref[0] = jnp.broadcast_to(total, (1, 128))
+
+
+def output_kernel(theta_ref, mv_ref, prof_ref, mw_ref, scale_ref, o_ref):
+    scale = scale_ref[0][:, 0:1]
+    half = mv_ref.shape[1] // 2
+    for lc in range(theta_ref.shape[0] // 256):
+        w = harmonic_tile(theta_ref, mv_ref, prof_ref, mw_ref, lc) * scale
+        for p in range(2):
+            o_ref[pl.ds(lc * 256, 256), 0, p, :] = w[:, p * half : (p + 1) * half]
+
+
+def harmonic_specs(n_l, n_cycle, width):
+    return [
+        pl.BlockSpec((n_l, n_cycle), lambda c: (0, 0)),
+        pl.BlockSpec((n_cycle, width), lambda c: (0, c)),
+        pl.BlockSpec((1, n_l, 1), lambda c: (c, 0, 0)),
+        pl.BlockSpec((1, width), lambda c: (0, 0)),
+    ]
+
+
 def theta_table(cycle_ids, n_cycle):
     degrees = jnp.arange(L, dtype=jnp.int32)
     odd = 2 * cycle_ids + 1
@@ -163,20 +195,36 @@
     moved = lax.all_to_all(sendbuf, ("blk", "grp"), 0, 0, tiled=True)
     moved = moved.reshape(n_cycle, chan_dev * 2 * M_DEV)
     theta_tab = theta_table(jnp.arange(n_cycle, dtype=jnp.int32), n_cycle)
-    harmonic = jnp.dot(theta_tab, moved, preferred_element_type=jnp.float32).reshape(
-        L, chan_dev, 2, M_DEV
-    )
     onehot = (
         beam_index[:, None] == jnp.arange(beam_profile.shape[0], dtype=jnp.int32)[None, :]
     ).astype(jnp.float32)
     profiles = jnp.dot(onehot, beam_profile, precision=lax.Precision.HIGHEST)
-    shaped = harmonic * profiles.T[:, :, None, None]
     orders = lax.axis_index("grp") * M_DEV + jnp.arange(M_DEV, dtype=jnp.int32)
     mweight = 0.25 + orders.astype(jnp.float32) / m_width
-    weighted = shaped * mweight[None, None, None, :]
-    power_part = jnp.sum(weighted * weighted, axis=(0, 2, 3))
+    mw_row = jnp.concatenate([mweight, mweight])[None, :]
+    prof_col = profiles[:, :, None]
+    width = 2 * M_DEV
+    specs = harmonic_specs(L, n_cycle, width)
+    vmem = pltpu.CompilerParams(vmem_limit_bytes=32 * 1024 * 1024)
+    power_part = pl.pallas_call(
+        power_kernel,
+        grid=(chan_dev,),
+        in_specs=specs,
+        out_specs=pl.BlockSpec((1, 1, 128), lambda c: (c, 0, 0)),
+        out_shape=jax.ShapeDtypeStruct((chan_dev, 1, 128), jnp.float32),
+        compiler_params=vmem,
+    )(theta_tab, moved, prof_col, mw_row)[:, 0, 0]
     power = ring_sum(power_part, subs[3:])
-    return weighted * lax.rsqrt(power / (2.0 * L * m_width) + 1e-06)[None, :, None, None]
+    scale = lax.rsqrt(power / (2.0 * L * m_width) + 1e-06)
+    scale = jnp.broadcast_to(scale[:, None, None], (chan_dev, 1, 128))
+    return pl.pallas_call(
+        output_kernel,
+        grid=(chan_dev,),
+        in_specs=specs + [pl.BlockSpec((1, 1, 128), lambda c: (c, 0, 0))],
+        out_specs=pl.BlockSpec((L, 1, 2, M_DEV), lambda c: (0, c, 0, 0)),
+        out_shape=jax.ShapeDtypeStruct((L, chan_dev, 2, M_DEV), jnp.float32),
+        compiler_params=vmem,
+    )(theta_tab, moved, prof_col, mw_row, scale)
 
 
 def solution(mesh):

time: 233 us -> 201 us (0.86)
  local copies, waits for them, and re-layouts: 50.3 us -> 26.7 us
  Pallas kernels: 24.6 us -> 43.7 us
  matrix products: 32.9 us -> 15.6 us
  waiting for transfers between devices: 76.9 us -> 66.4 us
    mul x1 -> x0, local copies, waits for them, and re-layouts: 21.5 us -> none  [body(): weighted * lax.rsqrt(power / (2.0 * L * m_width) + 1e-06)[None, :, None,...]
    pallas_call x0 -> x2, Pallas kernels: none -> 19.2 us  [the longest x1 11.2 us: body(): pl.pallas_call(output_kernel, grid=(chan_dev,), in_specs=specs + [pl.Bloc...]
    dot_general x1 -> x0, matrix products: 17.2 us -> none  [body(): jnp.dot(theta_tab, moved, preferred_element_type=jnp.float32)]
    transpose x0 -> x1, local copies, waits for them, and re-layouts: none -> 11.1 us  [body(): fourier.transpose(1, 4, 0, 2, 3, 5)]
    all_to_all x1, waiting for transfers between devices: 50.9 us -> 40.4 us  [body(): moved = lax.all_to_all(sendbuf, ('blk', 'grp'), 0, 0, tiled=True)]
    all_to_all x1 -> x0, local copies, waits for them, and re-layouts: 9.46 us -> none  [body(): moved = lax.all_to_all(sendbuf, ('blk', 'grp'), 0, 0, tiled=True)]
    convert_element_type x0 -> x1, other arithmetic: none -> 7.96 us  [theta_table(): return (jnp.cos(angle) * weight[None, :]).astype(jnp.bfloat16)]
    mul x1 -> x0, other arithmetic: 7.03 us -> none  [body(): weighted * lax.rsqrt(power / (2.0 * L * m_width) + 1e-06)[None, :, None,...]
  transfers between devices with their start and end apart: 14 -> 14, of which waited for: 13 -> 13; matrix products, arithmetic and copies ran while one was open for 5% -> 11% of each run, Pallas kernels for 0% -> 0%
where the time goes in v2:
time: 201 us
  waiting for transfers between devices  66.4 us (33%)
  Pallas kernels  43.7 us (22%)
  local copies, waits for them, and re-layouts  26.7 us (13%)
  other arithmetic  24.3 us (12%)
  starting transfers between devices  23.7 us (12%)
  matrix products  15.6 us (8%)
    all_to_all x1, waiting for transfers between devices, body(): moved = lax.all_to_all(sendbuf, ('blk', 'grp'), 0, 0, tiled=True)  40.4 us
    ppermute x13, waiting for transfers between devices, ring_sum(): lax.ppermute(v, axis, shift_perm(size, stride, total, k))  26 us
    pallas_call x1, Pallas kernels, cycle_fourier(): pl.pallas_call(fourier_kernel, grid=(n_cyc,), in_specs=[pl.BlockSpec((1,...  24.6 us
    ppermute x13, starting transfers between devices, ring_sum(): lax.ppermute(v, axis, shift_perm(size, stride, total, k))  17.7 us
    pallas_call x1, Pallas kernels, body(): pl.pallas_call(output_kernel, grid=(chan_dev,), in_specs=specs + [pl.Bloc...  11.2 us
    transpose x1, local copies, waits for them, and re-layouts, body(): fourier.transpose(1, 4, 0, 2, 3, 5)  11.1 us
    dot_general x1, matrix products, body(): correction = jnp.dot(projected.T, basis, precision=lax.Precision.HIGHEST)  10.3 us
    cos x2, other arithmetic, cos_sin_of_phase(): return (jnp.cos(angle), jnp.sin(angle))  8.81 us
  transfers between devices with their start and end apart: 14, of which 13 were waited for; matrix products, arithmetic and copies ran while one was open for 11% of the time, Pallas kernels for 0%

profile of v2, /device:TPU:0, one launch (start us, length us, event | category | flops | bytes accessed | tf_op | source)
XLA Modules:
  0.0 200.7 jit_solution(598035482231822436)
XLA Ops:
  0.8 3.0 %convolution_convert_fusion = bf16[8192,16]{0,1:T(8,128)(2,1)S(1)} fusion(bf16[256,16]{0,1:T(8,128)(2,1)} %param.6, bf16[256,8192]{1,0:T(8,128)(2,1)} %param.5, pred[8192]{0:T(1024)(128)(4,1)S(1)} %bitcast.37), kind=kOutput, calls=%fused_computation.2 | convolution fusion | flops 69337088 | bytes 4472832 | tf_op jit(solution)/shard_map/dot_general | solution.py:173
  6.0 7.0 %fusion.35 = (f32[4,16,1024]{2,1,0:T(8,128)S(1)}, f32[4,16,1024]{2,1,0:T(8,128)S(1)}, f32[4,16,1024]{2,1,0:T(8,128)S(1)}, f32[4,16,1024]{2,1,0:T(8,128)S(1)}) fusion(f32[4]{0:T(128)S(1)} %get-tuple-element.16, pred[4]{0:T(512)(128)(4,1)S(1)} %broadcast_compare_fusion, s32[4]{0:T(128)S(1)} %get-tuple-element.15, s32[16,1024]{1,0:T(8,128)S(1)} %iota_multiply_fusion, ...), kind=kLoop, calls=%fused_computation.55 | loop fusion | flops 1376256 | bytes 1114404 | tf_op jit(solution)/shard_map/cos | solution.py:16
  13.3 2.9 %collective-permute-start.3 = (f32[16,272]{0,1:T(8,128)S(1)}, f32[16,272]{0,1:T(8,128)S(1)}, u32[]{:S(2)}, u32[]{:S(2)}) collective-permute-start(f32[16,272]{0,1:T(8,128)S(1)} %add.192), channel_id=1, source_target_pairs={{0,24},{4,28},{8,0},{12,4},{16,8},{20,12},{24,16},{28,20},{32,56},... | collective-permute-start | bytes 52232 | tf_op jit(solution)/shard_map/ppermute | solution.py:155
  19.7 3.0 %collective-permute-done.3 = f32[16,272]{0,1:T(8,128)S(1)} collective-permute-done((f32[16,272]{0,1:T(8,128)S(1)}, f32[16,272]{0,1:T(8,128)S(1)}, u32[]{:S(2)}, u32[]{:S(2)}) %collective-permute-start.3) | collective-permute-done | bytes 17440 | tf_op jit(solution)/shard_map/ppermute | solution.py:155
  24.3 2.2 %collective-permute-done.1 = f32[16,272]{0,1:T(8,128)S(1)} collective-permute-done((f32[16,272]{0,1:T(8,128)S(1)}, f32[16,272]{0,1:T(8,128)S(1)}, u32[]{:S(2)}, u32[]{:S(2)}) %collective-permute-start.1) | collective-permute-done | bytes 17440 | tf_op jit(solution)/shard_map/ppermute | solution.py:155
  26.5 3.1 %collective-permute-start.6 = (f32[16,272]{0,1:T(8,128)S(1)}, f32[16,272]{0,1:T(8,128)S(1)}, u32[]{:S(2)}, u32[]{:S(2)}) collective-permute-start(f32[16,272]{0,1:T(8,128)S(1)} %add_add_fusion.2), channel_id=1, source_target_pairs={{0,96},{4,100},{8,104},{12,108},{16,112},{20,116},{24,120},{28,124... | collective-permute-start | bytes 52232 | tf_op jit(solution)/shard_map/ppermute | solution.py:155
  31.2 2.0 multiply_add_fusion
  33.2 2.5 %collective-permute-done.6 = f32[16,272]{0,1:T(8,128)S(1)} collective-permute-done((f32[16,272]{0,1:T(8,128)S(1)}, f32[16,272]{0,1:T(8,128)S(1)}, u32[]{:S(2)}, u32[]{:S(2)}) %collective-permute-start.6) | collective-permute-done | bytes 17440 | tf_op jit(solution)/shard_map/ppermute | solution.py:155
  35.7 2.0 collective-permute-done.5
  39.4 4.1 %collective-permute-start.9 = (f32[16,272]{0,1:T(8,128)S(1)}, f32[16,272]{0,1:T(8,128)S(1)}, u32[]{:S(2)}, u32[]{:S(2)}) collective-permute-start(f32[16,272]{0,1:T(8,128)S(1)} %add_add_fusion.1), channel_id=1, source_target_pairs={{0,3},{1,0},{2,1},{3,2},{4,7},{5,4},{6,5},{7,6},{8,11},{9,8},{10,9... | collective-permute-start | bytes 52232 | tf_op jit(solution)/shard_map/ppermute | solution.py:155
  44.8 4.8 %collective-permute-done.9 = f32[16,272]{0,1:T(8,128)S(1)} collective-permute-done((f32[16,272]{0,1:T(8,128)S(1)}, f32[16,272]{0,1:T(8,128)S(1)}, u32[]{:S(2)}, u32[]{:S(2)}) %collective-permute-start.9) | collective-permute-done | bytes 17440 | tf_op jit(solution)/shard_map/ppermute | solution.py:155
  57.9 10.3 %fusion.x_ref = bf16[256,8192]{1,0:T(8,128)(2,1)} fusion(f32[16,256]{1,0:T(8,128)S(1)} %fusion.28, f32[16,8192]{1,0:T(8,128)S(1)} %fusion.42, bf16[256,8192]{1,0:T(8,128)(2,1)} %param.5, pred[8192]{0:T(1024)(128)(4,1)S(1)} %bitcast.39), kind=kOutput, calls=%fused_computation.1 | convolution fusion | flops 411041792 | bytes 8937472 | tf_op jit(solution)/shard_map/dot_general | solution.py:188
  68.3 24.6 %shard_map.55 = bf16[4,256,2048]{2,1,0:T(8,128)(2,1)} custom-call(f32[4,16,1024]{2,1,0:T(8,128)S(1)} %get-tuple-element.13.ca_ref, f32[4,16,1024]{2,1,0:T(8,128)S(1)} %get-tuple-element.14.sa_ref, f32[4,128,1024]{2,1,0:T(8,128)S(1)} %bitcast.32, f32[4,128,1024]{2,1,0:T(8,128)S(1)} %bitcast.31, f32[4,1,128]{2,1,0:T(1,128)S(1)} %broadcast_in_dim.24.inv_ref, ...), custom_call_target="tpu_custom_call" | custom-call | tf_op jit(solution)/shard_map/pallas_call | solution.py:74
  92.9 11.1 %copy.19 = bf16[32,4,4,8,2,256]{5,4,3,2,1,0:T(2,128)(2,1)} copy(bf16[32,4,4,8,2,256]{5,3,1,4,0,2:T(8,128)(2,1)} %bitcast.36) | data formatting | bytes 8388608 | tf_op jit(solution)/shard_map/transpose | solution.py:192
  104.0 6.0 %all-to-all-start = ((bf16[128,4,8,2,256]{4,3,2,1,0:T(2,128)(2,1)}), bf16[128,4,8,2,256]{4,3,2,1,0:T(2,128)(2,1)}, u32[]{:S(2)}, u32[]{:S(2)}) async-start(bf16[128,4,8,2,256]{4,3,2,1,0:T(2,128)(2,1)} %bitcast.35), calls=%async_computation | async-start | bytes 8388608 | tf_op jit(solution)/shard_map/all_to_all | solution.py:195
  110.2 2.7 %copy.21.prof_ref = f32[8,1024,1]{2,1,0:T(8,128)} copy(f32[8,1024,1]{1,0,2:T(8,128)S(1)} %convolution_bitcast_fusion) | data formatting | bytes 65536 | tf_op jit(solution)/shard_map/broadcast_in_dim | solution.py:205
  113.0 8.0 %fusion.7.theta_ref = bf16[1024,512]{1,0:T(8,128)(2,1)S(1)} fusion(f32[512]{0:T(512)S(1)} %sine_multiply_fusion, s32[512]{0:T(512)S(1)} %multiply_add_fusion.1), kind=kLoop, calls=%fused_computation.13 | loop fusion | flops 8388608 | bytes 1052672 | tf_op jit(solution)/shard_map/convert_element_type | solution.py:133
  120.9 40.4 %all-to-all-done = bf16[128,4,8,2,256]{4,3,2,1,0:T(2,128)(2,1)} async-done(((bf16[128,4,8,2,256]{4,3,2,1,0:T(2,128)(2,1)}), bf16[128,4,8,2,256]{4,3,2,1,0:T(2,128)(2,1)}, u32[]{:S(2)}, u32[]{:S(2)}) %all-to-all-start) | async-done | bytes 4194336 | tf_op jit(solution)/shard_map/all_to_all | solution.py:195
  161.4 7.8 %reshape.297.mv_ref = bf16[512,4096]{1,0:T(8,128)(2,1)} reshape(bf16[128,4,8,2,256]{4,3,2,1,0:T(2,128)(2,1)} %all-to-all-done) | data formatting | bytes 8388608 | tf_op jit(solution)/shard_map/reshape | solution.py:196
  169.1 2.2 %copy-done.1 = f32[8,1024,1]{2,1,0:T(8,128)S(1)} copy-done((f32[8,1024,1]{2,1,0:T(8,128)S(1)}, f32[8,1024,1]{2,1,0:T(8,128)}, u32[]{:S(2)}) %copy-start.1) | copy-done | bytes 32792
  171.3 2.2 %copy-done.2 = bf16[512,4096]{1,0:T(8,128)(2,1)S(1)} copy-done((bf16[512,4096]{1,0:T(8,128)(2,1)S(1)}, bf16[512,4096]{1,0:T(8,128)(2,1)}, u32[]{:S(2)}) %copy-start.2) | copy-done | bytes 4194328
  173.5 7.9 %shard_map.56 = f32[8,1,128]{2,1,0:T(1,128)S(1)} custom-call(bf16[1024,512]{1,0:T(8,128)(2,1)S(1)} %fusion.7.theta_ref, bf16[512,4096]{1,0:T(8,128)(2,1)S(1)} %copy-done.2, f32[8,1024,1]{2,1,0:T(8,128)S(1)} %copy-done.1, f32[1,512]{1,0:T(1,128)S(1)} %bitcast.33), custom_call_target="tpu_custom_call" | custom-call | tf_op jit(solution)/shard_map/pallas_call | solution.py:209
  185.2 3.4 %collective-permute-done.11 = f32[8]{0:T(128)S(1)} collective-permute-done((f32[8]{0:T(128)S(1)}, f32[8]{0:T(128)S(1)}, u32[]{:S(2)}, u32[]{:S(2)}) %collective-permute-start.11) | collective-permute-done | bytes 64 | tf_op jit(solution)/shard_map/ppermute | solution.py:155
  189.4 11.2 %shard_map.57 = f32[1024,8,2,256]{3,2,1,0:T(2,128)} custom-call(bf16[1024,512]{1,0:T(8,128)(2,1)S(1)} %fusion.7.theta_ref, bf16[512,4096]{1,0:T(8,128)(2,1)S(1)} %copy-done.2, f32[8,1024,1]{2,1,0:T(8,128)S(1)} %copy-done.1, f32[1,512]{1,0:T(1,128)S(1)} %bitcast.34, f32[8,1,128]{2,1,0:T(1,128)S(1)} %broadcast_in_dim.30.scale_ref), custom_call_target="tpu_custom_call" | custom-call | tf_op jit(solution)/shard_map/pallas_call | solution.py:220
  (69 shorter events, 26.1 us)
Async XLA Ops:
  0.0 110.0 %copy-start = (f32[8,1024]{1,0:T(8,128)S(1)}, f32[8,1024]{1,0:T(8,128)}, u32[]{:S(2)}) copy-start(f32[8,1024]{1,0:T(8,128)} %param.8) | copy-start | bytes 98308
  0.8 3.5 %copy-start.4 = (bf16[256,8192]{1,0:T(8,128)(2,1)S(1)}, bf16[256,8192]{1,0:T(8,128)(2,1)}, u32[]{:S(2)}) copy-start(bf16[256,8192]{1,0:T(8,128)(2,1)} %param.5) | copy-start | bytes 12582916
  4.2 1.5 copy-start.5
  5.6 7.6 %collective-permute-start = (f32[16,272]{0,1:T(8,128)S(1)}, f32[16,272]{0,1:T(8,128)S(1)}, u32[]{:S(2)}, u32[]{:S(2)}) collective-permute-start(f32[16,272]{0,1:T(8,128)S(1)} %copy.17), channel_id=1, source_target_pairs={{0,4},{4,0},{8,12},{12,8},{16,20},{20,16},{24,28},{28,24},{32,36},... | collective-permute-start | bytes 52232 | tf_op jit(solution)/shard_map/ppermute | solution.py:155
  13.3 9.5 %collective-permute-start.3 = (f32[16,272]{0,1:T(8,128)S(1)}, f32[16,272]{0,1:T(8,128)S(1)}, u32[]{:S(2)}, u32[]{:S(2)}) collective-permute-start(f32[16,272]{0,1:T(8,128)S(1)} %add.192), channel_id=1, source_target_pairs={{0,24},{4,28},{8,0},{12,4},{16,8},{20,12},{24,16},{28,20},{32,56},... | collective-permute-start | bytes 52232 | tf_op jit(solution)/shard_map/ppermute | solution.py:155
  16.2 8.1 %collective-permute-start.2 = (f32[16,272]{0,1:T(8,128)S(1)}, f32[16,272]{0,1:T(8,128)S(1)}, u32[]{:S(2)}, u32[]{:S(2)}) collective-permute-start(f32[16,272]{0,1:T(8,128)S(1)} %add.192), channel_id=1, source_target_pairs={{0,16},{4,20},{8,24},{12,28},{16,0},{20,4},{24,8},{28,12},{32,48},... | collective-permute-start | bytes 52232 | tf_op jit(solution)/shard_map/ppermute | solution.py:155
  17.0 9.5 %collective-permute-start.1 = (f32[16,272]{0,1:T(8,128)S(1)}, f32[16,272]{0,1:T(8,128)S(1)}, u32[]{:S(2)}, u32[]{:S(2)}) collective-permute-start(f32[16,272]{0,1:T(8,128)S(1)} %add.192), channel_id=1, source_target_pairs={{0,8},{4,12},{8,16},{12,20},{16,24},{20,28},{24,0},{28,4},{32,40},... | collective-permute-start | bytes 52232 | tf_op jit(solution)/shard_map/ppermute | solution.py:155
  26.5 9.2 %collective-permute-start.6 = (f32[16,272]{0,1:T(8,128)S(1)}, f32[16,272]{0,1:T(8,128)S(1)}, u32[]{:S(2)}, u32[]{:S(2)}) collective-permute-start(f32[16,272]{0,1:T(8,128)S(1)} %add_add_fusion.2), channel_id=1, source_target_pairs={{0,96},{4,100},{8,104},{12,108},{16,112},{20,116},{24,120},{28,124... | collective-permute-start | bytes 52232 | tf_op jit(solution)/shard_map/ppermute | solution.py:155
  29.6 8.1 %collective-permute-start.5 = (f32[16,272]{0,1:T(8,128)S(1)}, f32[16,272]{0,1:T(8,128)S(1)}, u32[]{:S(2)}, u32[]{:S(2)}) collective-permute-start(f32[16,272]{0,1:T(8,128)S(1)} %add_add_fusion.2), channel_id=1, source_target_pairs={{0,64},{4,68},{8,72},{12,76},{16,80},{20,84},{24,88},{28,92},{32,9... | collective-permute-start | bytes 52232 | tf_op jit(solution)/shard_map/ppermute | solution.py:155
  30.2 9.2 %collective-permute-start.4 = (f32[16,272]{0,1:T(8,128)S(1)}, f32[16,272]{0,1:T(8,128)S(1)}, u32[]{:S(2)}, u32[]{:S(2)}) collective-permute-start(f32[16,272]{0,1:T(8,128)S(1)} %add_add_fusion.2), channel_id=1, source_target_pairs={{0,32},{4,36},{8,40},{12,44},{16,48},{20,52},{24,56},{28,60},{32,6... | collective-permute-start | bytes 52232 | tf_op jit(solution)/shard_map/ppermute | solution.py:155
  39.4 10.2 %collective-permute-start.9 = (f32[16,272]{0,1:T(8,128)S(1)}, f32[16,272]{0,1:T(8,128)S(1)}, u32[]{:S(2)}, u32[]{:S(2)}) collective-permute-start(f32[16,272]{0,1:T(8,128)S(1)} %add_add_fusion.1), channel_id=1, source_target_pairs={{0,3},{1,0},{2,1},{3,2},{4,7},{5,4},{6,5},{7,6},{8,11},{9,8},{10,9... | collective-permute-start | bytes 52232 | tf_op jit(solution)/shard_map/ppermute | solution.py:155
  43.5 8.0 %collective-permute-start.8 = (f32[16,272]{0,1:T(8,128)S(1)}, f32[16,272]{0,1:T(8,128)S(1)}, u32[]{:S(2)}, u32[]{:S(2)}) collective-permute-start(f32[16,272]{0,1:T(8,128)S(1)} %add_add_fusion.1), channel_id=1, source_target_pairs={{0,2},{1,3},{2,0},{3,1},{4,6},{5,7},{6,4},{7,5},{8,10},{9,11},{10,... | collective-permute-start | bytes 52232 | tf_op jit(solution)/shard_map/ppermute | solution.py:155
  43.5 9.5 %collective-permute-start.7 = (f32[16,272]{0,1:T(8,128)S(1)}, f32[16,272]{0,1:T(8,128)S(1)}, u32[]{:S(2)}, u32[]{:S(2)}) collective-permute-start(f32[16,272]{0,1:T(8,128)S(1)} %add_add_fusion.1), channel_id=1, source_target_pairs={{0,1},{1,2},{2,3},{3,0},{4,5},{5,6},{6,7},{7,4},{8,9},{9,10},{10,1... | collective-permute-start | bytes 52232 | tf_op jit(solution)/shard_map/ppermute | solution.py:155
  57.9 10.5 %copy-start.3 = (f32[4,8,16,1024]{3,2,1,0:T(8,128)S(1)}, f32[4,8,16,1024]{3,2,1,0:T(8,128)}, u32[]{:S(2)}) copy-start(f32[4,8,16,1024]{3,2,1,0:T(8,128)} %get-tuple-element.6) | copy-start | bytes 6291460
  104.0 6.0 %copy-start.6 = (s32[8]{0:T(128)S(1)}, s32[8]{0:T(128)}, u32[]{:S(2)}) copy-start(s32[8]{0:T(128)} %param.9) | copy-start | bytes 100
  104.0 57.4 %all-to-all-start = ((bf16[128,4,8,2,256]{4,3,2,1,0:T(2,128)(2,1)}), bf16[128,4,8,2,256]{4,3,2,1,0:T(2,128)(2,1)}, u32[]{:S(2)}, u32[]{:S(2)}) async-start(bf16[128,4,8,2,256]{4,3,2,1,0:T(2,128)(2,1)} %bitcast.35), calls=%async_computation | async-start | bytes 8388608 | tf_op jit(solution)/shard_map/all_to_all | solution.py:195
  169.1 2.2 %copy-start.1 = (f32[8,1024,1]{2,1,0:T(8,128)S(1)}, f32[8,1024,1]{2,1,0:T(8,128)}, u32[]{:S(2)}) copy-start(f32[8,1024,1]{2,1,0:T(8,128)} %copy.21.prof_ref) | copy-start | bytes 98308
  171.3 2.2 %copy-start.2 = (bf16[512,4096]{1,0:T(8,128)(2,1)S(1)}, bf16[512,4096]{1,0:T(8,128)(2,1)}, u32[]{:S(2)}) copy-start(bf16[512,4096]{1,0:T(8,128)(2,1)} %reshape.297.mv_ref) | copy-start | bytes 12582916
  181.6 3.6 %collective-permute-start.12 = (f32[8]{0:T(128)S(1)}, f32[8]{0:T(128)S(1)}, u32[]{:S(2)}, u32[]{:S(2)}) collective-permute-start(f32[8]{0:T(128)S(1)} %slice_reduce_fusion), channel_id=1, source_target_pairs={{0,3},{1,0},{2,1},{3,2},{4,7},{5,4},{6,5},{7,6},{8,11},{9,8},{10,9... | collective-permute-start | bytes 104 | tf_op jit(solution)/shard_map/ppermute | solution.py:155
  183.6 5.1 %collective-permute-start.11 = (f32[8]{0:T(128)S(1)}, f32[8]{0:T(128)S(1)}, u32[]{:S(2)}, u32[]{:S(2)}) collective-permute-start(f32[8]{0:T(128)S(1)} %slice_reduce_fusion), channel_id=1, source_target_pairs={{0,2},{1,3},{2,0},{3,1},{4,6},{5,7},{6,4},{7,5},{8,10},{9,11},{10,... | collective-permute-start | bytes 104 | tf_op jit(solution)/shard_map/ppermute | solution.py:155
  184.6 4.8 %collective-permute-start.10 = (f32[8]{0:T(128)S(1)}, f32[8]{0:T(128)S(1)}, u32[]{:S(2)}, u32[]{:S(2)}) collective-permute-start(f32[8]{0:T(128)S(1)} %slice_reduce_fusion), channel_id=1, source_target_pairs={{0,1},{1,2},{2,3},{3,0},{4,5},{5,6},{6,7},{7,4},{8,9},{9,10},{10,1... | collective-permute-start | bytes 104 | tf_op jit(solution)/shard_map/ppermute | solution.py:155

commit v3 on v2

--- a/solution.py
+++ b/solution.py
@@ -37,8 +37,13 @@
     return ca, sa, cb, sb
 
 
-def fourier_kernel(ca_ref, sa_ref, cb_ref, sb_ref, inv_ref, len_ref, x_ref, o_ref, tab_ref):
+def fourier_kernel(
+    ca_ref, sa_ref, cb_ref, sb_ref, inv_ref, len_ref, sky_ref, proj_ref, basis_ref, o_ref,
+    tab_ref, clean_ref,
+):
     m_width = cb_ref.shape[2]
+    n_grp = o_ref.shape[0] // (sky_ref.shape[0] // o_ref.shape[1])
+    chan_dev = o_ref.shape[1]
     inv = inv_ref[0][:, 0:1]
     length = len_ref[0][:, 0:1]
 
@@ -56,21 +61,41 @@
         return carry
 
     lax.fori_loop(0, RPIX // J_LO, build, 0)
-    width = 2 * m_width
-    step = 512
-    for q in range(width // step):
-        o_ref[0, :, q * step : (q + 1) * step] = jnp.dot(
-            x_ref[...], tab_ref[:, q * step : (q + 1) * step], preferred_element_type=jnp.float32
-        ).astype(jnp.bfloat16)
-
-
-def cycle_fourier(cleaned, cycle_len, m_width):
+    cols = lax.broadcasted_iota(jnp.int32, (1, RPIX), 1)
+    masked = jnp.where(cols < length, sky_ref[...].astype(jnp.float32), 0.0)
+    correction = jnp.dot(
+        proj_ref[...], basis_ref[...], preferred_element_type=jnp.float32,
+        precision=lax.Precision.HIGHEST,
+    )
+    clean_ref[...] = (masked - correction).astype(jnp.bfloat16)
+    m_dev = m_width // n_grp
+    step = 2 * m_dev
+    n_blk = sky_ref.shape[0] // chan_dev
+    for q in range(2 * m_width // step):
+        res = jnp.dot(
+            clean_ref[...], tab_ref[:, q * step : (q + 1) * step], preferred_element_type=jnp.float32
+        )
+        part = (q * step) // m_width
+        for h in range(step // m_dev):
+            grp_dest = (q * step - part * m_width) // m_dev + h
+            for blk_dest in range(n_blk):
+                slab = res[blk_dest * chan_dev : (blk_dest + 1) * chan_dev, h * m_dev : (h + 1) * m_dev]
+                o_ref[blk_dest * n_grp + grp_dest, :, part * m_dev : (part + 1) * m_dev] = slab.astype(
+                    jnp.bfloat16
+                )
+
+
+def cycle_fourier(sky_map, projected_t, basis, cycle_len, m_width, n_blk, n_grp):
     n_cyc = cycle_len.shape[0]
-    n_chan = cleaned.shape[0]
+    n_chan = sky_map.shape[0]
+    n_mode = basis.shape[0]
+    n_dev = n_blk * n_grp
+    chan_dev = n_chan // n_blk
     ca, sa, cb, sb = small_tables(cycle_len, m_width)
     inv = jnp.broadcast_to(lax.rsqrt(cycle_len.astype(jnp.float32))[:, None, None], (n_cyc, 1, 128))
     lens = jnp.broadcast_to(cycle_len[:, None, None], (n_cyc, 1, 128))
     n_hi = RPIX // J_LO
+    m_dev = m_width // n_grp
     return pl.pallas_call(
         fourier_kernel,
         grid=(n_cyc,),
@@ -82,12 +107,17 @@
             pl.BlockSpec((1, 1, 128), lambda k: (k, 0, 0)),
             pl.BlockSpec((1, 1, 128), lambda k: (k, 0, 0)),
             pl.BlockSpec((n_chan, RPIX), lambda k: (0, k)),
+            pl.BlockSpec((n_chan, n_mode), lambda k: (0, 0)),
+            pl.BlockSpec((n_mode, RPIX), lambda k: (0, k)),
         ],
-        out_specs=pl.BlockSpec((1, n_chan, 2 * m_width), lambda k: (k, 0, 0)),
-        out_shape=jax.ShapeDtypeStruct((n_cyc, n_chan, 2 * m_width), jnp.bfloat16),
-        scratch_shapes=[pltpu.VMEM((RPIX, 2 * m_width), jnp.bfloat16)],
+        out_specs=pl.BlockSpec((n_dev, None, chan_dev, 2 * m_dev), lambda k: (0, k, 0, 0)),
+        out_shape=jax.ShapeDtypeStruct((n_dev, n_cyc, chan_dev, 2 * m_dev), jnp.bfloat16),
+        scratch_shapes=[
+            pltpu.VMEM((RPIX, 2 * m_width), jnp.bfloat16),
+            pltpu.VMEM((n_chan, RPIX), jnp.bfloat16),
+        ],
         compiler_params=pltpu.CompilerParams(vmem_limit_bytes=48 * 1024 * 1024),
-    )(ca, sa, cb, sb, inv, lens, cleaned)
+    )(ca, sa, cb, sb, inv, lens, sky_map, projected_t, basis)
 
 
 def harmonic_tile(theta_ref, mv_ref, prof_ref, mw_ref, lc):
@@ -185,13 +215,7 @@
     lower = jnp.linalg.cholesky(gram_sum)
     basis = jax.scipy.linalg.solve_triangular(lower, amps_wide, lower=True)
     projected = jax.scipy.linalg.solve_triangular(lower, cross_sum, lower=True)
-    correction = jnp.dot(projected.T, basis, precision=lax.Precision.HIGHEST)
-    cleaned = (masked.astype(jnp.float32) - correction).astype(jnp.bfloat16)
-    fourier = cycle_fourier(cleaned, cycle_len, m_width)
-    fourier = fourier.reshape(cycle_dev, n_blk, chan_dev, 2, n_grp, M_DEV)
-    sendbuf = fourier.transpose(1, 4, 0, 2, 3, 5).reshape(
-        n_blk * n_grp, cycle_dev, chan_dev, 2, M_DEV
-    )
+    sendbuf = cycle_fourier(sky_map, projected.T, basis, cycle_len, m_width, n_blk, n_grp)
     moved = lax.all_to_all(sendbuf, ("blk", "grp"), 0, 0, tiled=True)
     moved = moved.reshape(n_cycle, chan_dev * 2 * M_DEV)
     theta_tab = theta_table(jnp.arange(n_cycle, dtype=jnp.int32), n_cycle)

time: 201 us -> 180 us (0.90)
  local copies, waits for them, and re-layouts: 26.7 us -> 9.88 us
  matrix products: 15.6 us -> 5.29 us
  Pallas kernels: 43.7 us -> 50.3 us
    transpose x1 -> x0, local copies, waits for them, and re-layouts: 11.1 us -> none  [body(): fourier.transpose(1, 4, 0, 2, 3, 5)]
    dot_general x1 -> x0, matrix products: 10.3 us -> none  [body(): correction = jnp.dot(projected.T, basis, precision=lax.Precision.HIGHEST)]
    reshape x1 -> x0, local copies, waits for them, and re-layouts: 7.78 us -> none  [body(): moved = moved.reshape(n_cycle, chan_dev * 2 * M_DEV)]
    pallas_call x1, Pallas kernels: 24.6 us -> 31.1 us  [cycle_fourier(): pl.pallas_call(fourier_kernel, grid=(n_cyc,), in_specs=[pl.BlockSpec((1,...]
    unnamed x15 -> x14, local copies, waits for them, and re-layouts: 4.62 us -> 6.66 us
  transfers between devices with their start and end apart: 14 -> 14, of which waited for: 13 -> 13; matrix products, arithmetic and copies ran while one was open for 11% -> 12% of each run, Pallas kernels for 0% -> 0%
where the time goes in v3:
time: 180 us
  waiting for transfers between devices  66.2 us (37%)
  Pallas kernels  50.3 us (28%)
  other arithmetic  24.2 us (13%)
  starting transfers between devices  23.9 us (13%)
  local copies, waits for them, and re-layouts  9.88 us (5%)
  matrix products  5.29 us (3%)
    all_to_all x1, waiting for transfers between devices, body(): moved = lax.all_to_all(sendbuf, ('blk', 'grp'), 0, 0, tiled=True)  40.2 us
    pallas_call x1, Pallas kernels, cycle_fourier(): pl.pallas_call(fourier_kernel, grid=(n_cyc,), in_specs=[pl.BlockSpec((1,...  31.1 us
    ppermute x13, waiting for transfers between devices, ring_sum(): lax.ppermute(v, axis, shift_perm(size, stride, total, k))  26 us
    ppermute x13, starting transfers between devices, ring_sum(): lax.ppermute(v, axis, shift_perm(size, stride, total, k))  17.7 us
    pallas_call x1, Pallas kernels, body(): pl.pallas_call(output_kernel, grid=(chan_dev,), in_specs=specs + [pl.Bloc...  11.2 us
    cos x2, other arithmetic, cos_sin_of_phase(): return (jnp.cos(angle), jnp.sin(angle))  8.81 us
    pallas_call x1, Pallas kernels, body(): pl.pallas_call(power_kernel, grid=(chan_dev,), in_specs=specs, out_specs=...  7.99 us
    convert_element_type x1, other arithmetic, theta_table(): return (jnp.cos(angle) * weight[None, :]).astype(jnp.bfloat16)  7.96 us
  transfers between devices with their start and end apart: 14, of which 13 were waited for; matrix products, arithmetic and copies ran while one was open for 12% of the time, Pallas kernels for 0%

profile of v3, /device:TPU:0, one launch (start us, length us, event | category | flops | bytes accessed | tf_op | source)
XLA Modules:
  0.0 180.1 jit_solution(978150340806999291)
XLA Ops:
  0.8 3.0 %convolution_convert_fusion = bf16[8192,16]{0,1:T(8,128)(2,1)S(1)} fusion(bf16[256,16]{0,1:T(8,128)(2,1)} %param.6, bf16[256,8192]{1,0:T(8,128)(2,1)} %sky_ref.1, pred[8192]{0:T(1024)(128)(4,1)S(1)} %bitcast.34), kind=kOutput, calls=%fused_computation | convolution fusion | flops 69337088 | bytes 4472832 | tf_op jit(solution)/shard_map/dot_general | solution.py:203
  6.3 7.0 %fusion.34 = (f32[4,16,1024]{2,1,0:T(8,128)S(1)}, f32[4,16,1024]{2,1,0:T(8,128)S(1)}, f32[4,16,1024]{2,1,0:T(8,128)S(1)}, f32[4,16,1024]{2,1,0:T(8,128)S(1)}) fusion(f32[4]{0:T(128)S(1)} %get-tuple-element.16, pred[4]{0:T(512)(128)(4,1)S(1)} %broadcast_compare_fusion, s32[4]{0:T(128)S(1)} %get-tuple-element.15, s32[16,1024]{1,0:T(8,128)S(1)} %iota_multiply_fusion, ...), kind=kLoop, calls=%fused_computation.53 | loop fusion | flops 1376256 | bytes 1114404 | tf_op jit(solution)/shard_map/cos | solution.py:16
  13.5 2.9 %collective-permute-start.3 = (f32[16,272]{0,1:T(8,128)S(1)}, f32[16,272]{0,1:T(8,128)S(1)}, u32[]{:S(2)}, u32[]{:S(2)}) collective-permute-start(f32[16,272]{0,1:T(8,128)S(1)} %add.192), channel_id=1, source_target_pairs={{0,24},{4,28},{8,0},{12,4},{16,8},{20,12},{24,16},{28,20},{32,56},... | collective-permute-start | bytes 52232 | tf_op jit(solution)/shard_map/ppermute | solution.py:185
  18.1 1.8 %fusion.38 = (f32[4,8,1024]{2,1,0:T(8,128)S(1)}, f32[4,8,1024]{2,1,0:T(8,128)S(1)}) fusion(f32[4]{0:T(128)S(1)} %get-tuple-element.16, pred[4]{0:T(512)(128)(4,1)S(1)} %broadcast_compare_fusion, s32[4]{0:T(128)S(1)} %get-tuple-element.15, s32[4,8]{1,0:T(4,128)S(1)} %remainder_select_fusion.1), kind=kLoop, calls=%fused_computation.58 | loop fusion | flops 360448 | bytes 262308 | tf_op jit(solution)/shard_map/cos | solution.py:16
  20.0 3.0 %collective-permute-done.3 = f32[16,272]{0,1:T(8,128)S(1)} collective-permute-done((f32[16,272]{0,1:T(8,128)S(1)}, f32[16,272]{0,1:T(8,128)S(1)}, u32[]{:S(2)}, u32[]{:S(2)}) %collective-permute-start.3) | collective-permute-done | bytes 17440 | tf_op jit(solution)/shard_map/ppermute | solution.py:185
  24.5 2.2 %collective-permute-done.1 = f32[16,272]{0,1:T(8,128)S(1)} collective-permute-done((f32[16,272]{0,1:T(8,128)S(1)}, f32[16,272]{0,1:T(8,128)S(1)}, u32[]{:S(2)}, u32[]{:S(2)}) %collective-permute-start.1) | collective-permute-done | bytes 17440 | tf_op jit(solution)/shard_map/ppermute | solution.py:185
  26.7 3.1 %collective-permute-start.6 = (f32[16,272]{0,1:T(8,128)S(1)}, f32[16,272]{0,1:T(8,128)S(1)}, u32[]{:S(2)}, u32[]{:S(2)}) collective-permute-start(f32[16,272]{0,1:T(8,128)S(1)} %add_add_fusion.2), channel_id=1, source_target_pairs={{0,96},{4,100},{8,104},{12,108},{16,112},{20,116},{24,120},{28,124... | collective-permute-start | bytes 52232 | tf_op jit(solution)/shard_map/ppermute | solution.py:185
  31.4 2.0 %multiply_add_fusion = (f32[4,8,16,1024]{3,2,1,0:T(8,128)S(1)}, f32[4,8,16,1024]{3,2,1,0:T(8,128)}) fusion(f32[4,16,1024]{2,1,0:T(8,128)S(1)} %get-tuple-element.8, f32[4,8,1024]{2,1,0:T(8,128)S(1)} %get-tuple-element.10, f32[4,16,1024]{2,1,0:T(8,128)S(1)} %get-tuple-element.7, f32[4,8,1024]{2,1,0:T(8,128)S(1)} %get-tuple-element.9), kind=kLoop, calls=%fused_computation.14 | loop fusion | flops 3145728 | bytes 4980736 | tf_op jit(solution)/shard_map/add | solution.py:20
  33.4 2.5 %collective-permute-done.6 = f32[16,272]{0,1:T(8,128)S(1)} collective-permute-done((f32[16,272]{0,1:T(8,128)S(1)}, f32[16,272]{0,1:T(8,128)S(1)}, u32[]{:S(2)}, u32[]{:S(2)}) %collective-permute-start.6) | collective-permute-done | bytes 17440 | tf_op jit(solution)/shard_map/ppermute | solution.py:185
  35.9 2.0 %collective-permute-done.5 = f32[16,272]{0,1:T(8,128)S(1)} collective-permute-done((f32[16,272]{0,1:T(8,128)S(1)}, f32[16,272]{0,1:T(8,128)S(1)}, u32[]{:S(2)}, u32[]{:S(2)}) %collective-permute-start.5) | collective-permute-done | bytes 17440 | tf_op jit(solution)/shard_map/ppermute | solution.py:185
  37.9 1.7 collective-permute-done.4
  39.7 4.1 %collective-permute-start.9 = (f32[16,272]{0,1:T(8,128)S(1)}, f32[16,272]{0,1:T(8,128)S(1)}, u32[]{:S(2)}, u32[]{:S(2)}) collective-permute-start(f32[16,272]{0,1:T(8,128)S(1)} %add_add_fusion.1), channel_id=1, source_target_pairs={{0,3},{1,0},{2,1},{3,2},{4,7},{5,4},{6,5},{7,6},{8,11},{9,8},{10,9... | collective-permute-start | bytes 52232 | tf_op jit(solution)/shard_map/ppermute | solution.py:185
  45.0 4.8 %collective-permute-done.9 = f32[16,272]{0,1:T(8,128)S(1)} collective-permute-done((f32[16,272]{0,1:T(8,128)S(1)}, f32[16,272]{0,1:T(8,128)S(1)}, u32[]{:S(2)}, u32[]{:S(2)}) %collective-permute-start.9) | collective-permute-done | bytes 17440 | tf_op jit(solution)/shard_map/ppermute | solution.py:185
  49.9 1.9 %collective-permute-done.8 = f32[16,272]{0,1:T(8,128)S(1)} collective-permute-done((f32[16,272]{0,1:T(8,128)S(1)}, f32[16,272]{0,1:T(8,128)S(1)}, u32[]{:S(2)}, u32[]{:S(2)}) %collective-permute-start.8) | collective-permute-done | bytes 17440 | tf_op jit(solution)/shard_map/ppermute | solution.py:185
  59.9 31.1 %shard_map.55 = bf16[128,4,8,512]{3,2,1,0:T(8,128)(2,1)} custom-call(f32[4,16,1024]{2,1,0:T(8,128)S(1)} %get-tuple-element.13.ca_ref, f32[4,16,1024]{2,1,0:T(8,128)S(1)} %get-tuple-element.14.sa_ref, f32[4,128,1024]{2,1,0:T(8,128)S(1)} %bitcast.31, f32[4,128,1024]{2,1,0:T(8,128)S(1)} %bitcast.30, f32[4,1,128]{2,1,0:T(1,128)S(1)} %broadcast_in_dim.24.inv_ref, ...), custom_call_target="tpu_custom_call" | custom-call | tf_op jit(solution)/shard_map/pallas_call | solution.py:99
  90.9 6.2 %all-to-all-start = ((bf16[128,4,8,512]{3,2,1,0:T(8,128)(2,1)}), bf16[128,4,8,512]{3,2,1,0:T(8,128)(2,1)}, u32[]{:S(2)}, u32[]{:S(2)}) async-start(bf16[128,4,8,512]{3,2,1,0:T(8,128)(2,1)} %shard_map.55), calls=%async_computation | async-start | bytes 8388608 | tf_op jit(solution)/shard_map/all_to_all | solution.py:219
  97.3 2.7 %copy.21.prof_ref = f32[8,1024,1]{2,1,0:T(8,128)} copy(f32[8,1024,1]{1,0,2:T(8,128)S(1)} %convolution_bitcast_fusion) | data formatting | bytes 65536 | tf_op jit(solution)/shard_map/broadcast_in_dim | solution.py:229
  100.1 8.0 %fusion.6.theta_ref = bf16[1024,512]{1,0:T(8,128)(2,1)S(1)} fusion(f32[512]{0:T(512)S(1)} %sine_multiply_fusion, s32[512]{0:T(512)S(1)} %multiply_add_fusion.1), kind=kLoop, calls=%fused_computation.11 | loop fusion | flops 8388608 | bytes 1052672 | tf_op jit(solution)/shard_map/convert_element_type | solution.py:163
  108.1 40.2 %all-to-all-done = bf16[128,4,8,512]{3,2,1,0:T(8,128)(2,1)} async-done(((bf16[128,4,8,512]{3,2,1,0:T(8,128)(2,1)}), bf16[128,4,8,512]{3,2,1,0:T(8,128)(2,1)}, u32[]{:S(2)}, u32[]{:S(2)}) %all-to-all-start) | async-done | bytes 4194336 | tf_op jit(solution)/shard_map/all_to_all | solution.py:219
  148.3 4.6 %copy.24 = bf16[64,8,8,512]{3,1,2,0:T(8,128)(2,1)S(1)} copy(bf16[64,8,8,512]{3,2,1,0:T(8,128)(2,1)} %bitcast.10) | data formatting | bytes 8388608
  152.9 8.0 %shard_map.56 = f32[8,1,128]{2,1,0:T(1,128)S(1)} custom-call(bf16[1024,512]{1,0:T(8,128)(2,1)S(1)} %fusion.6.theta_ref, bf16[512,4096]{1,0:T(8,128)(2,1)S(1)} %bitcast.28, f32[8,1024,1]{2,1,0:T(8,128)S(1)} %copy-done.1, f32[1,512]{1,0:T(1,128)S(1)} %bitcast.32), custom_call_target="tpu_custom_call" | custom-call | tf_op jit(solution)/shard_map/pallas_call | solution.py:233
  161.0 1.9 %collective-permute-start.12 = (f32[8]{0:T(128)S(1)}, f32[8]{0:T(128)S(1)}, u32[]{:S(2)}, u32[]{:S(2)}) collective-permute-start(f32[8]{0:T(128)S(1)} %slice_reduce_fusion), channel_id=1, source_target_pairs={{0,3},{1,0},{2,1},{3,2},{4,7},{5,4},{6,5},{7,6},{8,11},{9,8},{10,9... | collective-permute-start | bytes 104 | tf_op jit(solution)/shard_map/ppermute | solution.py:185
  164.7 3.4 %collective-permute-done.11 = f32[8]{0:T(128)S(1)} collective-permute-done((f32[8]{0:T(128)S(1)}, f32[8]{0:T(128)S(1)}, u32[]{:S(2)}, u32[]{:S(2)}) %collective-permute-start.11) | collective-permute-done | bytes 64 | tf_op jit(solution)/shard_map/ppermute | solution.py:185
  168.9 11.2 %shard_map.57 = f32[1024,8,2,256]{3,2,1,0:T(2,128)} custom-call(bf16[1024,512]{1,0:T(8,128)(2,1)S(1)} %fusion.6.theta_ref, bf16[512,4096]{1,0:T(8,128)(2,1)S(1)} %bitcast.29, f32[8,1024,1]{2,1,0:T(8,128)S(1)} %copy-done.1, f32[1,512]{1,0:T(1,128)S(1)} %bitcast.33, f32[8,1,128]{2,1,0:T(1,128)S(1)} %broadcast_in_dim.30.scale_ref), custom_call_target="tpu_custom_call" | custom-call | tf_op jit(solution)/shard_map/pallas_call | solution.py:244
  (65 shorter events, 20.4 us)
Async XLA Ops:
  0.0 97.1 %copy-start = (f32[8,1024]{1,0:T(8,128)S(1)}, f32[8,1024]{1,0:T(8,128)}, u32[]{:S(2)}) copy-start(f32[8,1024]{1,0:T(8,128)} %param.8) | copy-start | bytes 98308
  0.8 3.5 %copy-start.3 = (bf16[256,8192]{1,0:T(8,128)(2,1)S(1)}, bf16[256,8192]{1,0:T(8,128)(2,1)}, u32[]{:S(2)}) copy-start(bf16[256,8192]{1,0:T(8,128)(2,1)} %sky_ref.1) | copy-start | bytes 12582916
  4.2 1.7 copy-start.4
  5.8 7.6 %collective-permute-start = (f32[16,272]{0,1:T(8,128)S(1)}, f32[16,272]{0,1:T(8,128)S(1)}, u32[]{:S(2)}, u32[]{:S(2)}) collective-permute-start(f32[16,272]{0,1:T(8,128)S(1)} %copy.17), channel_id=1, source_target_pairs={{0,4},{4,0},{8,12},{12,8},{16,20},{20,16},{24,28},{28,24},{32,36},... | collective-permute-start | bytes 52232 | tf_op jit(solution)/shard_map/ppermute | solution.py:185
  13.5 9.5 %collective-permute-start.3 = (f32[16,272]{0,1:T(8,128)S(1)}, f32[16,272]{0,1:T(8,128)S(1)}, u32[]{:S(2)}, u32[]{:S(2)}) collective-permute-start(f32[16,272]{0,1:T(8,128)S(1)} %add.192), channel_id=1, source_target_pairs={{0,24},{4,28},{8,0},{12,4},{16,8},{20,12},{24,16},{28,20},{32,56},... | collective-permute-start | bytes 52232 | tf_op jit(solution)/shard_map/ppermute | solution.py:185
  16.4 8.1 %collective-permute-start.2 = (f32[16,272]{0,1:T(8,128)S(1)}, f32[16,272]{0,1:T(8,128)S(1)}, u32[]{:S(2)}, u32[]{:S(2)}) collective-permute-start(f32[16,272]{0,1:T(8,128)S(1)} %add.192), channel_id=1, source_target_pairs={{0,16},{4,20},{8,24},{12,28},{16,0},{20,4},{24,8},{28,12},{32,48},... | collective-permute-start | bytes 52232 | tf_op jit(solution)/shard_map/ppermute | solution.py:185
  17.2 9.5 %collective-permute-start.1 = (f32[16,272]{0,1:T(8,128)S(1)}, f32[16,272]{0,1:T(8,128)S(1)}, u32[]{:S(2)}, u32[]{:S(2)}) collective-permute-start(f32[16,272]{0,1:T(8,128)S(1)} %add.192), channel_id=1, source_target_pairs={{0,8},{4,12},{8,16},{12,20},{16,24},{20,28},{24,0},{28,4},{32,40},... | collective-permute-start | bytes 52232 | tf_op jit(solution)/shard_map/ppermute | solution.py:185
  26.7 9.2 %collective-permute-start.6 = (f32[16,272]{0,1:T(8,128)S(1)}, f32[16,272]{0,1:T(8,128)S(1)}, u32[]{:S(2)}, u32[]{:S(2)}) collective-permute-start(f32[16,272]{0,1:T(8,128)S(1)} %add_add_fusion.2), channel_id=1, source_target_pairs={{0,96},{4,100},{8,104},{12,108},{16,112},{20,116},{24,120},{28,124... | collective-permute-start | bytes 52232 | tf_op jit(solution)/shard_map/ppermute | solution.py:185
  29.8 8.1 %collective-permute-start.5 = (f32[16,272]{0,1:T(8,128)S(1)}, f32[16,272]{0,1:T(8,128)S(1)}, u32[]{:S(2)}, u32[]{:S(2)}) collective-permute-start(f32[16,272]{0,1:T(8,128)S(1)} %add_add_fusion.2), channel_id=1, source_target_pairs={{0,64},{4,68},{8,72},{12,76},{16,80},{20,84},{24,88},{28,92},{32,9... | collective-permute-start | bytes 52232 | tf_op jit(solution)/shard_map/ppermute | solution.py:185
  30.4 9.2 %collective-permute-start.4 = (f32[16,272]{0,1:T(8,128)S(1)}, f32[16,272]{0,1:T(8,128)S(1)}, u32[]{:S(2)}, u32[]{:S(2)}) collective-permute-start(f32[16,272]{0,1:T(8,128)S(1)} %add_add_fusion.2), channel_id=1, source_target_pairs={{0,32},{4,36},{8,40},{12,44},{16,48},{20,52},{24,56},{28,60},{32,6... | collective-permute-start | bytes 52232 | tf_op jit(solution)/shard_map/ppermute | solution.py:185
  39.7 10.2 %collective-permute-start.9 = (f32[16,272]{0,1:T(8,128)S(1)}, f32[16,272]{0,1:T(8,128)S(1)}, u32[]{:S(2)}, u32[]{:S(2)}) collective-permute-start(f32[16,272]{0,1:T(8,128)S(1)} %add_add_fusion.1), channel_id=1, source_target_pairs={{0,3},{1,0},{2,1},{3,2},{4,7},{5,4},{6,5},{7,6},{8,11},{9,8},{10,9... | collective-permute-start | bytes 52232 | tf_op jit(solution)/shard_map/ppermute | solution.py:185
  43.8 8.0 %collective-permute-start.8 = (f32[16,272]{0,1:T(8,128)S(1)}, f32[16,272]{0,1:T(8,128)S(1)}, u32[]{:S(2)}, u32[]{:S(2)}) collective-permute-start(f32[16,272]{0,1:T(8,128)S(1)} %add_add_fusion.1), channel_id=1, source_target_pairs={{0,2},{1,3},{2,0},{3,1},{4,6},{5,7},{6,4},{7,5},{8,10},{9,11},{10,... | collective-permute-start | bytes 52232 | tf_op jit(solution)/shard_map/ppermute | solution.py:185
  43.8 9.5 %collective-permute-start.7 = (f32[16,272]{0,1:T(8,128)S(1)}, f32[16,272]{0,1:T(8,128)S(1)}, u32[]{:S(2)}, u32[]{:S(2)}) collective-permute-start(f32[16,272]{0,1:T(8,128)S(1)} %add_add_fusion.1), channel_id=1, source_target_pairs={{0,1},{1,2},{2,3},{3,0},{4,5},{5,6},{6,7},{7,4},{8,9},{9,10},{10,1... | collective-permute-start | bytes 52232 | tf_op jit(solution)/shard_map/ppermute | solution.py:185
  58.3 1.6 copy-start.2
  90.9 6.2 %copy-start.5 = (s32[8]{0:T(128)S(1)}, s32[8]{0:T(128)}, u32[]{:S(2)}) copy-start(s32[8]{0:T(128)} %param.9) | copy-start | bytes 100
  90.9 57.4 %all-to-all-start = ((bf16[128,4,8,512]{3,2,1,0:T(8,128)(2,1)}), bf16[128,4,8,512]{3,2,1,0:T(8,128)(2,1)}, u32[]{:S(2)}, u32[]{:S(2)}) async-start(bf16[128,4,8,512]{3,2,1,0:T(8,128)(2,1)} %shard_map.55), calls=%async_computation | async-start | bytes 8388608 | tf_op jit(solution)/shard_map/all_to_all | solution.py:219
  148.3 4.6 %copy-start.1 = (f32[8,1024,1]{2,1,0:T(8,128)S(1)}, f32[8,1024,1]{2,1,0:T(8,128)}, u32[]{:S(2)}) copy-start(f32[8,1024,1]{2,1,0:T(8,128)} %copy.21.prof_ref) | copy-start | bytes 98308
  161.0 3.6 %collective-permute-start.12 = (f32[8]{0:T(128)S(1)}, f32[8]{0:T(128)S(1)}, u32[]{:S(2)}, u32[]{:S(2)}) collective-permute-start(f32[8]{0:T(128)S(1)} %slice_reduce_fusion), channel_id=1, source_target_pairs={{0,3},{1,0},{2,1},{3,2},{4,7},{5,4},{6,5},{7,6},{8,11},{9,8},{10,9... | collective-permute-start | bytes 104 | tf_op jit(solution)/shard_map/ppermute | solution.py:185
  163.0 5.1 %collective-permute-start.11 = (f32[8]{0:T(128)S(1)}, f32[8]{0:T(128)S(1)}, u32[]{:S(2)}, u32[]{:S(2)}) collective-permute-start(f32[8]{0:T(128)S(1)} %slice_reduce_fusion), channel_id=1, source_target_pairs={{0,2},{1,3},{2,0},{3,1},{4,6},{5,7},{6,4},{7,5},{8,10},{9,11},{10,... | collective-permute-start | bytes 104 | tf_op jit(solution)/shard_map/ppermute | solution.py:185
  164.0 4.8 %collective-permute-start.10 = (f32[8]{0:T(128)S(1)}, f32[8]{0:T(128)S(1)}, u32[]{:S(2)}, u32[]{:S(2)}) collective-permute-start(f32[8]{0:T(128)S(1)} %slice_reduce_fusion), channel_id=1, source_target_pairs={{0,1},{1,2},{2,3},{3,0},{4,5},{5,6},{6,7},{7,4},{8,9},{9,10},{10,1... | collective-permute-start | bytes 104 | tf_op jit(solution)/shard_map/ppermute | solution.py:185

commit v4 on v3

--- a/solution.py
+++ b/solution.py
@@ -37,13 +37,8 @@
     return ca, sa, cb, sb
 
 
-def fourier_kernel(
-    ca_ref, sa_ref, cb_ref, sb_ref, inv_ref, len_ref, sky_ref, proj_ref, basis_ref, o_ref,
-    tab_ref, clean_ref,
-):
+def table_kernel(ca_ref, sa_ref, cb_ref, sb_ref, inv_ref, len_ref, tab_ref):
     m_width = cb_ref.shape[2]
-    n_grp = o_ref.shape[0] // (sky_ref.shape[0] // o_ref.shape[1])
-    chan_dev = o_ref.shape[1]
     inv = inv_ref[0][:, 0:1]
     length = len_ref[0][:, 0:1]
 
@@ -56,11 +51,41 @@
         weight = jnp.where(rows < length, inv, 0.0)
         cos_t, sin_t = add_angles(ca, sa, cb, sb)
         r0 = pl.multiple_of(t * J_LO, J_LO)
-        tab_ref[pl.ds(r0, J_LO), 0:m_width] = (cos_t * weight).astype(jnp.bfloat16)
-        tab_ref[pl.ds(r0, J_LO), m_width : 2 * m_width] = (-sin_t * weight).astype(jnp.bfloat16)
+        tab_ref[0, pl.ds(r0, J_LO), 0:m_width] = (cos_t * weight).astype(jnp.bfloat16)
+        tab_ref[0, pl.ds(r0, J_LO), m_width : 2 * m_width] = (-sin_t * weight).astype(jnp.bfloat16)
         return carry
 
     lax.fori_loop(0, RPIX // J_LO, build, 0)
+
+
+def cycle_tables(cycle_len, m_width):
+    n_cyc = cycle_len.shape[0]
+    ca, sa, cb, sb = small_tables(cycle_len, m_width)
+    inv = jnp.broadcast_to(lax.rsqrt(cycle_len.astype(jnp.float32))[:, None, None], (n_cyc, 1, 128))
+    lens = jnp.broadcast_to(cycle_len[:, None, None], (n_cyc, 1, 128))
+    n_hi = RPIX // J_LO
+    return pl.pallas_call(
+        table_kernel,
+        grid=(n_cyc,),
+        in_specs=[
+            pl.BlockSpec((1, n_hi, m_width), lambda k: (k, 0, 0)),
+            pl.BlockSpec((1, n_hi, m_width), lambda k: (k, 0, 0)),
+            pl.BlockSpec((1, J_LO, m_width), lambda k: (k, 0, 0)),
+            pl.BlockSpec((1, J_LO, m_width), lambda k: (k, 0, 0)),
+            pl.BlockSpec((1, 1, 128), lambda k: (k, 0, 0)),
+            pl.BlockSpec((1, 1, 128), lambda k: (k, 0, 0)),
+        ],
+        out_specs=pl.BlockSpec((1, RPIX, 2 * m_width), lambda k: (k, 0, 0)),
+        out_shape=jax.ShapeDtypeStruct((n_cyc, RPIX, 2 * m_width), jnp.bfloat16),
+        compiler_params=pltpu.CompilerParams(vmem_limit_bytes=40 * 1024 * 1024),
+    )(ca, sa, cb, sb, inv, lens)
+
+
+def fourier_kernel(len_ref, sky_ref, proj_ref, basis_ref, tab_ref, o_ref, clean_ref):
+    m_width = tab_ref.shape[2] // 2
+    n_grp = o_ref.shape[0] // (sky_ref.shape[0] // o_ref.shape[1])
+    chan_dev = o_ref.shape[1]
+    length = len_ref[0][:, 0:1]
     cols = lax.broadcasted_iota(jnp.int32, (1, RPIX), 1)
     masked = jnp.where(cols < length, sky_ref[...].astype(jnp.float32), 0.0)
     correction = jnp.dot(
@@ -73,7 +98,7 @@
     n_blk = sky_ref.shape[0] // chan_dev
     for q in range(2 * m_width // step):
         res = jnp.dot(
-            clean_ref[...], tab_ref[:, q * step : (q + 1) * step], preferred_element_type=jnp.float32
+            clean_ref[...], tab_ref[0, :, q * step : (q + 1) * step], preferred_element_type=jnp.float32
         )
         part = (q * step) // m_width
         for h in range(step // m_dev):
@@ -85,39 +110,30 @@
                 )
 
 
-def cycle_fourier(sky_map, projected_t, basis, cycle_len, m_width, n_blk, n_grp):
+def cycle_fourier(sky_map, projected_t, basis, tables, cycle_len, n_blk, n_grp):
     n_cyc = cycle_len.shape[0]
     n_chan = sky_map.shape[0]
     n_mode = basis.shape[0]
     n_dev = n_blk * n_grp
     chan_dev = n_chan // n_blk
-    ca, sa, cb, sb = small_tables(cycle_len, m_width)
-    inv = jnp.broadcast_to(lax.rsqrt(cycle_len.astype(jnp.float32))[:, None, None], (n_cyc, 1, 128))
+    width = tables.shape[2]
     lens = jnp.broadcast_to(cycle_len[:, None, None], (n_cyc, 1, 128))
-    n_hi = RPIX // J_LO
-    m_dev = m_width // n_grp
+    m_dev = width // 2 // n_grp
     return pl.pallas_call(
         fourier_kernel,
         grid=(n_cyc,),
         in_specs=[
-            pl.BlockSpec((1, n_hi, m_width), lambda k: (k, 0, 0)),
-            pl.BlockSpec((1, n_hi, m_width), lambda k: (k, 0, 0)),
-            pl.BlockSpec((1, J_LO, m_width), lambda k: (k, 0, 0)),
-            pl.BlockSpec((1, J_LO, m_width), lambda k: (k, 0, 0)),
-            pl.BlockSpec((1, 1, 128), lambda k: (k, 0, 0)),
             pl.BlockSpec((1, 1, 128), lambda k: (k, 0, 0)),
             pl.BlockSpec((n_chan, RPIX), lambda k: (0, k)),
             pl.BlockSpec((n_chan, n_mode), lambda k: (0, 0)),
             pl.BlockSpec((n_mode, RPIX), lambda k: (0, k)),
+            pl.BlockSpec((1, RPIX, width), lambda k: (k, 0, 0)),
         ],
         out_specs=pl.BlockSpec((n_dev, None, chan_dev, 2 * m_dev), lambda k: (0, k, 0, 0)),
         out_shape=jax.ShapeDtypeStruct((n_dev, n_cyc, chan_dev, 2 * m_dev), jnp.bfloat16),
-        scratch_shapes=[
-            pltpu.VMEM((RPIX, 2 * m_width), jnp.bfloat16),
-            pltpu.VMEM((n_chan, RPIX), jnp.bfloat16),
-        ],
+        scratch_shapes=[pltpu.VMEM((n_chan, RPIX), jnp.bfloat16)],
         compiler_params=pltpu.CompilerParams(vmem_limit_bytes=48 * 1024 * 1024),
-    )(ca, sa, cb, sb, inv, lens, sky_map, projected_t, basis)
+    )(lens, sky_map, projected_t, basis, tables)
 
 
 def harmonic_tile(theta_ref, mv_ref, prof_ref, mw_ref, lc):
@@ -208,6 +224,7 @@
         mode_amps, masked, (((1,), (1,)), ((), ())), preferred_element_type=jnp.float32
     )
     amps_wide = mode_amps.astype(jnp.float32)
+    tables = cycle_tables(cycle_len, m_width)
     subs = sub_axes(n_blk, n_grp)
     sums = ring_sum(jnp.concatenate([gram_part, cross_part], axis=1), subs)
     gram_sum = sums[:, :n_mode]
@@ -215,7 +232,7 @@
     lower = jnp.linalg.cholesky(gram_sum)
     basis = jax.scipy.linalg.solve_triangular(lower, amps_wide, lower=True)
     projected = jax.scipy.linalg.solve_triangular(lower, cross_sum, lower=True)
-    sendbuf = cycle_fourier(sky_map, projected.T, basis, cycle_len, m_width, n_blk, n_grp)
+    sendbuf = cycle_fourier(sky_map, projected.T, basis, tables, cycle_len, n_blk, n_grp)
     moved = lax.all_to_all(sendbuf, ("blk", "grp"), 0, 0, tiled=True)
     moved = moved.reshape(n_cycle, chan_dev * 2 * M_DEV)
     theta_tab = theta_table(jnp.arange(n_cycle, dtype=jnp.int32), n_cycle)

time: 180 us -> 175 us (0.972)
  waiting for transfers between devices: 66.2 us -> 51.4 us
  starting transfers between devices: 23.9 us -> 29.6 us
  Pallas kernels: 50.3 us -> 55.1 us
    pallas_call x0 -> x1, Pallas kernels: none -> 16.2 us  [cycle_tables(): pl.pallas_call(table_kernel, grid=(n_cyc,), in_specs=[pl.BlockSpec((1, n_...]
    ppermute x13, waiting for transfers between devices: 26 us -> 11.2 us  [ring_sum(): lax.ppermute(v, axis, shift_perm(size, stride, total, k))]
    pallas_call x1, Pallas kernels: 31.1 us -> 19.8 us  [cycle_fourier(): pl.pallas_call(fourier_kernel, grid=(n_cyc,), in_specs=[pl.BlockSpec((1,...]
    ppermute x13, starting transfers between devices: 17.7 us -> 22.1 us  [ring_sum(): lax.ppermute(v, axis, shift_perm(size, stride, total, k))]
  transfers between devices with their start and end apart: 14 -> 14, of which waited for: 13 -> 7; matrix products, arithmetic and copies ran while one was open for 12% -> 12% of each run, Pallas kernels for 0% -> 9%
where the time goes in v4:
time: 175 us
  Pallas kernels  55.1 us (31%)
  waiting for transfers between devices  51.4 us (29%)
  starting transfers between devices  29.6 us (17%)
  other arithmetic  22.9 us (13%)
  local copies, waits for them, and re-layouts  10.3 us (6%)
  matrix products  5.29 us (3%)
    all_to_all x1, waiting for transfers between devices, body(): moved = lax.all_to_all(sendbuf, ('blk', 'grp'), 0, 0, tiled=True)  40.2 us
    ppermute x13, starting transfers between devices, ring_sum(): lax.ppermute(v, axis, shift_perm(size, stride, total, k))  22.1 us
    pallas_call x1, Pallas kernels, cycle_fourier(): pl.pallas_call(fourier_kernel, grid=(n_cyc,), in_specs=[pl.BlockSpec((1,...  19.8 us
    pallas_call x1, Pallas kernels, cycle_tables(): pl.pallas_call(table_kernel, grid=(n_cyc,), in_specs=[pl.BlockSpec((1, n_...  16.2 us
    ppermute x13, waiting for transfers between devices, ring_sum(): lax.ppermute(v, axis, shift_perm(size, stride, total, k))  11.2 us
    pallas_call x1, Pallas kernels, body(): pl.pallas_call(output_kernel, grid=(chan_dev,), in_specs=specs + [pl.Bloc...  11.2 us
    cos x2, other arithmetic, cos_sin_of_phase(): return (jnp.cos(angle), jnp.sin(angle))  8.81 us
    convert_element_type x1, other arithmetic, theta_table(): return (jnp.cos(angle) * weight[None, :]).astype(jnp.bfloat16)  7.96 us
  transfers between devices with their start and end apart: 14, of which 7 were waited for; matrix products, arithmetic and copies ran while one was open for 12% of the time, Pallas kernels for 9%

profile of v4, /device:TPU:0, one launch (start us, length us, event | category | flops | bytes accessed | tf_op | source)
XLA Modules:
  0.0 174.9 jit_solution(13317628323045659797)
XLA Ops:
  0.8 3.0 %convolution_convert_fusion = bf16[8192,16]{0,1:T(8,128)(2,1)S(1)} fusion(bf16[256,16]{0,1:T(8,128)(2,1)} %param.6, bf16[256,8192]{1,0:T(8,128)(2,1)} %sky_ref.1, pred[8192]{0:T(1024)(128)(4,1)S(1)} %bitcast.34), kind=kOutput, calls=%fused_computation | convolution fusion | flops 69337088 | bytes 4472832 | tf_op jit(solution)/shard_map/dot_general | solution.py:219
  6.3 7.0 %fusion.34 = (f32[4,16,1024]{2,1,0:T(8,128)S(1)}, f32[4,16,1024]{2,1,0:T(8,128)S(1)}, f32[4,16,1024]{2,1,0:T(8,128)S(1)}, f32[4,16,1024]{2,1,0:T(8,128)S(1)}) fusion(f32[4]{0:T(128)S(1)} %get-tuple-element.16, pred[4]{0:T(512)(128)(4,1)S(1)} %broadcast_compare_fusion, s32[4]{0:T(128)S(1)} %get-tuple-element.15, s32[16,1024]{1,0:T(8,128)S(1)} %iota_multiply_fusion, ...), kind=kLoop, calls=%fused_computation.53 | loop fusion | flops 1376256 | bytes 1114404 | tf_op jit(solution)/shard_map/cos | solution.py:16
  13.5 1.7 collective-permute-start.1
  15.2 2.7 %collective-permute-start.2 = (f32[16,272]{0,1:T(8,128)S(1)}, f32[16,272]{0,1:T(8,128)S(1)}, u32[]{:S(2)}, u32[]{:S(2)}) collective-permute-start(f32[16,272]{0,1:T(8,128)S(1)} %add.184), channel_id=1, source_target_pairs={{0,16},{4,20},{8,24},{12,28},{16,0},{20,4},{24,8},{28,12},{32,48},... | collective-permute-start | bytes 52232 | tf_op jit(solution)/shard_map/ppermute | solution.py:201
  17.9 1.4 collective-permute-start.3
  19.3 1.8 %fusion.38 = (f32[4,8,1024]{2,1,0:T(8,128)S(1)}, f32[4,8,1024]{2,1,0:T(8,128)S(1)}) fusion(f32[4]{0:T(128)S(1)} %get-tuple-element.16, pred[4]{0:T(512)(128)(4,1)S(1)} %broadcast_compare_fusion, s32[4]{0:T(128)S(1)} %get-tuple-element.15, s32[4,8]{1,0:T(4,128)S(1)} %remainder_select_fusion.1), kind=kLoop, calls=%fused_computation.58 | loop fusion | flops 360448 | bytes 262308 | tf_op jit(solution)/shard_map/cos | solution.py:16
  21.2 3.7 %collective-permute-done.2 = f32[16,272]{0,1:T(8,128)S(1)} collective-permute-done((f32[16,272]{0,1:T(8,128)S(1)}, f32[16,272]{0,1:T(8,128)S(1)}, u32[]{:S(2)}, u32[]{:S(2)}) %collective-permute-start.2) | collective-permute-done | bytes 17440 | tf_op jit(solution)/shard_map/ppermute | solution.py:201
  24.9 1.6 collective-permute-start.4
  26.6 2.9 %collective-permute-start.5 = (f32[16,272]{0,1:T(8,128)S(1)}, f32[16,272]{0,1:T(8,128)S(1)}, u32[]{:S(2)}, u32[]{:S(2)}) collective-permute-start(f32[16,272]{0,1:T(8,128)S(1)} %add_add_fusion.2), channel_id=1, source_target_pairs={{0,64},{4,68},{8,72},{12,76},{16,80},{20,84},{24,88},{28,92},{32,9... | collective-permute-start | bytes 52232 | tf_op jit(solution)/shard_map/ppermute | solution.py:201
  31.6 4.0 %collective-permute-done.5 = f32[16,272]{0,1:T(8,128)S(1)} collective-permute-done((f32[16,272]{0,1:T(8,128)S(1)}, f32[16,272]{0,1:T(8,128)S(1)}, u32[]{:S(2)}, u32[]{:S(2)}) %collective-permute-start.5) | collective-permute-done | bytes 17440 | tf_op jit(solution)/shard_map/ppermute | solution.py:201
  35.7 2.0 %collective-permute-start.7 = (f32[16,272]{0,1:T(8,128)S(1)}, f32[16,272]{0,1:T(8,128)S(1)}, u32[]{:S(2)}, u32[]{:S(2)}) collective-permute-start(f32[16,272]{0,1:T(8,128)S(1)} %add_add_fusion.1), channel_id=1, source_target_pairs={{0,1},{1,2},{2,3},{3,0},{4,5},{5,6},{6,7},{7,4},{8,9},{9,10},{10,1... | collective-permute-start | bytes 52232 | tf_op jit(solution)/shard_map/ppermute | solution.py:201
  37.7 3.6 %collective-permute-start.8 = (f32[16,272]{0,1:T(8,128)S(1)}, f32[16,272]{0,1:T(8,128)S(1)}, u32[]{:S(2)}, u32[]{:S(2)}) collective-permute-start(f32[16,272]{0,1:T(8,128)S(1)} %add_add_fusion.1), channel_id=1, source_target_pairs={{0,2},{1,3},{2,0},{3,1},{4,6},{5,7},{6,4},{7,5},{8,10},{9,11},{10,... | collective-permute-start | bytes 52232 | tf_op jit(solution)/shard_map/ppermute | solution.py:201
  42.4 16.2 %shard_map.55.tab_ref = bf16[4,2048,2048]{2,1,0:T(8,128)(2,1)} custom-call(f32[4,16,1024]{2,1,0:T(8,128)S(1)} %get-tuple-element.13.ca_ref, f32[4,16,1024]{2,1,0:T(8,128)S(1)} %get-tuple-element.14.sa_ref, f32[4,128,1024]{2,1,0:T(8,128)S(1)} %bitcast.31, f32[4,128,1024]{2,1,0:T(8,128)S(1)} %bitcast.30, f32[4,1,128]{2,1,0:T(1,128)S(1)} %broadcast_in_dim.26.inv_ref, ...), custom_call_target="tpu_custom_call" | custom-call | tf_op jit(solution)/shard_map/pallas_call | solution.py:67
  58.8 1.5 cholesky.16
  63.5 19.8 %shard_map.56 = bf16[128,4,8,512]{3,2,1,0:T(8,128)(2,1)S(1)} custom-call(s32[4,1,128]{2,1,0:T(1,128)S(1)} %broadcast_in_dim.23.len_ref, bf16[256,8192]{1,0:T(8,128)(2,1)} %sky_ref.1, f32[256,16]{1,0:T(8,128)S(1)} %fusion.27.proj_ref, f32[16,8192]{1,0:T(8,128)S(1)} %fusion.41.basis_ref, bf16[4,2048,2048]{2,1,0:T(8,128)(2,1)} %shard_map.55.tab_ref), custom_call_target="tpu_custom_call" | custom-call | tf_op jit(solution)/shard_map/pallas_call | solution.py:122
  83.3 2.0 %copy-done.2 = bf16[128,4,8,512]{3,2,1,0:T(8,128)(2,1)} copy-done((bf16[128,4,8,512]{3,2,1,0:T(8,128)(2,1)}, bf16[128,4,8,512]{3,2,1,0:T(8,128)(2,1)S(1)}, u32[]{:S(2)}) %copy-start.2) | copy-done | bytes 4194328
  85.3 7.5 %all-to-all-start = ((bf16[128,4,8,512]{3,2,1,0:T(8,128)(2,1)}), bf16[128,4,8,512]{3,2,1,0:T(8,128)(2,1)}, u32[]{:S(2)}, u32[]{:S(2)}) async-start(bf16[128,4,8,512]{3,2,1,0:T(8,128)(2,1)} %copy-done.2), calls=%async_computation | async-start | bytes 8388608 | tf_op jit(solution)/shard_map/all_to_all | solution.py:236
  93.1 2.7 %copy.21.prof_ref = f32[8,1024,1]{2,1,0:T(8,128)} copy(f32[8,1024,1]{1,0,2:T(8,128)S(1)} %convolution_bitcast_fusion) | data formatting | bytes 65536 | tf_op jit(solution)/shard_map/broadcast_in_dim | solution.py:246
  95.9 8.0 %fusion.6.theta_ref = bf16[1024,512]{1,0:T(8,128)(2,1)S(1)} fusion(f32[512]{0:T(512)S(1)} %sine_multiply_fusion, s32[512]{0:T(512)S(1)} %multiply_add_fusion.1), kind=kLoop, calls=%fused_computation.11 | loop fusion | flops 8388608 | bytes 1052672 | tf_op jit(solution)/shard_map/convert_element_type | solution.py:179
  103.8 40.2 %all-to-all-done = bf16[128,4,8,512]{3,2,1,0:T(8,128)(2,1)} async-done(((bf16[128,4,8,512]{3,2,1,0:T(8,128)(2,1)}), bf16[128,4,8,512]{3,2,1,0:T(8,128)(2,1)}, u32[]{:S(2)}, u32[]{:S(2)}) %all-to-all-start) | async-done | bytes 4194336 | tf_op jit(solution)/shard_map/all_to_all | solution.py:236
  144.1 4.6 %copy.24 = bf16[64,8,8,512]{3,1,2,0:T(8,128)(2,1)S(1)} copy(bf16[64,8,8,512]{3,2,1,0:T(8,128)(2,1)} %bitcast.10) | data formatting | bytes 8388608
  148.7 7.8 %shard_map.57 = f32[8,1,128]{2,1,0:T(1,128)S(1)} custom-call(bf16[1024,512]{1,0:T(8,128)(2,1)S(1)} %fusion.6.theta_ref, bf16[512,4096]{1,0:T(8,128)(2,1)S(1)} %bitcast.28, f32[8,1024,1]{2,1,0:T(8,128)S(1)} %copy-done.1, f32[1,512]{1,0:T(1,128)S(1)} %bitcast.32), custom_call_target="tpu_custom_call" | custom-call | tf_op jit(solution)/shard_map/pallas_call | solution.py:250
  157.6 2.5 %collective-permute-start.11 = (f32[8]{0:T(128)S(1)}, f32[8]{0:T(128)S(1)}, u32[]{:S(2)}, u32[]{:S(2)}) collective-permute-start(f32[8]{0:T(128)S(1)} %slice_reduce_fusion), channel_id=1, source_target_pairs={{0,2},{1,3},{2,0},{3,1},{4,6},{5,7},{6,4},{7,5},{8,10},{9,11},{10,... | collective-permute-start | bytes 104 | tf_op jit(solution)/shard_map/ppermute | solution.py:201
  163.7 11.2 %shard_map.58 = f32[1024,8,2,256]{3,2,1,0:T(2,128)} custom-call(bf16[1024,512]{1,0:T(8,128)(2,1)S(1)} %fusion.6.theta_ref, bf16[512,4096]{1,0:T(8,128)(2,1)S(1)} %bitcast.29, f32[8,1024,1]{2,1,0:T(8,128)S(1)} %copy-done.1, f32[1,512]{1,0:T(1,128)S(1)} %bitcast.33, f32[8,1,128]{2,1,0:T(1,128)S(1)} %broadcast_in_dim.30.scale_ref), custom_call_target="tpu_custom_call" | custom-call | tf_op jit(solution)/shard_map/pallas_call | solution.py:261
  (66 shorter events, 15.1 us)
Async XLA Ops:
  0.0 92.9 %copy-start = (f32[8,1024]{1,0:T(8,128)S(1)}, f32[8,1024]{1,0:T(8,128)}, u32[]{:S(2)}) copy-start(f32[8,1024]{1,0:T(8,128)} %param.8) | copy-start | bytes 98308
  0.8 3.5 %copy-start.3 = (bf16[256,8192]{1,0:T(8,128)(2,1)S(1)}, bf16[256,8192]{1,0:T(8,128)(2,1)}, u32[]{:S(2)}) copy-start(bf16[256,8192]{1,0:T(8,128)(2,1)} %sky_ref.1) | copy-start | bytes 12582916
  4.2 1.7 copy-start.4
  5.8 7.6 %collective-permute-start = (f32[16,272]{0,1:T(8,128)S(1)}, f32[16,272]{0,1:T(8,128)S(1)}, u32[]{:S(2)}, u32[]{:S(2)}) collective-permute-start(f32[16,272]{0,1:T(8,128)S(1)} %copy.17), channel_id=1, source_target_pairs={{0,4},{4,0},{8,12},{12,8},{16,20},{20,16},{24,28},{28,24},{32,36},... | collective-permute-start | bytes 52232 | tf_op jit(solution)/shard_map/ppermute | solution.py:201
  13.5 7.7 %collective-permute-start.1 = (f32[16,272]{0,1:T(8,128)S(1)}, f32[16,272]{0,1:T(8,128)S(1)}, u32[]{:S(2)}, u32[]{:S(2)}) collective-permute-start(f32[16,272]{0,1:T(8,128)S(1)} %add.184), channel_id=1, source_target_pairs={{0,8},{4,12},{8,16},{12,20},{16,24},{20,28},{24,0},{28,4},{32,40},... | collective-permute-start | bytes 52232 | tf_op jit(solution)/shard_map/ppermute | solution.py:201
  15.2 9.7 %collective-permute-start.2 = (f32[16,272]{0,1:T(8,128)S(1)}, f32[16,272]{0,1:T(8,128)S(1)}, u32[]{:S(2)}, u32[]{:S(2)}) collective-permute-start(f32[16,272]{0,1:T(8,128)S(1)} %add.184), channel_id=1, source_target_pairs={{0,16},{4,20},{8,24},{12,28},{16,0},{20,4},{24,8},{28,12},{32,48},... | collective-permute-start | bytes 52232 | tf_op jit(solution)/shard_map/ppermute | solution.py:201
  17.9 7.0 %collective-permute-start.3 = (f32[16,272]{0,1:T(8,128)S(1)}, f32[16,272]{0,1:T(8,128)S(1)}, u32[]{:S(2)}, u32[]{:S(2)}) collective-permute-start(f32[16,272]{0,1:T(8,128)S(1)} %add.184), channel_id=1, source_target_pairs={{0,24},{4,28},{8,0},{12,4},{16,8},{20,12},{24,16},{28,20},{32,56},... | collective-permute-start | bytes 52232 | tf_op jit(solution)/shard_map/ppermute | solution.py:201
  24.9 6.7 %collective-permute-start.4 = (f32[16,272]{0,1:T(8,128)S(1)}, f32[16,272]{0,1:T(8,128)S(1)}, u32[]{:S(2)}, u32[]{:S(2)}) collective-permute-start(f32[16,272]{0,1:T(8,128)S(1)} %add_add_fusion.2), channel_id=1, source_target_pairs={{0,32},{4,36},{8,40},{12,44},{16,48},{20,52},{24,56},{28,60},{32,6... | collective-permute-start | bytes 52232 | tf_op jit(solution)/shard_map/ppermute | solution.py:201
  26.6 9.1 %collective-permute-start.5 = (f32[16,272]{0,1:T(8,128)S(1)}, f32[16,272]{0,1:T(8,128)S(1)}, u32[]{:S(2)}, u32[]{:S(2)}) collective-permute-start(f32[16,272]{0,1:T(8,128)S(1)} %add_add_fusion.2), channel_id=1, source_target_pairs={{0,64},{4,68},{8,72},{12,76},{16,80},{20,84},{24,88},{28,92},{32,9... | collective-permute-start | bytes 52232 | tf_op jit(solution)/shard_map/ppermute | solution.py:201
  29.5 6.2 %collective-permute-start.6 = (f32[16,272]{0,1:T(8,128)S(1)}, f32[16,272]{0,1:T(8,128)S(1)}, u32[]{:S(2)}, u32[]{:S(2)}) collective-permute-start(f32[16,272]{0,1:T(8,128)S(1)} %add_add_fusion.2), channel_id=1, source_target_pairs={{0,96},{4,100},{8,104},{12,108},{16,112},{20,116},{24,120},{28,124... | collective-permute-start | bytes 52232 | tf_op jit(solution)/shard_map/ppermute | solution.py:201
  35.7 23.0 %collective-permute-start.7 = (f32[16,272]{0,1:T(8,128)S(1)}, f32[16,272]{0,1:T(8,128)S(1)}, u32[]{:S(2)}, u32[]{:S(2)}) collective-permute-start(f32[16,272]{0,1:T(8,128)S(1)} %add_add_fusion.1), channel_id=1, source_target_pairs={{0,1},{1,2},{2,3},{3,0},{4,5},{5,6},{6,7},{7,4},{8,9},{9,10},{10,1... | collective-permute-start | bytes 52232 | tf_op jit(solution)/shard_map/ppermute | solution.py:201
  37.7 21.0 %collective-permute-start.8 = (f32[16,272]{0,1:T(8,128)S(1)}, f32[16,272]{0,1:T(8,128)S(1)}, u32[]{:S(2)}, u32[]{:S(2)}) collective-permute-start(f32[16,272]{0,1:T(8,128)S(1)} %add_add_fusion.1), channel_id=1, source_target_pairs={{0,2},{1,3},{2,0},{3,1},{4,6},{5,7},{6,4},{7,5},{8,10},{9,11},{10,... | collective-permute-start | bytes 52232 | tf_op jit(solution)/shard_map/ppermute | solution.py:201
  41.2 17.4 %collective-permute-start.9 = (f32[16,272]{0,1:T(8,128)S(1)}, f32[16,272]{0,1:T(8,128)S(1)}, u32[]{:S(2)}, u32[]{:S(2)}) collective-permute-start(f32[16,272]{0,1:T(8,128)S(1)} %add_add_fusion.1), channel_id=1, source_target_pairs={{0,3},{1,0},{2,1},{3,2},{4,7},{5,4},{6,5},{7,6},{8,11},{9,8},{10,9... | collective-permute-start | bytes 52232 | tf_op jit(solution)/shard_map/ppermute | solution.py:201
  83.3 2.0 %copy-start.2 = (bf16[128,4,8,512]{3,2,1,0:T(8,128)(2,1)}, bf16[128,4,8,512]{3,2,1,0:T(8,128)(2,1)S(1)}, u32[]{:S(2)}) copy-start(bf16[128,4,8,512]{3,2,1,0:T(8,128)(2,1)S(1)} %shard_map.56) | copy-start | bytes 12582916
  85.3 7.6 %copy-start.5 = (s32[8]{0:T(128)S(1)}, s32[8]{0:T(128)}, u32[]{:S(2)}) copy-start(s32[8]{0:T(128)} %param.9) | copy-start | bytes 100
  85.3 58.7 %all-to-all-start = ((bf16[128,4,8,512]{3,2,1,0:T(8,128)(2,1)}), bf16[128,4,8,512]{3,2,1,0:T(8,128)(2,1)}, u32[]{:S(2)}, u32[]{:S(2)}) async-start(bf16[128,4,8,512]{3,2,1,0:T(8,128)(2,1)} %copy-done.2), calls=%async_computation | async-start | bytes 8388608 | tf_op jit(solution)/shard_map/all_to_all | solution.py:236
  144.1 4.6 %copy-start.1 = (f32[8,1024,1]{2,1,0:T(8,128)S(1)}, f32[8,1024,1]{2,1,0:T(8,128)}, u32[]{:S(2)}) copy-start(f32[8,1024,1]{2,1,0:T(8,128)} %copy.21.prof_ref) | copy-start | bytes 98308
  156.7 4.8 %collective-permute-start.10 = (f32[8]{0:T(128)S(1)}, f32[8]{0:T(128)S(1)}, u32[]{:S(2)}, u32[]{:S(2)}) collective-permute-start(f32[8]{0:T(128)S(1)} %slice_reduce_fusion), channel_id=1, source_target_pairs={{0,1},{1,2},{2,3},{3,0},{4,5},{5,6},{6,7},{7,4},{8,9},{9,10},{10,1... | collective-permute-start | bytes 104 | tf_op jit(solution)/shard_map/ppermute | solution.py:201
  157.6 5.1 %collective-permute-start.11 = (f32[8]{0:T(128)S(1)}, f32[8]{0:T(128)S(1)}, u32[]{:S(2)}, u32[]{:S(2)}) collective-permute-start(f32[8]{0:T(128)S(1)} %slice_reduce_fusion), channel_id=1, source_target_pairs={{0,2},{1,3},{2,0},{3,1},{4,6},{5,7},{6,4},{7,5},{8,10},{9,11},{10,... | collective-permute-start | bytes 104 | tf_op jit(solution)/shard_map/ppermute | solution.py:201
  160.1 3.6 %collective-permute-start.12 = (f32[8]{0:T(128)S(1)}, f32[8]{0:T(128)S(1)}, u32[]{:S(2)}, u32[]{:S(2)}) collective-permute-start(f32[8]{0:T(128)S(1)} %slice_reduce_fusion), channel_id=1, source_target_pairs={{0,3},{1,0},{2,1},{3,2},{4,7},{5,4},{6,5},{7,6},{8,11},{9,8},{10,9... | collective-permute-start | bytes 104 | tf_op jit(solution)/shard_map/ppermute | solution.py:201

commit v5 on v4

--- a/solution.py
+++ b/solution.py
@@ -37,16 +37,45 @@
     return ca, sa, cb, sb
 
 
-def table_kernel(ca_ref, sa_ref, cb_ref, sb_ref, inv_ref, len_ref, tab_ref):
-    m_width = cb_ref.shape[2]
+def small_phases(cycle_len, m_width):
+    period = 2 * cycle_len[:, None, None]
+    orders = jnp.arange(m_width, dtype=jnp.int32)[None, None, :]
+    j_hi = jnp.arange(RPIX // J_LO, dtype=jnp.int32)[None, :, None]
+    j_mid = jnp.arange(J_LO // 16, dtype=jnp.int32)[None, :, None]
+    j_q = jnp.arange(16, dtype=jnp.int32)[None, :, None]
+    p_hi = (2 * J_LO * j_hi) % period * orders % period
+    p_mid = (32 * j_mid) % period * orders % period
+    p_q = orders * (2 * j_q + 1) % period
+    return jnp.concatenate([p_hi, p_q, p_mid], axis=1)
+
+
+def table_kernel(phase_ref, inv_ref, len_ref, tab_ref, hi_c, hi_s, lo_c, lo_s):
+    m_width = phase_ref.shape[2]
+    n_hi = RPIX // J_LO
+    n_mid = J_LO // 16
     inv = inv_ref[0][:, 0:1]
     length = len_ref[0][:, 0:1]
+    size = length.astype(jnp.float32)
+
+    def cos_sin(rows):
+        angle = jnp.pi * phase_ref[0, rows, :].astype(jnp.float32) / size
+        return jnp.cos(angle), jnp.sin(angle)
+
+    c, s_ = cos_sin(pl.ds(0, n_hi))
+    hi_c[...] = c
+    hi_s[...] = s_
+    cq, sq = cos_sin(pl.ds(n_hi, 16))
+    cm, sm = cos_sin(pl.ds(n_hi + 16, n_mid))
+    for jm in range(n_mid):
+        c_lo, s_lo = add_angles(cm[jm : jm + 1], sm[jm : jm + 1], cq, sq)
+        lo_c[jm * 16 : (jm + 1) * 16, :] = c_lo
+        lo_s[jm * 16 : (jm + 1) * 16, :] = s_lo
 
     def build(t, carry):
-        ca = ca_ref[0, pl.ds(t, 1), :]
-        sa = sa_ref[0, pl.ds(t, 1), :]
-        cb = cb_ref[0]
-        sb = sb_ref[0]
+        ca = hi_c[pl.ds(t, 1), :]
+        sa = hi_s[pl.ds(t, 1), :]
+        cb = lo_c[...]
+        sb = lo_s[...]
         rows = t * J_LO + lax.broadcasted_iota(jnp.int32, (J_LO, 1), 0)
         weight = jnp.where(rows < length, inv, 0.0)
         cos_t, sin_t = add_angles(ca, sa, cb, sb)
@@ -55,30 +84,34 @@
         tab_ref[0, pl.ds(r0, J_LO), m_width : 2 * m_width] = (-sin_t * weight).astype(jnp.bfloat16)
         return carry
 
-    lax.fori_loop(0, RPIX // J_LO, build, 0)
+    lax.fori_loop(0, n_hi, build, 0)
 
 
 def cycle_tables(cycle_len, m_width):
     n_cyc = cycle_len.shape[0]
-    ca, sa, cb, sb = small_tables(cycle_len, m_width)
+    phases = small_phases(cycle_len, m_width)
     inv = jnp.broadcast_to(lax.rsqrt(cycle_len.astype(jnp.float32))[:, None, None], (n_cyc, 1, 128))
     lens = jnp.broadcast_to(cycle_len[:, None, None], (n_cyc, 1, 128))
     n_hi = RPIX // J_LO
+    n_rows = phases.shape[1]
     return pl.pallas_call(
         table_kernel,
         grid=(n_cyc,),
         in_specs=[
-            pl.BlockSpec((1, n_hi, m_width), lambda k: (k, 0, 0)),
-            pl.BlockSpec((1, n_hi, m_width), lambda k: (k, 0, 0)),
-            pl.BlockSpec((1, J_LO, m_width), lambda k: (k, 0, 0)),
-            pl.BlockSpec((1, J_LO, m_width), lambda k: (k, 0, 0)),
+            pl.BlockSpec((1, n_rows, m_width), lambda k: (k, 0, 0)),
             pl.BlockSpec((1, 1, 128), lambda k: (k, 0, 0)),
             pl.BlockSpec((1, 1, 128), lambda k: (k, 0, 0)),
         ],
         out_specs=pl.BlockSpec((1, RPIX, 2 * m_width), lambda k: (k, 0, 0)),
         out_shape=jax.ShapeDtypeStruct((n_cyc, RPIX, 2 * m_width), jnp.bfloat16),
+        scratch_shapes=[
+            pltpu.VMEM((n_hi, m_width), jnp.float32),
+            pltpu.VMEM((n_hi, m_width), jnp.float32),
+            pltpu.VMEM((J_LO, m_width), jnp.float32),
+            pltpu.VMEM((J_LO, m_width), jnp.float32),
+        ],
         compiler_params=pltpu.CompilerParams(vmem_limit_bytes=40 * 1024 * 1024),
-    )(ca, sa, cb, sb, inv, lens)
+    )(phases, inv, lens)
 
 
 def fourier_kernel(len_ref, sky_ref, proj_ref, basis_ref, tab_ref, o_ref, clean_ref):

time: 175 us -> 176 us (level)
  Pallas kernels: 55.1 us -> 58.2 us
  other arithmetic: 22.9 us -> 20 us
    cos x2 -> x0, other arithmetic: 8.81 us -> none  [cos_sin_of_phase(): return (jnp.cos(angle), jnp.sin(angle))]
    select_n x3 -> x5, other arithmetic: 0.39 us -> 6.83 us  [the longest x3 5.27 us: small_phases(): p_hi = 2 * J_LO * j_hi % period * orders % period]
    pallas_call x1, Pallas kernels: 16.2 us -> 19.3 us  [cycle_tables(): pl.pallas_call(table_kernel, grid=(n_cyc,), in_specs=[pl.BlockSpec((1, n_...]
  transfers between devices with their start and end apart: 14 -> 14, of which waited for: 7 -> 8; matrix products, arithmetic and copies ran while one was open for 12% -> 10% of each run, Pallas kernels for 9% -> 11%
where the time goes in v5:
time: 176 us
  Pallas kernels  58.2 us (33%)
  waiting for transfers between devices  52.8 us (30%)
  starting transfers between devices  29.4 us (17%)
  other arithmetic  20 us (11%)
  local copies, waits for them, and re-layouts  10.3 us (6%)
  matrix products  5.3 us (3%)
    all_to_all x1, waiting for transfers between devices, body(): moved = lax.all_to_all(sendbuf, ('blk', 'grp'), 0, 0, tiled=True)  40.4 us
    ppermute x13, starting transfers between devices, ring_sum(): lax.ppermute(v, axis, shift_perm(size, stride, total, k))  22.1 us
    pallas_call x1, Pallas kernels, cycle_fourier(): pl.pallas_call(fourier_kernel, grid=(n_cyc,), in_specs=[pl.BlockSpec((1,...  19.8 us
    pallas_call x1, Pallas kernels, cycle_tables(): pl.pallas_call(table_kernel, grid=(n_cyc,), in_specs=[pl.BlockSpec((1, n_...  19.3 us
    ppermute x13, waiting for transfers between devices, ring_sum(): lax.ppermute(v, axis, shift_perm(size, stride, total, k))  12.3 us
    pallas_call x1, Pallas kernels, body(): pl.pallas_call(output_kernel, grid=(chan_dev,), in_specs=specs + [pl.Bloc...  11.2 us
    convert_element_type x1, other arithmetic, theta_table(): return (jnp.cos(angle) * weight[None, :]).astype(jnp.bfloat16)  7.96 us
    pallas_call x1, Pallas kernels, body(): pl.pallas_call(power_kernel, grid=(chan_dev,), in_specs=specs, out_specs=...  7.84 us
  transfers between devices with their start and end apart: 14, of which 8 were waited for; matrix products, arithmetic and copies ran while one was open for 10% of the time, Pallas kernels for 11%

profile of v5, /device:TPU:0, one launch (start us, length us, event | category | flops | bytes accessed | tf_op | source)
XLA Modules:
  0.0 176.2 jit_solution(12611113971796039688)
XLA Ops:
  0.8 3.0 %convolution_convert_fusion = bf16[8192,16]{0,1:T(8,128)(2,1)S(1)} fusion(bf16[256,16]{0,1:T(8,128)(2,1)} %param.6, bf16[256,8192]{1,0:T(8,128)(2,1)} %sky_ref.1, pred[8192]{0:T(1024)(128)(4,1)S(1)} %bitcast.30), kind=kOutput, calls=%fused_computation | convolution fusion | flops 69337088 | bytes 4472832 | tf_op jit(solution)/shard_map/dot_general | solution.py:252
  6.3 5.1 %add_select_fusion.1 = (s32[4,16,1024]{2,1,0:T(8,128)S(1)}, s32[4,16,1024]{2,1,0:T(8,128)S(1)}) fusion(s32[4]{0:T(128)S(1)} %compare_select_fusion, s32[4,16]{1,0:T(4,128)S(1)} %remainder_select_fusion.2, pred[4]{0:T(512)(128)(4,1)S(1)} %broadcast_compare_fusion, s32[16,1024]{1,0:T(8,128)S(1)} %iota_multiply_fusion), kind=kLoop, calls=%fused_computation.23 | loop fusion | flops 983040 | bytes 590100 | tf_op jit(solution)/shard_map/jit(remainder)/select_n | solution.py:46
  11.6 1.7 collective-permute-start.1
  13.3 2.7 %collective-permute-start.2 = (f32[16,272]{0,1:T(8,128)S(1)}, f32[16,272]{0,1:T(8,128)S(1)}, u32[]{:S(2)}, u32[]{:S(2)}) collective-permute-start(f32[16,272]{0,1:T(8,128)S(1)} %add.163), channel_id=1, source_target_pairs={{0,16},{4,20},{8,24},{12,28},{16,0},{20,4},{24,8},{28,12},{32,48},... | collective-permute-start | bytes 52232 | tf_op jit(solution)/shard_map/ppermute | solution.py:234
  16.0 1.4 collective-permute-start.3
  17.4 1.4 add_select_fusion.2
  18.9 4.1 %collective-permute-done.2 = f32[16,272]{0,1:T(8,128)S(1)} collective-permute-done((f32[16,272]{0,1:T(8,128)S(1)}, f32[16,272]{0,1:T(8,128)S(1)}, u32[]{:S(2)}, u32[]{:S(2)}) %collective-permute-start.2) | collective-permute-done | bytes 17440 | tf_op jit(solution)/shard_map/ppermute | solution.py:234
  23.0 1.6 collective-permute-start.4
  24.7 2.9 %collective-permute-start.5 = (f32[16,272]{0,1:T(8,128)S(1)}, f32[16,272]{0,1:T(8,128)S(1)}, u32[]{:S(2)}, u32[]{:S(2)}) collective-permute-start(f32[16,272]{0,1:T(8,128)S(1)} %add_add_fusion.2), channel_id=1, source_target_pairs={{0,64},{4,68},{8,72},{12,76},{16,80},{20,84},{24,88},{28,92},{32,9... | collective-permute-start | bytes 52232 | tf_op jit(solution)/shard_map/ppermute | solution.py:234
  29.8 4.0 %collective-permute-done.5 = f32[16,272]{0,1:T(8,128)S(1)} collective-permute-done((f32[16,272]{0,1:T(8,128)S(1)}, f32[16,272]{0,1:T(8,128)S(1)}, u32[]{:S(2)}, u32[]{:S(2)}) %collective-permute-start.5) | collective-permute-done | bytes 17440 | tf_op jit(solution)/shard_map/ppermute | solution.py:234
  33.8 2.0 %collective-permute-start.7 = (f32[16,272]{0,1:T(8,128)S(1)}, f32[16,272]{0,1:T(8,128)S(1)}, u32[]{:S(2)}, u32[]{:S(2)}) collective-permute-start(f32[16,272]{0,1:T(8,128)S(1)} %add_add_fusion.1), channel_id=1, source_target_pairs={{0,1},{1,2},{2,3},{3,0},{4,5},{5,6},{6,7},{7,4},{8,9},{9,10},{10,1... | collective-permute-start | bytes 52232 | tf_op jit(solution)/shard_map/ppermute | solution.py:234
  35.8 3.6 %collective-permute-start.8 = (f32[16,272]{0,1:T(8,128)S(1)}, f32[16,272]{0,1:T(8,128)S(1)}, u32[]{:S(2)}, u32[]{:S(2)}) collective-permute-start(f32[16,272]{0,1:T(8,128)S(1)} %add_add_fusion.1), channel_id=1, source_target_pairs={{0,2},{1,3},{2,0},{3,1},{4,6},{5,7},{6,4},{7,5},{8,10},{9,11},{10,... | collective-permute-start | bytes 52232 | tf_op jit(solution)/shard_map/ppermute | solution.py:234
  40.6 19.3 %shard_map.55.tab_ref = bf16[4,2048,2048]{2,1,0:T(8,128)(2,1)} custom-call(s32[4,40,1024]{2,1,0:T(8,128)S(1)} %pad_add_fusion.phase_ref, f32[4,1,128]{2,1,0:T(1,128)S(1)} %broadcast_in_dim.27.inv_ref, s32[4,1,128]{2,1,0:T(1,128)S(1)} %broadcast_in_dim.23.len_ref), custom_call_target="tpu_custom_call" | custom-call | tf_op jit(solution)/shard_map/pallas_call | solution.py:97
  60.1 1.5 cholesky.16
  64.8 19.8 %shard_map.56 = bf16[128,4,8,512]{3,2,1,0:T(8,128)(2,1)S(1)} custom-call(s32[4,1,128]{2,1,0:T(1,128)S(1)} %broadcast_in_dim.23.len_ref, bf16[256,8192]{1,0:T(8,128)(2,1)} %sky_ref.1, f32[256,16]{1,0:T(8,128)S(1)} %fusion.18.proj_ref, f32[16,8192]{1,0:T(8,128)S(1)} %fusion.26.basis_ref, bf16[4,2048,2048]{2,1,0:T(8,128)(2,1)} %shard_map.55.tab_ref), custom_call_target="tpu_custom_call" | custom-call | tf_op jit(solution)/shard_map/pallas_call | solution.py:155
  84.6 2.0 %copy-done.2 = bf16[128,4,8,512]{3,2,1,0:T(8,128)(2,1)} copy-done((bf16[128,4,8,512]{3,2,1,0:T(8,128)(2,1)}, bf16[128,4,8,512]{3,2,1,0:T(8,128)(2,1)S(1)}, u32[]{:S(2)}) %copy-start.2) | copy-done | bytes 4194328
  86.6 7.3 %all-to-all-start = ((bf16[128,4,8,512]{3,2,1,0:T(8,128)(2,1)}), bf16[128,4,8,512]{3,2,1,0:T(8,128)(2,1)}, u32[]{:S(2)}, u32[]{:S(2)}) async-start(bf16[128,4,8,512]{3,2,1,0:T(8,128)(2,1)} %copy-done.2), calls=%async_computation | async-start | bytes 8388608 | tf_op jit(solution)/shard_map/all_to_all | solution.py:269
  94.2 2.7 %copy.21.prof_ref = f32[8,1024,1]{2,1,0:T(8,128)} copy(f32[8,1024,1]{1,0,2:T(8,128)S(1)} %convolution_bitcast_fusion) | data formatting | bytes 65536 | tf_op jit(solution)/shard_map/broadcast_in_dim | solution.py:279
  96.9 8.0 %fusion.6.theta_ref = bf16[1024,512]{1,0:T(8,128)(2,1)S(1)} fusion(f32[512]{0:T(512)S(1)} %sine_multiply_fusion, s32[512]{0:T(512)S(1)} %multiply_add_fusion), kind=kLoop, calls=%fused_computation.11 | loop fusion | flops 8388608 | bytes 1052672 | tf_op jit(solution)/shard_map/convert_element_type | solution.py:212
  104.9 40.4 %all-to-all-done = bf16[128,4,8,512]{3,2,1,0:T(8,128)(2,1)} async-done(((bf16[128,4,8,512]{3,2,1,0:T(8,128)(2,1)}), bf16[128,4,8,512]{3,2,1,0:T(8,128)(2,1)}, u32[]{:S(2)}, u32[]{:S(2)}) %all-to-all-start) | async-done | bytes 4194336 | tf_op jit(solution)/shard_map/all_to_all | solution.py:269
  145.3 4.6 %copy.24 = bf16[64,8,8,512]{3,1,2,0:T(8,128)(2,1)S(1)} copy(bf16[64,8,8,512]{3,2,1,0:T(8,128)(2,1)} %bitcast.8) | data formatting | bytes 8388608
  150.0 7.8 %shard_map.57 = f32[8,1,128]{2,1,0:T(1,128)S(1)} custom-call(bf16[1024,512]{1,0:T(8,128)(2,1)S(1)} %fusion.6.theta_ref, bf16[512,4096]{1,0:T(8,128)(2,1)S(1)} %bitcast.26, f32[8,1024,1]{2,1,0:T(8,128)S(1)} %copy-done.1, f32[1,512]{1,0:T(1,128)S(1)} %bitcast.28), custom_call_target="tpu_custom_call" | custom-call | tf_op jit(solution)/shard_map/pallas_call | solution.py:283
  158.8 2.5 %collective-permute-start.11 = (f32[8]{0:T(128)S(1)}, f32[8]{0:T(128)S(1)}, u32[]{:S(2)}, u32[]{:S(2)}) collective-permute-start(f32[8]{0:T(128)S(1)} %slice_reduce_fusion), channel_id=1, source_target_pairs={{0,2},{1,3},{2,0},{3,1},{4,6},{5,7},{6,4},{7,5},{8,10},{9,11},{10,... | collective-permute-start | bytes 104 | tf_op jit(solution)/shard_map/ppermute | solution.py:234
  165.0 11.2 %shard_map.58 = f32[1024,8,2,256]{3,2,1,0:T(2,128)} custom-call(bf16[1024,512]{1,0:T(8,128)(2,1)S(1)} %fusion.6.theta_ref, bf16[512,4096]{1,0:T(8,128)(2,1)S(1)} %bitcast.27, f32[8,1024,1]{2,1,0:T(8,128)S(1)} %copy-done.1, f32[1,512]{1,0:T(1,128)S(1)} %bitcast.29, f32[8,1,128]{2,1,0:T(1,128)S(1)} %broadcast_in_dim.30.scale_ref), custom_call_target="tpu_custom_call" | custom-call | tf_op jit(solution)/shard_map/pallas_call | solution.py:294
  (66 shorter events, 15.3 us)
Async XLA Ops:
  0.0 94.0 %copy-start = (f32[8,1024]{1,0:T(8,128)S(1)}, f32[8,1024]{1,0:T(8,128)}, u32[]{:S(2)}) copy-start(f32[8,1024]{1,0:T(8,128)} %param.8) | copy-start | bytes 98308
  0.8 3.5 %copy-start.3 = (bf16[256,8192]{1,0:T(8,128)(2,1)S(1)}, bf16[256,8192]{1,0:T(8,128)(2,1)}, u32[]{:S(2)}) copy-start(bf16[256,8192]{1,0:T(8,128)(2,1)} %sky_ref.1) | copy-start | bytes 12582916
  4.2 1.7 copy-start.4
  5.8 5.7 %collective-permute-start = (f32[16,272]{0,1:T(8,128)S(1)}, f32[16,272]{0,1:T(8,128)S(1)}, u32[]{:S(2)}, u32[]{:S(2)}) collective-permute-start(f32[16,272]{0,1:T(8,128)S(1)} %copy.17), channel_id=1, source_target_pairs={{0,4},{4,0},{8,12},{12,8},{16,20},{20,16},{24,28},{28,24},{32,36},... | collective-permute-start | bytes 52232 | tf_op jit(solution)/shard_map/ppermute | solution.py:234
  11.6 7.3 %collective-permute-start.1 = (f32[16,272]{0,1:T(8,128)S(1)}, f32[16,272]{0,1:T(8,128)S(1)}, u32[]{:S(2)}, u32[]{:S(2)}) collective-permute-start(f32[16,272]{0,1:T(8,128)S(1)} %add.163), channel_id=1, source_target_pairs={{0,8},{4,12},{8,16},{12,20},{16,24},{20,28},{24,0},{28,4},{32,40},... | collective-permute-start | bytes 52232 | tf_op jit(solution)/shard_map/ppermute | solution.py:234
  13.3 9.7 %collective-permute-start.2 = (f32[16,272]{0,1:T(8,128)S(1)}, f32[16,272]{0,1:T(8,128)S(1)}, u32[]{:S(2)}, u32[]{:S(2)}) collective-permute-start(f32[16,272]{0,1:T(8,128)S(1)} %add.163), channel_id=1, source_target_pairs={{0,16},{4,20},{8,24},{12,28},{16,0},{20,4},{24,8},{28,12},{32,48},... | collective-permute-start | bytes 52232 | tf_op jit(solution)/shard_map/ppermute | solution.py:234
  16.0 7.0 %collective-permute-start.3 = (f32[16,272]{0,1:T(8,128)S(1)}, f32[16,272]{0,1:T(8,128)S(1)}, u32[]{:S(2)}, u32[]{:S(2)}) collective-permute-start(f32[16,272]{0,1:T(8,128)S(1)} %add.163), channel_id=1, source_target_pairs={{0,24},{4,28},{8,0},{12,4},{16,8},{20,12},{24,16},{28,20},{32,56},... | collective-permute-start | bytes 52232 | tf_op jit(solution)/shard_map/ppermute | solution.py:234
  23.0 6.7 %collective-permute-start.4 = (f32[16,272]{0,1:T(8,128)S(1)}, f32[16,272]{0,1:T(8,128)S(1)}, u32[]{:S(2)}, u32[]{:S(2)}) collective-permute-start(f32[16,272]{0,1:T(8,128)S(1)} %add_add_fusion.2), channel_id=1, source_target_pairs={{0,32},{4,36},{8,40},{12,44},{16,48},{20,52},{24,56},{28,60},{32,6... | collective-permute-start | bytes 52232 | tf_op jit(solution)/shard_map/ppermute | solution.py:234
  24.7 9.1 %collective-permute-start.5 = (f32[16,272]{0,1:T(8,128)S(1)}, f32[16,272]{0,1:T(8,128)S(1)}, u32[]{:S(2)}, u32[]{:S(2)}) collective-permute-start(f32[16,272]{0,1:T(8,128)S(1)} %add_add_fusion.2), channel_id=1, source_target_pairs={{0,64},{4,68},{8,72},{12,76},{16,80},{20,84},{24,88},{28,92},{32,9... | collective-permute-start | bytes 52232 | tf_op jit(solution)/shard_map/ppermute | solution.py:234
  27.6 6.2 %collective-permute-start.6 = (f32[16,272]{0,1:T(8,128)S(1)}, f32[16,272]{0,1:T(8,128)S(1)}, u32[]{:S(2)}, u32[]{:S(2)}) collective-permute-start(f32[16,272]{0,1:T(8,128)S(1)} %add_add_fusion.2), channel_id=1, source_target_pairs={{0,96},{4,100},{8,104},{12,108},{16,112},{20,116},{24,120},{28,124... | collective-permute-start | bytes 52232 | tf_op jit(solution)/shard_map/ppermute | solution.py:234
  33.8 26.1 %collective-permute-start.7 = (f32[16,272]{0,1:T(8,128)S(1)}, f32[16,272]{0,1:T(8,128)S(1)}, u32[]{:S(2)}, u32[]{:S(2)}) collective-permute-start(f32[16,272]{0,1:T(8,128)S(1)} %add_add_fusion.1), channel_id=1, source_target_pairs={{0,1},{1,2},{2,3},{3,0},{4,5},{5,6},{6,7},{7,4},{8,9},{9,10},{10,1... | collective-permute-start | bytes 52232 | tf_op jit(solution)/shard_map/ppermute | solution.py:234
  35.8 24.1 %collective-permute-start.8 = (f32[16,272]{0,1:T(8,128)S(1)}, f32[16,272]{0,1:T(8,128)S(1)}, u32[]{:S(2)}, u32[]{:S(2)}) collective-permute-start(f32[16,272]{0,1:T(8,128)S(1)} %add_add_fusion.1), channel_id=1, source_target_pairs={{0,2},{1,3},{2,0},{3,1},{4,6},{5,7},{6,4},{7,5},{8,10},{9,11},{10,... | collective-permute-start | bytes 52232 | tf_op jit(solution)/shard_map/ppermute | solution.py:234
  39.4 20.6 %collective-permute-start.9 = (f32[16,272]{0,1:T(8,128)S(1)}, f32[16,272]{0,1:T(8,128)S(1)}, u32[]{:S(2)}, u32[]{:S(2)}) collective-permute-start(f32[16,272]{0,1:T(8,128)S(1)} %add_add_fusion.1), channel_id=1, source_target_pairs={{0,3},{1,0},{2,1},{3,2},{4,7},{5,4},{6,5},{7,6},{8,11},{9,8},{10,9... | collective-permute-start | bytes 52232 | tf_op jit(solution)/shard_map/ppermute | solution.py:234
  84.6 2.0 %copy-start.2 = (bf16[128,4,8,512]{3,2,1,0:T(8,128)(2,1)}, bf16[128,4,8,512]{3,2,1,0:T(8,128)(2,1)S(1)}, u32[]{:S(2)}) copy-start(bf16[128,4,8,512]{3,2,1,0:T(8,128)(2,1)S(1)} %shard_map.56) | copy-start | bytes 12582916
  86.6 7.4 %copy-start.5 = (s32[8]{0:T(128)S(1)}, s32[8]{0:T(128)}, u32[]{:S(2)}) copy-start(s32[8]{0:T(128)} %param.9) | copy-start | bytes 100
  86.6 58.7 %all-to-all-start = ((bf16[128,4,8,512]{3,2,1,0:T(8,128)(2,1)}), bf16[128,4,8,512]{3,2,1,0:T(8,128)(2,1)}, u32[]{:S(2)}, u32[]{:S(2)}) async-start(bf16[128,4,8,512]{3,2,1,0:T(8,128)(2,1)} %copy-done.2), calls=%async_computation | async-start | bytes 8388608 | tf_op jit(solution)/shard_map/all_to_all | solution.py:269
  145.3 4.6 %copy-start.1 = (f32[8,1024,1]{2,1,0:T(8,128)S(1)}, f32[8,1024,1]{2,1,0:T(8,128)}, u32[]{:S(2)}) copy-start(f32[8,1024,1]{2,1,0:T(8,128)} %copy.21.prof_ref) | copy-start | bytes 98308
  158.0 4.8 %collective-permute-start.10 = (f32[8]{0:T(128)S(1)}, f32[8]{0:T(128)S(1)}, u32[]{:S(2)}, u32[]{:S(2)}) collective-permute-start(f32[8]{0:T(128)S(1)} %slice_reduce_fusion), channel_id=1, source_target_pairs={{0,1},{1,2},{2,3},{3,0},{4,5},{5,6},{6,7},{7,4},{8,9},{9,10},{10,1... | collective-permute-start | bytes 104 | tf_op jit(solution)/shard_map/ppermute | solution.py:234
  158.8 5.1 %collective-permute-start.11 = (f32[8]{0:T(128)S(1)}, f32[8]{0:T(128)S(1)}, u32[]{:S(2)}, u32[]{:S(2)}) collective-permute-start(f32[8]{0:T(128)S(1)} %slice_reduce_fusion), channel_id=1, source_target_pairs={{0,2},{1,3},{2,0},{3,1},{4,6},{5,7},{6,4},{7,5},{8,10},{9,11},{10,... | collective-permute-start | bytes 104 | tf_op jit(solution)/shard_map/ppermute | solution.py:234
  161.4 3.6 %collective-permute-start.12 = (f32[8]{0:T(128)S(1)}, f32[8]{0:T(128)S(1)}, u32[]{:S(2)}, u32[]{:S(2)}) collective-permute-start(f32[8]{0:T(128)S(1)} %slice_reduce_fusion), channel_id=1, source_target_pairs={{0,3},{1,0},{2,1},{3,2},{4,7},{5,4},{6,5},{7,6},{8,11},{9,8},{10,9... | collective-permute-start | bytes 104 | tf_op jit(solution)/shard_map/ppermute | solution.py:234

commit v6 on v4

--- a/solution.py
+++ b/solution.py
@@ -81,10 +81,12 @@
     )(ca, sa, cb, sb, inv, lens)
 
 
-def fourier_kernel(len_ref, sky_ref, proj_ref, basis_ref, tab_ref, o_ref, clean_ref):
+def fourier_kernel(len_ref, sky_ref, proj_ref, basis_ref, tab_ref, oa_ref, ob_ref, clean_ref):
+    o_ref = oa_ref
     m_width = tab_ref.shape[2] // 2
-    n_grp = o_ref.shape[0] // (sky_ref.shape[0] // o_ref.shape[1])
-    chan_dev = o_ref.shape[1]
+    chan_dev = 2 * o_ref.shape[1]
+    n_grp = o_ref.shape[0] // (sky_ref.shape[0] // chan_dev)
+    half_c = o_ref.shape[1]
     length = len_ref[0][:, 0:1]
     cols = lax.broadcasted_iota(jnp.int32, (1, RPIX), 1)
     masked = jnp.where(cols < length, sky_ref[...].astype(jnp.float32), 0.0)
@@ -104,10 +106,12 @@
         for h in range(step // m_dev):
             grp_dest = (q * step - part * m_width) // m_dev + h
             for blk_dest in range(n_blk):
-                slab = res[blk_dest * chan_dev : (blk_dest + 1) * chan_dev, h * m_dev : (h + 1) * m_dev]
-                o_ref[blk_dest * n_grp + grp_dest, :, part * m_dev : (part + 1) * m_dev] = slab.astype(
-                    jnp.bfloat16
-                )
+                for half, ref in ((0, oa_ref), (1, ob_ref)):
+                    row = blk_dest * chan_dev + half * half_c
+                    slab = res[row : row + half_c, h * m_dev : (h + 1) * m_dev]
+                    ref[blk_dest * n_grp + grp_dest, :, part * m_dev : (part + 1) * m_dev] = (
+                        slab.astype(jnp.bfloat16)
+                    )
 
 
 def cycle_fourier(sky_map, projected_t, basis, tables, cycle_len, n_blk, n_grp):
@@ -129,8 +133,14 @@
             pl.BlockSpec((n_mode, RPIX), lambda k: (0, k)),
             pl.BlockSpec((1, RPIX, width), lambda k: (k, 0, 0)),
         ],
-        out_specs=pl.BlockSpec((n_dev, None, chan_dev, 2 * m_dev), lambda k: (0, k, 0, 0)),
-        out_shape=jax.ShapeDtypeStruct((n_dev, n_cyc, chan_dev, 2 * m_dev), jnp.bfloat16),
+        out_specs=[
+            pl.BlockSpec((n_dev, None, chan_dev // 2, 2 * m_dev), lambda k: (0, k, 0, 0)),
+            pl.BlockSpec((n_dev, None, chan_dev // 2, 2 * m_dev), lambda k: (0, k, 0, 0)),
+        ],
+        out_shape=[
+            jax.ShapeDtypeStruct((n_dev, n_cyc, chan_dev // 2, 2 * m_dev), jnp.bfloat16),
+            jax.ShapeDtypeStruct((n_dev, n_cyc, chan_dev // 2, 2 * m_dev), jnp.bfloat16),
+        ],
         scratch_shapes=[pltpu.VMEM((n_chan, RPIX), jnp.bfloat16)],
         compiler_params=pltpu.CompilerParams(vmem_limit_bytes=48 * 1024 * 1024),
     )(lens, sky_map, projected_t, basis, tables)
@@ -159,11 +169,15 @@
             o_ref[pl.ds(lc * 256, 256), 0, p, :] = w[:, p * half : (p + 1) * half]
 
 
-def harmonic_specs(n_l, n_cycle, width):
+def output_kernel_aliased(theta_ref, mv_ref, prof_ref, mw_ref, scale_ref, prev_ref, o_ref):
+    output_kernel(theta_ref, mv_ref, prof_ref, mw_ref, scale_ref, o_ref)
+
+
+def harmonic_specs(n_l, n_cycle, width, offset):
     return [
         pl.BlockSpec((n_l, n_cycle), lambda c: (0, 0)),
         pl.BlockSpec((n_cycle, width), lambda c: (0, c)),
-        pl.BlockSpec((1, n_l, 1), lambda c: (c, 0, 0)),
+        pl.BlockSpec((1, n_l, 1), lambda c: (c + offset, 0, 0)),
         pl.BlockSpec((1, width), lambda c: (0, 0)),
     ]
 
@@ -232,9 +246,7 @@
     lower = jnp.linalg.cholesky(gram_sum)
     basis = jax.scipy.linalg.solve_triangular(lower, amps_wide, lower=True)
     projected = jax.scipy.linalg.solve_triangular(lower, cross_sum, lower=True)
-    sendbuf = cycle_fourier(sky_map, projected.T, basis, tables, cycle_len, n_blk, n_grp)
-    moved = lax.all_to_all(sendbuf, ("blk", "grp"), 0, 0, tiled=True)
-    moved = moved.reshape(n_cycle, chan_dev * 2 * M_DEV)
+    sends = cycle_fourier(sky_map, projected.T, basis, tables, cycle_len, n_blk, n_grp)
     theta_tab = theta_table(jnp.arange(n_cycle, dtype=jnp.int32), n_cycle)
     onehot = (
         beam_index[:, None] == jnp.arange(beam_profile.shape[0], dtype=jnp.int32)[None, :]
@@ -245,27 +257,44 @@
     mw_row = jnp.concatenate([mweight, mweight])[None, :]
     prof_col = profiles[:, :, None]
     width = 2 * M_DEV
-    specs = harmonic_specs(L, n_cycle, width)
+    half_c = chan_dev // 2
     vmem = pltpu.CompilerParams(vmem_limit_bytes=32 * 1024 * 1024)
-    power_part = pl.pallas_call(
-        power_kernel,
-        grid=(chan_dev,),
-        in_specs=specs,
-        out_specs=pl.BlockSpec((1, 1, 128), lambda c: (c, 0, 0)),
-        out_shape=jax.ShapeDtypeStruct((chan_dev, 1, 128), jnp.float32),
-        compiler_params=vmem,
-    )(theta_tab, moved, prof_col, mw_row)[:, 0, 0]
-    power = ring_sum(power_part, subs[3:])
-    scale = lax.rsqrt(power / (2.0 * L * m_width) + 1e-06)
-    scale = jnp.broadcast_to(scale[:, None, None], (chan_dev, 1, 128))
-    return pl.pallas_call(
-        output_kernel,
-        grid=(chan_dev,),
-        in_specs=specs + [pl.BlockSpec((1, 1, 128), lambda c: (c, 0, 0))],
-        out_specs=pl.BlockSpec((L, 1, 2, M_DEV), lambda c: (0, c, 0, 0)),
-        out_shape=jax.ShapeDtypeStruct((L, chan_dev, 2, M_DEV), jnp.float32),
-        compiler_params=vmem,
-    )(theta_tab, moved, prof_col, mw_row, scale)
+    out = None
+    for half, sendbuf in enumerate(sends):
+        moved = lax.all_to_all(sendbuf, ("blk", "grp"), 0, 0, tiled=True)
+        moved = moved.reshape(n_cycle, half_c * width)
+        specs = harmonic_specs(L, n_cycle, width, half * half_c)
+        power_part = pl.pallas_call(
+            power_kernel,
+            grid=(half_c,),
+            in_specs=specs,
+            out_specs=pl.BlockSpec((1, 1, 128), lambda c: (c, 0, 0)),
+            out_shape=jax.ShapeDtypeStruct((half_c, 1, 128), jnp.float32),
+            compiler_params=vmem,
+        )(theta_tab, moved, prof_col, mw_row)[:, 0, 0]
+        power = ring_sum(power_part, subs[3:])
+        scale = lax.rsqrt(power / (2.0 * L * m_width) + 1e-06)
+        scale = jnp.broadcast_to(scale[:, None, None], (half_c, 1, 128))
+        args = [theta_tab, moved, prof_col, mw_row, scale]
+        in_specs = specs + [pl.BlockSpec((1, 1, 128), lambda c: (c, 0, 0))]
+        aliases = {}
+        kernel = output_kernel
+        if out is not None:
+            args.append(out)
+            in_specs.append(pl.BlockSpec(memory_space=pl.ANY))
+            aliases = {len(args) - 1: 0}
+            kernel = output_kernel_aliased
+        offset = half * half_c
+        out = pl.pallas_call(
+            kernel,
+            grid=(half_c,),
+            in_specs=in_specs,
+            out_specs=pl.BlockSpec((L, 1, 2, M_DEV), lambda c: (0, c + offset, 0, 0)),
+            out_shape=jax.ShapeDtypeStruct((L, chan_dev, 2, M_DEV), jnp.float32),
+            input_output_aliases=aliases,
+            compiler_params=vmem,
+        )(*args)
+    return out
 
 
 def solution(mesh):

time: 175 us -> 180 us (1.029)
  waiting for transfers between devices: 51.4 us -> 13.8 us
  blocking collectives: 0 us -> 36.4 us
  starting transfers between devices: 29.6 us -> 33.4 us
  Pallas kernels: 55.1 us -> 57.3 us
    all_to_all x0 -> x1, blocking collectives: none -> 36.4 us  [body(): moved = lax.all_to_all(sendbuf, ('blk', 'grp'), 0, 0, tiled=True)]
    all_to_all x1, waiting for transfers between devices: 40.2 us -> 5.93 us  [body(): moved = lax.all_to_all(sendbuf, ('blk', 'grp'), 0, 0, tiled=True)]
    ppermute x13 -> x16, starting transfers between devices: 22.1 us -> 27.3 us  [ring_sum(): lax.ppermute(v, axis, shift_perm(size, stride, total, k))]
    ppermute x13 -> x16, waiting for transfers between devices: 11.2 us -> 7.91 us  [ring_sum(): lax.ppermute(v, axis, shift_perm(size, stride, total, k))]
    pallas_call x2 -> x4, Pallas kernels: 19 us -> 20.4 us  [the longest x2 12.4 us: body(): pl.pallas_call(kernel, grid=(half_c,), in_specs=in_specs, out_specs=pl.Bl...]
    unnamed x14 -> x17, local copies, waits for them, and re-layouts: 7.07 us -> 6.08 us
  transfers between devices with their start and end apart: 14 -> 17, of which waited for: 7 -> 4; matrix products, arithmetic and copies ran while one was open for 12% -> 15% of each run, Pallas kernels for 9% -> 17%
where the time goes in v6:
time: 180 us; the launch traced here: 179 us
  Pallas kernels  57.3 us (32%)
  blocking collectives  36.4 us (20%)
  starting transfers between devices  33.4 us (19%)
  other arithmetic  22.9 us (13%)
  waiting for transfers between devices  13.8 us (8%)
  local copies, waits for them, and re-layouts  9.47 us (5%)
  matrix products  5.29 us (3%)
    all_to_all x1, blocking collectives, body(): moved = lax.all_to_all(sendbuf, ('blk', 'grp'), 0, 0, tiled=True)  36.4 us
    ppermute x16, starting transfers between devices, ring_sum(): lax.ppermute(v, axis, shift_perm(size, stride, total, k))  27.3 us
    pallas_call x1, Pallas kernels, cycle_fourier(): pl.pallas_call(fourier_kernel, grid=(n_cyc,), in_specs=[pl.BlockSpec((1,...  20.7 us
    pallas_call x1, Pallas kernels, cycle_tables(): pl.pallas_call(table_kernel, grid=(n_cyc,), in_specs=[pl.BlockSpec((1, n_...  16.2 us
    pallas_call x2, Pallas kernels, body(): pl.pallas_call(kernel, grid=(half_c,), in_specs=in_specs, out_specs=pl.Bl...  12.4 us
    cos x2, other arithmetic, cos_sin_of_phase(): return (jnp.cos(angle), jnp.sin(angle))  8.81 us
    pallas_call x2, Pallas kernels, body(): pl.pallas_call(power_kernel, grid=(half_c,), in_specs=specs, out_specs=pl...  7.97 us
    convert_element_type x1, other arithmetic, theta_table(): return (jnp.cos(angle) * weight[None, :]).astype(jnp.bfloat16)  7.96 us
  transfers between devices with their start and end apart: 17, of which 4 were waited for; matrix products, arithmetic and copies ran while one was open for 15% of the time, Pallas kernels for 17%

profile of v6, /device:TPU:0, one launch (start us, length us, event | category | flops | bytes accessed | tf_op | source)
XLA Modules:
  0.0 179.0 jit_solution(8708123001546794593)
XLA Ops:
  0.8 3.0 %convolution_convert_fusion = bf16[8192,16]{0,1:T(8,128)(2,1)S(1)} fusion(bf16[256,16]{0,1:T(8,128)(2,1)} %param.6, bf16[256,8192]{1,0:T(8,128)(2,1)} %sky_ref.1, pred[8192]{0:T(1024)(128)(4,1)S(1)} %bitcast.42), kind=kOutput, calls=%fused_computation | convolution fusion | flops 69337088 | bytes 4472832 | tf_op jit(solution)/shard_map/dot_general | solution.py:233
  6.3 7.0 %fusion.34 = (f32[4,16,1024]{2,1,0:T(8,128)S(1)}, f32[4,16,1024]{2,1,0:T(8,128)S(1)}, f32[4,16,1024]{2,1,0:T(8,128)S(1)}, f32[4,16,1024]{2,1,0:T(8,128)S(1)}) fusion(f32[4]{0:T(128)S(1)} %get-tuple-element.20, pred[4]{0:T(512)(128)(4,1)S(1)} %broadcast_compare_fusion, s32[4]{0:T(128)S(1)} %get-tuple-element.19, s32[16,1024]{1,0:T(8,128)S(1)} %iota_multiply_fusion, ...), kind=kLoop, calls=%fused_computation.53 | loop fusion | flops 1376256 | bytes 1114404 | tf_op jit(solution)/shard_map/cos | solution.py:16
  15.2 2.7 %collective-permute-start.2 = (f32[16,272]{0,1:T(8,128)S(1)}, f32[16,272]{0,1:T(8,128)S(1)}, u32[]{:S(2)}, u32[]{:S(2)}) collective-permute-start(f32[16,272]{0,1:T(8,128)S(1)} %add.204), channel_id=1, source_target_pairs={{0,16},{4,20},{8,24},{12,28},{16,0},{20,4},{24,8},{28,12},{32,48},... | collective-permute-start | bytes 52232 | tf_op jit(solution)/shard_map/ppermute | solution.py:215
  19.3 1.8 %fusion.38 = (f32[4,8,1024]{2,1,0:T(8,128)S(1)}, f32[4,8,1024]{2,1,0:T(8,128)S(1)}) fusion(f32[4]{0:T(128)S(1)} %get-tuple-element.20, pred[4]{0:T(512)(128)(4,1)S(1)} %broadcast_compare_fusion, s32[4]{0:T(128)S(1)} %get-tuple-element.19, s32[4,8]{1,0:T(4,128)S(1)} %remainder_select_fusion.1), kind=kLoop, calls=%fused_computation.58 | loop fusion | flops 360448 | bytes 262308 | tf_op jit(solution)/shard_map/cos | solution.py:16
  21.2 3.7 %collective-permute-done.2 = f32[16,272]{0,1:T(8,128)S(1)} collective-permute-done((f32[16,272]{0,1:T(8,128)S(1)}, f32[16,272]{0,1:T(8,128)S(1)}, u32[]{:S(2)}, u32[]{:S(2)}) %collective-permute-start.2) | collective-permute-done | bytes 17440 | tf_op jit(solution)/shard_map/ppermute | solution.py:215
  26.6 2.9 %collective-permute-start.5 = (f32[16,272]{0,1:T(8,128)S(1)}, f32[16,272]{0,1:T(8,128)S(1)}, u32[]{:S(2)}, u32[]{:S(2)}) collective-permute-start(f32[16,272]{0,1:T(8,128)S(1)} %add_add_fusion.2), channel_id=1, source_target_pairs={{0,64},{4,68},{8,72},{12,76},{16,80},{20,84},{24,88},{28,92},{32,9... | collective-permute-start | bytes 52232 | tf_op jit(solution)/shard_map/ppermute | solution.py:215
  31.6 4.0 %collective-permute-done.5 = f32[16,272]{0,1:T(8,128)S(1)} collective-permute-done((f32[16,272]{0,1:T(8,128)S(1)}, f32[16,272]{0,1:T(8,128)S(1)}, u32[]{:S(2)}, u32[]{:S(2)}) %collective-permute-start.5) | collective-permute-done | bytes 17440 | tf_op jit(solution)/shard_map/ppermute | solution.py:215
  35.7 2.0 %collective-permute-start.7 = (f32[16,272]{0,1:T(8,128)S(1)}, f32[16,272]{0,1:T(8,128)S(1)}, u32[]{:S(2)}, u32[]{:S(2)}) collective-permute-start(f32[16,272]{0,1:T(8,128)S(1)} %add_add_fusion.1), channel_id=1, source_target_pairs={{0,1},{1,2},{2,3},{3,0},{4,5},{5,6},{6,7},{7,4},{8,9},{9,10},{10,1... | collective-permute-start | bytes 52232 | tf_op jit(solution)/shard_map/ppermute | solution.py:215
  37.7 3.6 %collective-permute-start.8 = (f32[16,272]{0,1:T(8,128)S(1)}, f32[16,272]{0,1:T(8,128)S(1)}, u32[]{:S(2)}, u32[]{:S(2)}) collective-permute-start(f32[16,272]{0,1:T(8,128)S(1)} %add_add_fusion.1), channel_id=1, source_target_pairs={{0,2},{1,3},{2,0},{3,1},{4,6},{5,7},{6,4},{7,5},{8,10},{9,11},{10,... | collective-permute-start | bytes 52232 | tf_op jit(solution)/shard_map/ppermute | solution.py:215
  42.4 16.2 %shard_map.55.tab_ref = bf16[4,2048,2048]{2,1,0:T(8,128)(2,1)} custom-call(f32[4,16,1024]{2,1,0:T(8,128)S(1)} %get-tuple-element.17.ca_ref, f32[4,16,1024]{2,1,0:T(8,128)S(1)} %get-tuple-element.18.sa_ref, f32[4,128,1024]{2,1,0:T(8,128)S(1)} %bitcast.36, f32[4,128,1024]{2,1,0:T(8,128)S(1)} %bitcast.35, f32[4,1,128]{2,1,0:T(1,128)S(1)} %broadcast_in_dim.29.inv_ref, ...), custom_call_target="tpu_custom_call" | custom-call | tf_op jit(solution)/shard_map/pallas_call | solution.py:67
  63.5 20.7 %shard_map.56 = (bf16[128,4,4,512]{3,2,1,0:T(4,128)(2,1)S(1)}, bf16[128,4,4,512]{3,2,1,0:T(4,128)(2,1)}) custom-call(s32[4,1,128]{2,1,0:T(1,128)S(1)} %broadcast_in_dim.25.len_ref, bf16[256,8192]{1,0:T(8,128)(2,1)} %sky_ref.1, f32[256,16]{1,0:T(8,128)S(1)} %fusion.27.proj_ref, f32[16,8192]{1,0:T(8,128)S(1)} %fusion.41.basis_ref, ...), custom_call_target="tpu_custom_call" | custom-call | tf_op jit(solution)/shard_map/pallas_call | solution.py:126
  84.1 36.4 %all_to_all.10 = bf16[128,4,4,512]{3,2,1,0:T(4,128)(2,1)} all-to-all(bf16[128,4,4,512]{3,2,1,0:T(4,128)(2,1)S(1)} %get-tuple-element.8), channel_id=1, replica_groups=mesh['blk'=32,'grp'=4] {'blk','grp'}, dimensions={0} | all-to-all | bytes 4194304 | tf_op jit(solution)/shard_map/all_to_all | solution.py:264
  120.6 6.1 %all-to-all-start = ((bf16[128,4,4,512]{3,2,1,0:T(4,128)(2,1)}), bf16[128,4,4,512]{3,2,1,0:T(4,128)(2,1)}, u32[]{:S(2)}, u32[]{:S(2)}) async-start(bf16[128,4,4,512]{3,2,1,0:T(4,128)(2,1)} %get-tuple-element.7), calls=%async_computation | async-start | bytes 4194304 | tf_op jit(solution)/shard_map/all_to_all | solution.py:264
  126.9 2.7 %copy.26.prof_ref = f32[8,1024,1]{2,1,0:T(8,128)} copy(f32[8,1024,1]{1,0,2:T(8,128)S(1)} %convolution_bitcast_fusion) | data formatting | bytes 65536 | tf_op jit(solution)/shard_map/broadcast_in_dim | solution.py:258
  129.7 8.0 %fusion.6.theta_ref = bf16[1024,512]{1,0:T(8,128)(2,1)S(1)} fusion(f32[512]{0:T(512)S(1)} %sine_multiply_fusion, s32[512]{0:T(512)S(1)} %multiply_add_fusion.1), kind=kLoop, calls=%fused_computation.11 | loop fusion | flops 8388608 | bytes 1052672 | tf_op jit(solution)/shard_map/convert_element_type | solution.py:193
  137.6 2.4 %copy.30 = bf16[64,8,4,512]{3,1,2,0:T(8,128)(2,1)S(1)} copy(bf16[64,8,4,512]{3,2,1,0:T(4,128)(2,1)} %bitcast.41) | data formatting | bytes 4194304
  140.5 4.0 %shard_map.58 = f32[4,1,128]{2,1,0:T(1,128)S(1)} custom-call(bf16[1024,512]{1,0:T(8,128)(2,1)S(1)} %fusion.6.theta_ref, bf16[512,2048]{1,0:T(8,128)(2,1)S(1)} %bitcast.31, f32[8,1024,1]{2,1,0:T(8,128)S(1)} %copy-done.2, f32[1,512]{1,0:T(1,128)S(1)} %bitcast.37), custom_call_target="tpu_custom_call" | custom-call | tf_op jit(solution)/shard_map/pallas_call | solution.py:267
  145.4 3.2 %collective-permute-start.14 = (f32[4]{0:T(128)S(1)}, f32[4]{0:T(128)S(1)}, u32[]{:S(2)}, u32[]{:S(2)}) collective-permute-start(f32[4]{0:T(128)S(1)} %slice_reduce_fusion), channel_id=1, source_target_pairs={{0,2},{1,3},{2,0},{3,1},{4,6},{5,7},{6,4},{7,5},{8,10},{9,11},{10,... | collective-permute-start | bytes 56 | tf_op jit(solution)/shard_map/ppermute | solution.py:215
  149.8 5.9 %all-to-all-done = bf16[128,4,4,512]{3,2,1,0:T(4,128)(2,1)} async-done(((bf16[128,4,4,512]{3,2,1,0:T(4,128)(2,1)}), bf16[128,4,4,512]{3,2,1,0:T(4,128)(2,1)}, u32[]{:S(2)}, u32[]{:S(2)}) %all-to-all-start) | async-done | bytes 2097184 | tf_op jit(solution)/shard_map/all_to_all | solution.py:264
  155.8 2.4 %copy.29 = bf16[64,8,4,512]{3,1,2,0:T(8,128)(2,1)S(1)} copy(bf16[64,8,4,512]{3,2,1,0:T(4,128)(2,1)} %bitcast.10) | data formatting | bytes 4194304
  158.6 4.0 %shard_map.57 = f32[4,1,128]{2,1,0:T(1,128)S(1)} custom-call(bf16[1024,512]{1,0:T(8,128)(2,1)S(1)} %fusion.6.theta_ref, bf16[512,2048]{1,0:T(8,128)(2,1)S(1)} %bitcast.33, f32[8,1024,1]{2,1,0:T(8,128)S(1)} %copy-done.3, f32[1,512]{1,0:T(1,128)S(1)} %bitcast.38), custom_call_target="tpu_custom_call" | custom-call | tf_op jit(solution)/shard_map/pallas_call | solution.py:267
  163.6 1.8 %collective-permute-start.11 = (f32[4]{0:T(128)S(1)}, f32[4]{0:T(128)S(1)}, u32[]{:S(2)}, u32[]{:S(2)}) collective-permute-start(f32[4]{0:T(128)S(1)} %slice_reduce_fusion.1), channel_id=1, source_target_pairs={{0,2},{1,3},{2,0},{3,1},{4,6},{5,7},{6,4},{7,5},{8,10},{9,11},{10,... | collective-permute-start | bytes 56 | tf_op jit(solution)/shard_map/ppermute | solution.py:215
  166.4 6.2 %shard_map.59.prev_ref = f32[1024,8,2,256]{3,2,1,0:T(2,128)} custom-call(bf16[1024,512]{1,0:T(8,128)(2,1)S(1)} %fusion.6.theta_ref, bf16[512,2048]{1,0:T(8,128)(2,1)S(1)} %bitcast.32, f32[8,1024,1]{2,1,0:T(8,128)S(1)} %copy-done.3, f32[1,512]{1,0:T(1,128)S(1)} %bitcast.39, f32[4,1,128]{2,1,0:T(1,128)S(1)} %broadcast_in_dim.33.scale_ref), custom_call_target="tpu_custom_call" | custom-call | tf_op jit(solution)/shard_map/pallas_call | solution.py:288
  172.7 6.2 %shard_map.60 = f32[1024,8,2,256]{3,2,1,0:T(2,128)} custom-call(bf16[1024,512]{1,0:T(8,128)(2,1)S(1)} %fusion.6.theta_ref, bf16[512,2048]{1,0:T(8,128)(2,1)S(1)} %bitcast.34, f32[8,1024,1]{2,1,0:T(8,128)S(1)} %copy-done.3, f32[1,512]{1,0:T(1,128)S(1)} %bitcast.40, f32[4,1,128]{2,1,0:T(1,128)S(1)} %broadcast_in_dim.32.scale_ref, ...), custom_call_target="tpu_custom_call", output_to_operand_aliasing={{}: (5, {})} | custom-call | tf_op jit(solution)/shard_map/pallas_call | solution.py:288
  (81 shorter events, 21.8 us)
Async XLA Ops:
  0.0 126.7 %copy-start = (f32[8,1024]{1,0:T(8,128)S(1)}, f32[8,1024]{1,0:T(8,128)}, u32[]{:S(2)}) copy-start(f32[8,1024]{1,0:T(8,128)} %param.8) | copy-start | bytes 98308
  0.8 3.5 %copy-start.4 = (bf16[256,8192]{1,0:T(8,128)(2,1)S(1)}, bf16[256,8192]{1,0:T(8,128)(2,1)}, u32[]{:S(2)}) copy-start(bf16[256,8192]{1,0:T(8,128)(2,1)} %sky_ref.1) | copy-start | bytes 12582916
  4.2 1.7 copy-start.5
  5.8 7.6 %collective-permute-start = (f32[16,272]{0,1:T(8,128)S(1)}, f32[16,272]{0,1:T(8,128)S(1)}, u32[]{:S(2)}, u32[]{:S(2)}) collective-permute-start(f32[16,272]{0,1:T(8,128)S(1)} %copy.20), channel_id=1, source_target_pairs={{0,4},{4,0},{8,12},{12,8},{16,20},{20,16},{24,28},{28,24},{32,36},... | collective-permute-start | bytes 52232 | tf_op jit(solution)/shard_map/ppermute | solution.py:215
  13.5 7.7 %collective-permute-start.1 = (f32[16,272]{0,1:T(8,128)S(1)}, f32[16,272]{0,1:T(8,128)S(1)}, u32[]{:S(2)}, u32[]{:S(2)}) collective-permute-start(f32[16,272]{0,1:T(8,128)S(1)} %add.204), channel_id=1, source_target_pairs={{0,8},{4,12},{8,16},{12,20},{16,24},{20,28},{24,0},{28,4},{32,40},... | collective-permute-start | bytes 52232 | tf_op jit(solution)/shard_map/ppermute | solution.py:215
  15.2 9.7 %collective-permute-start.2 = (f32[16,272]{0,1:T(8,128)S(1)}, f32[16,272]{0,1:T(8,128)S(1)}, u32[]{:S(2)}, u32[]{:S(2)}) collective-permute-start(f32[16,272]{0,1:T(8,128)S(1)} %add.204), channel_id=1, source_target_pairs={{0,16},{4,20},{8,24},{12,28},{16,0},{20,4},{24,8},{28,12},{32,48},... | collective-permute-start | bytes 52232 | tf_op jit(solution)/shard_map/ppermute | solution.py:215
  17.9 7.0 %collective-permute-start.3 = (f32[16,272]{0,1:T(8,128)S(1)}, f32[16,272]{0,1:T(8,128)S(1)}, u32[]{:S(2)}, u32[]{:S(2)}) collective-permute-start(f32[16,272]{0,1:T(8,128)S(1)} %add.204), channel_id=1, source_target_pairs={{0,24},{4,28},{8,0},{12,4},{16,8},{20,12},{24,16},{28,20},{32,56},... | collective-permute-start | bytes 52232 | tf_op jit(solution)/shard_map/ppermute | solution.py:215
  24.9 6.7 %collective-permute-start.4 = (f32[16,272]{0,1:T(8,128)S(1)}, f32[16,272]{0,1:T(8,128)S(1)}, u32[]{:S(2)}, u32[]{:S(2)}) collective-permute-start(f32[16,272]{0,1:T(8,128)S(1)} %add_add_fusion.2), channel_id=1, source_target_pairs={{0,32},{4,36},{8,40},{12,44},{16,48},{20,52},{24,56},{28,60},{32,6... | collective-permute-start | bytes 52232 | tf_op jit(solution)/shard_map/ppermute | solution.py:215
  26.6 9.1 %collective-permute-start.5 = (f32[16,272]{0,1:T(8,128)S(1)}, f32[16,272]{0,1:T(8,128)S(1)}, u32[]{:S(2)}, u32[]{:S(2)}) collective-permute-start(f32[16,272]{0,1:T(8,128)S(1)} %add_add_fusion.2), channel_id=1, source_target_pairs={{0,64},{4,68},{8,72},{12,76},{16,80},{20,84},{24,88},{28,92},{32,9... | collective-permute-start | bytes 52232 | tf_op jit(solution)/shard_map/ppermute | solution.py:215
  29.5 6.2 %collective-permute-start.6 = (f32[16,272]{0,1:T(8,128)S(1)}, f32[16,272]{0,1:T(8,128)S(1)}, u32[]{:S(2)}, u32[]{:S(2)}) collective-permute-start(f32[16,272]{0,1:T(8,128)S(1)} %add_add_fusion.2), channel_id=1, source_target_pairs={{0,96},{4,100},{8,104},{12,108},{16,112},{20,116},{24,120},{28,124... | collective-permute-start | bytes 52232 | tf_op jit(solution)/shard_map/ppermute | solution.py:215
  35.7 23.0 %collective-permute-start.7 = (f32[16,272]{0,1:T(8,128)S(1)}, f32[16,272]{0,1:T(8,128)S(1)}, u32[]{:S(2)}, u32[]{:S(2)}) collective-permute-start(f32[16,272]{0,1:T(8,128)S(1)} %add_add_fusion.1), channel_id=1, source_target_pairs={{0,1},{1,2},{2,3},{3,0},{4,5},{5,6},{6,7},{7,4},{8,9},{9,10},{10,1... | collective-permute-start | bytes 52232 | tf_op jit(solution)/shard_map/ppermute | solution.py:215
  37.7 21.0 %collective-permute-start.8 = (f32[16,272]{0,1:T(8,128)S(1)}, f32[16,272]{0,1:T(8,128)S(1)}, u32[]{:S(2)}, u32[]{:S(2)}) collective-permute-start(f32[16,272]{0,1:T(8,128)S(1)} %add_add_fusion.1), channel_id=1, source_target_pairs={{0,2},{1,3},{2,0},{3,1},{4,6},{5,7},{6,4},{7,5},{8,10},{9,11},{10,... | collective-permute-start | bytes 52232 | tf_op jit(solution)/shard_map/ppermute | solution.py:215
  41.2 17.4 %collective-permute-start.9 = (f32[16,272]{0,1:T(8,128)S(1)}, f32[16,272]{0,1:T(8,128)S(1)}, u32[]{:S(2)}, u32[]{:S(2)}) collective-permute-start(f32[16,272]{0,1:T(8,128)S(1)} %add_add_fusion.1), channel_id=1, source_target_pairs={{0,3},{1,0},{2,1},{3,2},{4,7},{5,4},{6,5},{7,6},{8,11},{9,8},{10,9... | collective-permute-start | bytes 52232 | tf_op jit(solution)/shard_map/ppermute | solution.py:215
  120.6 6.2 %copy-start.6 = (s32[8]{0:T(128)S(1)}, s32[8]{0:T(128)}, u32[]{:S(2)}) copy-start(s32[8]{0:T(128)} %param.9) | copy-start | bytes 100
  120.6 35.2 %all-to-all-start = ((bf16[128,4,4,512]{3,2,1,0:T(4,128)(2,1)}), bf16[128,4,4,512]{3,2,1,0:T(4,128)(2,1)}, u32[]{:S(2)}, u32[]{:S(2)}) async-start(bf16[128,4,4,512]{3,2,1,0:T(4,128)(2,1)} %get-tuple-element.7), calls=%async_computation | async-start | bytes 4194304 | tf_op jit(solution)/shard_map/all_to_all | solution.py:264
  137.6 2.8 %copy-start.2 = (f32[8,1024,1]{2,1,0:T(8,128)S(1)}, f32[8,1024,1]{2,1,0:T(8,128)}, u32[]{:S(2)}) copy-start(f32[8,1024,1]{2,1,0:T(8,128)} %copy.26.prof_ref) | copy-start | bytes 98308
  144.6 20.8 %collective-permute-start.13 = (f32[4]{0:T(128)S(1)}, f32[4]{0:T(128)S(1)}, u32[]{:S(2)}, u32[]{:S(2)}) collective-permute-start(f32[4]{0:T(128)S(1)} %slice_reduce_fusion), channel_id=1, source_target_pairs={{0,1},{1,2},{2,3},{3,0},{4,5},{5,6},{6,7},{7,4},{8,9},{9,10},{10,1... | collective-permute-start | bytes 56 | tf_op jit(solution)/shard_map/ppermute | solution.py:215
  145.4 20.9 %collective-permute-start.14 = (f32[4]{0:T(128)S(1)}, f32[4]{0:T(128)S(1)}, u32[]{:S(2)}, u32[]{:S(2)}) collective-permute-start(f32[4]{0:T(128)S(1)} %slice_reduce_fusion), channel_id=1, source_target_pairs={{0,2},{1,3},{2,0},{3,1},{4,6},{5,7},{6,4},{7,5},{8,10},{9,11},{10,... | collective-permute-start | bytes 56 | tf_op jit(solution)/shard_map/ppermute | solution.py:215
  148.6 17.7 %collective-permute-start.15 = (f32[4]{0:T(128)S(1)}, f32[4]{0:T(128)S(1)}, u32[]{:S(2)}, u32[]{:S(2)}) collective-permute-start(f32[4]{0:T(128)S(1)} %slice_reduce_fusion), channel_id=1, source_target_pairs={{0,3},{1,0},{2,1},{3,2},{4,7},{5,4},{6,5},{7,6},{8,11},{9,8},{10,9... | collective-permute-start | bytes 56 | tf_op jit(solution)/shard_map/ppermute | solution.py:215
  155.8 2.8 %copy-start.3 = (f32[8,1024,1]{2,1,0:T(8,128)S(1)}, f32[8,1024,1]{2,1,0:T(8,128)}, u32[]{:S(2)}) copy-start(f32[8,1024,1]{2,1,0:T(8,128)} %copy.26.prof_ref) | copy-start | bytes 98308
  162.7 10.0 %collective-permute-start.10 = (f32[4]{0:T(128)S(1)}, f32[4]{0:T(128)S(1)}, u32[]{:S(2)}, u32[]{:S(2)}) collective-permute-start(f32[4]{0:T(128)S(1)} %slice_reduce_fusion.1), channel_id=1, source_target_pairs={{0,1},{1,2},{2,3},{3,0},{4,5},{5,6},{6,7},{7,4},{8,9},{9,10},{10,1... | collective-permute-start | bytes 56 | tf_op jit(solution)/shard_map/ppermute | solution.py:215
  163.6 9.1 %collective-permute-start.11 = (f32[4]{0:T(128)S(1)}, f32[4]{0:T(128)S(1)}, u32[]{:S(2)}, u32[]{:S(2)}) collective-permute-start(f32[4]{0:T(128)S(1)} %slice_reduce_fusion.1), channel_id=1, source_target_pairs={{0,2},{1,3},{2,0},{3,1},{4,6},{5,7},{6,4},{7,5},{8,10},{9,11},{10,... | collective-permute-start | bytes 56 | tf_op jit(solution)/shard_map/ppermute | solution.py:215
  165.4 7.3 %collective-permute-start.12 = (f32[4]{0:T(128)S(1)}, f32[4]{0:T(128)S(1)}, u32[]{:S(2)}, u32[]{:S(2)}) collective-permute-start(f32[4]{0:T(128)S(1)} %slice_reduce_fusion.1), channel_id=1, source_target_pairs={{0,3},{1,0},{2,1},{3,2},{4,7},{5,4},{6,5},{7,6},{8,11},{9,8},{10,9... | collective-permute-start | bytes 56 | tf_op jit(solution)/shard_map/ppermute | solution.py:215
  172.7 6.2 %copy-start.1 = (f32[8,1024]{1,0:T(8,128)S(1)}, f32[8,1024]{1,0:T(8,128)}, u32[]{:S(2)}) copy-start(f32[8,1024]{1,0:T(8,128)} %param.8) | copy-start | bytes 98308

commit v7 on v4

--- a/solution.py
+++ b/solution.py
@@ -198,9 +198,16 @@
 
 def ring_sum(v, subs):
     for axis, size, stride, total in subs:
-        parts = [lax.ppermute(v, axis, shift_perm(size, stride, total, k)) for k in range(1, size)]
-        for part in parts:
-            v = v + part
+        if size & (size - 1):
+            parts = [lax.ppermute(v, axis, shift_perm(size, stride, total, k)) for k in range(1, size)]
+            for part in parts:
+                v = v + part
+            continue
+        k = 1
+        while k < size:
+            pairs = [(i, i ^ (k * stride)) for i in range(total)]
+            v = v + lax.ppermute(v, axis, pairs)
+            k *= 2
     return v
 
 

time: 175 us -> 181 us (1.034)
  waiting for transfers between devices: 51.4 us -> 59.3 us
  starting transfers between devices: 29.6 us -> 27.3 us
    ppermute x13 -> x9, waiting for transfers between devices: 11.2 us -> 19 us  [ring_sum(): v = v + lax.ppermute(v, axis, pairs)]
    ppermute x13 -> x9, starting transfers between devices: 22.1 us -> 19.2 us  [ring_sum(): v = v + lax.ppermute(v, axis, pairs)]
  transfers between devices with their start and end apart: 14 -> 10, of which waited for: 7 -> 8; matrix products, arithmetic and copies ran while one was open for 12% -> 12% of each run, Pallas kernels for 9% -> 9%
where the time goes in v7:
time: 181 us; the launch traced here: 180 us
  waiting for transfers between devices  59.3 us (33%)
  Pallas kernels  55.1 us (30%)
  starting transfers between devices  27.3 us (15%)
  other arithmetic  22.9 us (13%)
  local copies, waits for them, and re-layouts  10.3 us (6%)
  matrix products  5.3 us (3%)
    all_to_all x1, waiting for transfers between devices, body(): moved = lax.all_to_all(sendbuf, ('blk', 'grp'), 0, 0, tiled=True)  40.2 us
    pallas_call x1, Pallas kernels, cycle_fourier(): pl.pallas_call(fourier_kernel, grid=(n_cyc,), in_specs=[pl.BlockSpec((1,...  19.8 us
    ppermute x9, starting transfers between devices, ring_sum(): v = v + lax.ppermute(v, axis, pairs)  19.2 us
    ppermute x9, waiting for transfers between devices, ring_sum(): v = v + lax.ppermute(v, axis, pairs)  19 us
    pallas_call x1, Pallas kernels, cycle_tables(): pl.pallas_call(table_kernel, grid=(n_cyc,), in_specs=[pl.BlockSpec((1, n_...  16.2 us
    pallas_call x1, Pallas kernels, body(): pl.pallas_call(output_kernel, grid=(chan_dev,), in_specs=specs + [pl.Bloc...  11.2 us
    cos x2, other arithmetic, cos_sin_of_phase(): return (jnp.cos(angle), jnp.sin(angle))  8.81 us
    all_to_all x1, starting transfers between devices, body(): moved = lax.all_to_all(sendbuf, ('blk', 'grp'), 0, 0, tiled=True)  8.06 us
  transfers between devices with their start and end apart: 10, of which 8 were waited for; matrix products, arithmetic and copies ran while one was open for 12% of the time, Pallas kernels for 9%

profile of v7, /device:TPU:0, one launch (start us, length us, event | category | flops | bytes accessed | tf_op | source)
XLA Modules:
  0.0 180.4 jit_solution(9332966126888636742)
XLA Ops:
  0.8 3.0 %convolution_convert_fusion = bf16[8192,16]{0,1:T(8,128)(2,1)S(1)} fusion(bf16[256,16]{0,1:T(8,128)(2,1)} %param.6, bf16[256,8192]{1,0:T(8,128)(2,1)} %sky_ref.1, pred[8192]{0:T(1024)(128)(4,1)S(1)} %bitcast.34), kind=kOutput, calls=%fused_computation | convolution fusion | flops 69337088 | bytes 4472832 | tf_op jit(solution)/shard_map/dot_general | solution.py:226
  7.3 1.7 collective-permute-start.1
  9.0 7.0 %fusion.34 = (f32[4,16,1024]{2,1,0:T(8,128)S(1)}, f32[4,16,1024]{2,1,0:T(8,128)S(1)}, f32[4,16,1024]{2,1,0:T(8,128)S(1)}, f32[4,16,1024]{2,1,0:T(8,128)S(1)}) fusion(f32[4]{0:T(128)S(1)} %get-tuple-element.16, pred[4]{0:T(512)(128)(4,1)S(1)} %broadcast_compare_fusion, s32[4]{0:T(128)S(1)} %get-tuple-element.15, s32[16,1024]{1,0:T(8,128)S(1)} %iota_multiply_fusion, ...), kind=kLoop, calls=%fused_computation.50 | loop fusion | flops 1376256 | bytes 1114404 | tf_op jit(solution)/shard_map/cos | solution.py:16
  16.0 2.8 %collective-permute-start.2 = (f32[16,272]{0,1:T(8,128)S(1)}, f32[16,272]{0,1:T(8,128)S(1)}, u32[]{:S(2)}, u32[]{:S(2)}) collective-permute-start(f32[16,272]{0,1:T(8,128)S(1)} %add.173), channel_id=1, source_target_pairs={{0,16},{4,20},{8,24},{12,28},{16,0},{20,4},{24,8},{28,12},{32,48},... | collective-permute-start | bytes 52232 | tf_op jit(solution)/shard_map/ppermute | solution.py:209
  18.8 4.2 %collective-permute-done.2 = f32[16,272]{0,1:T(8,128)S(1)} collective-permute-done((f32[16,272]{0,1:T(8,128)S(1)}, f32[16,272]{0,1:T(8,128)S(1)}, u32[]{:S(2)}, u32[]{:S(2)}) %collective-permute-start.2) | collective-permute-done | bytes 17440 | tf_op jit(solution)/shard_map/ppermute | solution.py:209
  23.0 1.7 collective-permute-start.3
  24.9 3.3 %collective-permute-done.3 = f32[16,272]{0,1:T(8,128)S(1)} collective-permute-done((f32[16,272]{0,1:T(8,128)S(1)}, f32[16,272]{0,1:T(8,128)S(1)}, u32[]{:S(2)}, u32[]{:S(2)}) %collective-permute-start.3) | collective-permute-done | bytes 17440 | tf_op jit(solution)/shard_map/ppermute | solution.py:209
  28.2 3.4 %collective-permute-start.4 = (f32[16,272]{0,1:T(8,128)S(1)}, f32[16,272]{0,1:T(8,128)S(1)}, u32[]{:S(2)}, u32[]{:S(2)}) collective-permute-start(f32[16,272]{0,1:T(8,128)S(1)} %add.175), channel_id=1, source_target_pairs={{0,64},{4,68},{8,72},{12,76},{16,80},{20,84},{24,88},{28,92},{32,9... | collective-permute-start | bytes 52232 | tf_op jit(solution)/shard_map/ppermute | solution.py:209
  31.7 1.8 %fusion.38 = (f32[4,8,1024]{2,1,0:T(8,128)S(1)}, f32[4,8,1024]{2,1,0:T(8,128)S(1)}) fusion(f32[4]{0:T(128)S(1)} %get-tuple-element.16, pred[4]{0:T(512)(128)(4,1)S(1)} %broadcast_compare_fusion, s32[4]{0:T(128)S(1)} %get-tuple-element.15, s32[4,8]{1,0:T(4,128)S(1)} %remainder_select_fusion.1), kind=kLoop, calls=%fused_computation.55 | loop fusion | flops 360448 | bytes 262308 | tf_op jit(solution)/shard_map/cos | solution.py:16
  35.0 2.0 %collective-permute-start.5 = (f32[16,272]{0,1:T(8,128)S(1)}, f32[16,272]{0,1:T(8,128)S(1)}, u32[]{:S(2)}, u32[]{:S(2)}) collective-permute-start(f32[16,272]{0,1:T(8,128)S(1)} %add.176), channel_id=1, source_target_pairs={{0,1},{1,0},{2,3},{3,2},{4,5},{5,4},{6,7},{7,6},{8,9},{9,8},{10,11... | collective-permute-start | bytes 52232 | tf_op jit(solution)/shard_map/ppermute | solution.py:209
  37.7 2.5 %collective-permute-done.5 = f32[16,272]{0,1:T(8,128)S(1)} collective-permute-done((f32[16,272]{0,1:T(8,128)S(1)}, f32[16,272]{0,1:T(8,128)S(1)}, u32[]{:S(2)}, u32[]{:S(2)}) %collective-permute-start.5) | collective-permute-done | bytes 17440 | tf_op jit(solution)/shard_map/ppermute | solution.py:209
  40.2 5.3 %collective-permute-start.6 = (f32[16,272]{0,1:T(8,128)S(1)}, f32[16,272]{0,1:T(8,128)S(1)}, u32[]{:S(2)}, u32[]{:S(2)}) collective-permute-start(f32[16,272]{0,1:T(8,128)S(1)} %add.177), channel_id=1, source_target_pairs={{0,2},{1,3},{2,0},{3,1},{4,6},{5,7},{6,4},{7,5},{8,10},{9,11},{10,... | collective-permute-start | bytes 52232 | tf_op jit(solution)/shard_map/ppermute | solution.py:209
  45.7 16.2 %shard_map.55.tab_ref = bf16[4,2048,2048]{2,1,0:T(8,128)(2,1)} custom-call(f32[4,16,1024]{2,1,0:T(8,128)S(1)} %get-tuple-element.13.ca_ref, f32[4,16,1024]{2,1,0:T(8,128)S(1)} %get-tuple-element.14.sa_ref, f32[4,128,1024]{2,1,0:T(8,128)S(1)} %bitcast.31, f32[4,128,1024]{2,1,0:T(8,128)S(1)} %bitcast.30, f32[4,1,128]{2,1,0:T(1,128)S(1)} %broadcast_in_dim.26.inv_ref, ...), custom_call_target="tpu_custom_call" | custom-call | tf_op jit(solution)/shard_map/pallas_call | solution.py:67
  66.7 19.8 %shard_map.56 = bf16[128,4,8,512]{3,2,1,0:T(8,128)(2,1)S(1)} custom-call(s32[4,1,128]{2,1,0:T(1,128)S(1)} %broadcast_in_dim.23.len_ref, bf16[256,8192]{1,0:T(8,128)(2,1)} %sky_ref.1, f32[256,16]{1,0:T(8,128)S(1)} %fusion.27.proj_ref, f32[16,8192]{1,0:T(8,128)S(1)} %fusion.41.basis_ref, bf16[4,2048,2048]{2,1,0:T(8,128)(2,1)} %shard_map.55.tab_ref), custom_call_target="tpu_custom_call" | custom-call | tf_op jit(solution)/shard_map/pallas_call | solution.py:122
  86.6 2.0 %copy-done.2 = bf16[128,4,8,512]{3,2,1,0:T(8,128)(2,1)} copy-done((bf16[128,4,8,512]{3,2,1,0:T(8,128)(2,1)}, bf16[128,4,8,512]{3,2,1,0:T(8,128)(2,1)S(1)}, u32[]{:S(2)}) %copy-start.2) | copy-done | bytes 4194328
  88.6 8.1 %all-to-all-start = ((bf16[128,4,8,512]{3,2,1,0:T(8,128)(2,1)}), bf16[128,4,8,512]{3,2,1,0:T(8,128)(2,1)}, u32[]{:S(2)}, u32[]{:S(2)}) async-start(bf16[128,4,8,512]{3,2,1,0:T(8,128)(2,1)} %copy-done.2), calls=%async_computation | async-start | bytes 8388608 | tf_op jit(solution)/shard_map/all_to_all | solution.py:243
  96.9 2.7 %copy.21.prof_ref = f32[8,1024,1]{2,1,0:T(8,128)} copy(f32[8,1024,1]{1,0,2:T(8,128)S(1)} %convolution_bitcast_fusion) | data formatting | bytes 65536 | tf_op jit(solution)/shard_map/broadcast_in_dim | solution.py:253
  99.6 8.0 %fusion.6.theta_ref = bf16[1024,512]{1,0:T(8,128)(2,1)S(1)} fusion(f32[512]{0:T(512)S(1)} %sine_multiply_fusion, s32[512]{0:T(512)S(1)} %multiply_add_fusion.1), kind=kLoop, calls=%fused_computation.11 | loop fusion | flops 8388608 | bytes 1052672 | tf_op jit(solution)/shard_map/convert_element_type | solution.py:179
  107.6 40.2 %all-to-all-done = bf16[128,4,8,512]{3,2,1,0:T(8,128)(2,1)} async-done(((bf16[128,4,8,512]{3,2,1,0:T(8,128)(2,1)}), bf16[128,4,8,512]{3,2,1,0:T(8,128)(2,1)}, u32[]{:S(2)}, u32[]{:S(2)}) %all-to-all-start) | async-done | bytes 4194336 | tf_op jit(solution)/shard_map/all_to_all | solution.py:243
  147.8 4.6 %copy.24 = bf16[64,8,8,512]{3,1,2,0:T(8,128)(2,1)S(1)} copy(bf16[64,8,8,512]{3,2,1,0:T(8,128)(2,1)} %bitcast.10) | data formatting | bytes 8388608
  152.4 7.8 %shard_map.57 = f32[8,1,128]{2,1,0:T(1,128)S(1)} custom-call(bf16[1024,512]{1,0:T(8,128)(2,1)S(1)} %fusion.6.theta_ref, bf16[512,4096]{1,0:T(8,128)(2,1)S(1)} %bitcast.28, f32[8,1024,1]{2,1,0:T(8,128)S(1)} %copy-done.1, f32[1,512]{1,0:T(1,128)S(1)} %bitcast.32), custom_call_target="tpu_custom_call" | custom-call | tf_op jit(solution)/shard_map/pallas_call | solution.py:257
  161.3 2.7 %collective-permute-done.7 = f32[8]{0:T(128)S(1)} collective-permute-done((f32[8]{0:T(128)S(1)}, f32[8]{0:T(128)S(1)}, u32[]{:S(2)}, u32[]{:S(2)}) %collective-permute-start.7) | collective-permute-done | bytes 64 | tf_op jit(solution)/shard_map/ppermute | solution.py:209
  165.4 3.7 %collective-permute-done.8 = f32[8]{0:T(128)S(1)} collective-permute-done((f32[8]{0:T(128)S(1)}, f32[8]{0:T(128)S(1)}, u32[]{:S(2)}, u32[]{:S(2)}) %collective-permute-start.8) | collective-permute-done | bytes 64 | tf_op jit(solution)/shard_map/ppermute | solution.py:209
  169.2 11.2 %shard_map.58 = f32[1024,8,2,256]{3,2,1,0:T(2,128)} custom-call(bf16[1024,512]{1,0:T(8,128)(2,1)S(1)} %fusion.6.theta_ref, bf16[512,4096]{1,0:T(8,128)(2,1)S(1)} %bitcast.29, f32[8,1024,1]{2,1,0:T(8,128)S(1)} %copy-done.1, f32[1,512]{1,0:T(1,128)S(1)} %bitcast.33, f32[8,1,128]{2,1,0:T(1,128)S(1)} %broadcast_in_dim.30.scale_ref), custom_call_target="tpu_custom_call" | custom-call | tf_op jit(solution)/shard_map/pallas_call | solution.py:268
  (62 shorter events, 14.3 us)
Async XLA Ops:
  0.0 96.6 %copy-start = (f32[8,1024]{1,0:T(8,128)S(1)}, f32[8,1024]{1,0:T(8,128)}, u32[]{:S(2)}) copy-start(f32[8,1024]{1,0:T(8,128)} %param.8) | copy-start | bytes 98308
  0.8 3.5 %copy-start.3 = (bf16[256,8192]{1,0:T(8,128)(2,1)S(1)}, bf16[256,8192]{1,0:T(8,128)(2,1)}, u32[]{:S(2)}) copy-start(bf16[256,8192]{1,0:T(8,128)(2,1)} %sky_ref.1) | copy-start | bytes 12582916
  4.2 1.7 copy-start.4
  5.8 1.4 collective-permute-start
  7.3 8.7 %collective-permute-start.1 = (f32[16,272]{0,1:T(8,128)S(1)}, f32[16,272]{0,1:T(8,128)S(1)}, u32[]{:S(2)}, u32[]{:S(2)}) collective-permute-start(f32[16,272]{0,1:T(8,128)S(1)} %add.172), channel_id=1, source_target_pairs={{0,8},{4,12},{8,0},{12,4},{16,24},{20,28},{24,16},{28,20},{32,40},... | collective-permute-start | bytes 52232 | tf_op jit(solution)/shard_map/ppermute | solution.py:209
  16.0 7.0 %collective-permute-start.2 = (f32[16,272]{0,1:T(8,128)S(1)}, f32[16,272]{0,1:T(8,128)S(1)}, u32[]{:S(2)}, u32[]{:S(2)}) collective-permute-start(f32[16,272]{0,1:T(8,128)S(1)} %add.173), channel_id=1, source_target_pairs={{0,16},{4,20},{8,24},{12,28},{16,0},{20,4},{24,8},{28,12},{32,48},... | collective-permute-start | bytes 52232 | tf_op jit(solution)/shard_map/ppermute | solution.py:209
  23.0 5.1 %collective-permute-start.3 = (f32[16,272]{0,1:T(8,128)S(1)}, f32[16,272]{0,1:T(8,128)S(1)}, u32[]{:S(2)}, u32[]{:S(2)}) collective-permute-start(f32[16,272]{0,1:T(8,128)S(1)} %add.174), channel_id=1, source_target_pairs={{0,32},{4,36},{8,40},{12,44},{16,48},{20,52},{24,56},{28,60},{32,0... | collective-permute-start | bytes 52232 | tf_op jit(solution)/shard_map/ppermute | solution.py:209
  28.2 6.8 %collective-permute-start.4 = (f32[16,272]{0,1:T(8,128)S(1)}, f32[16,272]{0,1:T(8,128)S(1)}, u32[]{:S(2)}, u32[]{:S(2)}) collective-permute-start(f32[16,272]{0,1:T(8,128)S(1)} %add.175), channel_id=1, source_target_pairs={{0,64},{4,68},{8,72},{12,76},{16,80},{20,84},{24,88},{28,92},{32,9... | collective-permute-start | bytes 52232 | tf_op jit(solution)/shard_map/ppermute | solution.py:209
  35.0 5.1 %collective-permute-start.5 = (f32[16,272]{0,1:T(8,128)S(1)}, f32[16,272]{0,1:T(8,128)S(1)}, u32[]{:S(2)}, u32[]{:S(2)}) collective-permute-start(f32[16,272]{0,1:T(8,128)S(1)} %add.176), channel_id=1, source_target_pairs={{0,1},{1,0},{2,3},{3,2},{4,5},{5,4},{6,7},{7,6},{8,9},{9,8},{10,11... | collective-permute-start | bytes 52232 | tf_op jit(solution)/shard_map/ppermute | solution.py:209
  40.2 21.7 %collective-permute-start.6 = (f32[16,272]{0,1:T(8,128)S(1)}, f32[16,272]{0,1:T(8,128)S(1)}, u32[]{:S(2)}, u32[]{:S(2)}) collective-permute-start(f32[16,272]{0,1:T(8,128)S(1)} %add.177), channel_id=1, source_target_pairs={{0,2},{1,3},{2,0},{3,1},{4,6},{5,7},{6,4},{7,5},{8,10},{9,11},{10,... | collective-permute-start | bytes 52232 | tf_op jit(solution)/shard_map/ppermute | solution.py:209
  86.6 2.0 %copy-start.2 = (bf16[128,4,8,512]{3,2,1,0:T(8,128)(2,1)}, bf16[128,4,8,512]{3,2,1,0:T(8,128)(2,1)S(1)}, u32[]{:S(2)}) copy-start(bf16[128,4,8,512]{3,2,1,0:T(8,128)(2,1)S(1)} %shard_map.56) | copy-start | bytes 12582916
  88.6 8.1 %copy-start.5 = (s32[8]{0:T(128)S(1)}, s32[8]{0:T(128)}, u32[]{:S(2)}) copy-start(s32[8]{0:T(128)} %param.9) | copy-start | bytes 100
  88.6 59.2 %all-to-all-start = ((bf16[128,4,8,512]{3,2,1,0:T(8,128)(2,1)}), bf16[128,4,8,512]{3,2,1,0:T(8,128)(2,1)}, u32[]{:S(2)}, u32[]{:S(2)}) async-start(bf16[128,4,8,512]{3,2,1,0:T(8,128)(2,1)} %copy-done.2), calls=%async_computation | async-start | bytes 8388608 | tf_op jit(solution)/shard_map/all_to_all | solution.py:243
  147.8 4.6 %copy-start.1 = (f32[8,1024,1]{2,1,0:T(8,128)S(1)}, f32[8,1024,1]{2,1,0:T(8,128)}, u32[]{:S(2)}) copy-start(f32[8,1024,1]{2,1,0:T(8,128)} %copy.21.prof_ref) | copy-start | bytes 98308
  160.4 3.6 %collective-permute-start.7 = (f32[8]{0:T(128)S(1)}, f32[8]{0:T(128)S(1)}, u32[]{:S(2)}, u32[]{:S(2)}) collective-permute-start(f32[8]{0:T(128)S(1)} %slice_reduce_fusion), channel_id=1, source_target_pairs={{0,1},{1,0},{2,3},{3,2},{4,5},{5,4},{6,7},{7,6},{8,9},{9,8},{10,11... | collective-permute-start | bytes 104 | tf_op jit(solution)/shard_map/ppermute | solution.py:209
  164.1 5.1 %collective-permute-start.8 = (f32[8]{0:T(128)S(1)}, f32[8]{0:T(128)S(1)}, u32[]{:S(2)}, u32[]{:S(2)}) collective-permute-start(f32[8]{0:T(128)S(1)} %add.192), channel_id=1, source_target_pairs={{0,2},{1,3},{2,0},{3,1},{4,6},{5,7},{6,4},{7,5},{8,10},{9,11},{10,... | collective-permute-start | bytes 104 | tf_op jit(solution)/shard_map/ppermute | solution.py:209

commit v8 on v4

--- a/solution.py
+++ b/solution.py
@@ -43,16 +43,19 @@
     length = len_ref[0][:, 0:1]
 
     def build(t, carry):
-        ca = ca_ref[0, pl.ds(t, 1), :]
-        sa = sa_ref[0, pl.ds(t, 1), :]
+        ca = ca_ref[0, pl.ds(t, 1), :] * inv
+        sa = sa_ref[0, pl.ds(t, 1), :] * inv
         cb = cb_ref[0]
         sb = sb_ref[0]
         rows = t * J_LO + lax.broadcasted_iota(jnp.int32, (J_LO, 1), 0)
-        weight = jnp.where(rows < length, inv, 0.0)
-        cos_t, sin_t = add_angles(ca, sa, cb, sb)
+        keep = rows < length
+        cos_t = ca * cb - sa * sb
+        neg_sin_t = (-sa) * cb - ca * sb
         r0 = pl.multiple_of(t * J_LO, J_LO)
-        tab_ref[0, pl.ds(r0, J_LO), 0:m_width] = (cos_t * weight).astype(jnp.bfloat16)
-        tab_ref[0, pl.ds(r0, J_LO), m_width : 2 * m_width] = (-sin_t * weight).astype(jnp.bfloat16)
+        tab_ref[0, pl.ds(r0, J_LO), 0:m_width] = jnp.where(keep, cos_t, 0.0).astype(jnp.bfloat16)
+        tab_ref[0, pl.ds(r0, J_LO), m_width : 2 * m_width] = jnp.where(keep, neg_sin_t, 0.0).astype(
+            jnp.bfloat16
+        )
         return carry
 
     lax.fori_loop(0, RPIX // J_LO, build, 0)

time: 175 us -> 177 us (1.011)
  Pallas kernels: 55.1 us -> 57.4 us
    pallas_call x1, Pallas kernels: 16.2 us -> 18.5 us  [cycle_tables(): pl.pallas_call(table_kernel, grid=(n_cyc,), in_specs=[pl.BlockSpec((1, n_...]
  transfers between devices with their start and end apart: 14 -> 14, of which waited for: 7 -> 7; matrix products, arithmetic and copies ran while one was open for 12% -> 12% of each run, Pallas kernels for 9% -> 10%
where the time goes in v8:
time: 177 us
  Pallas kernels  57.4 us (32%)
  waiting for transfers between devices  51.4 us (29%)
  starting transfers between devices  29.6 us (17%)
  other arithmetic  22.9 us (13%)
  local copies, waits for them, and re-layouts  10.3 us (6%)
  matrix products  5.29 us (3%)
    all_to_all x1, waiting for transfers between devices, body(): moved = lax.all_to_all(sendbuf, ('blk', 'grp'), 0, 0, tiled=True)  40.2 us
    ppermute x13, starting transfers between devices, ring_sum(): lax.ppermute(v, axis, shift_perm(size, stride, total, k))  22.1 us
    pallas_call x1, Pallas kernels, cycle_fourier(): pl.pallas_call(fourier_kernel, grid=(n_cyc,), in_specs=[pl.BlockSpec((1,...  19.8 us
    pallas_call x1, Pallas kernels, cycle_tables(): pl.pallas_call(table_kernel, grid=(n_cyc,), in_specs=[pl.BlockSpec((1, n_...  18.5 us
    ppermute x13, waiting for transfers between devices, ring_sum(): lax.ppermute(v, axis, shift_perm(size, stride, total, k))  11.2 us
    pallas_call x1, Pallas kernels, body(): pl.pallas_call(output_kernel, grid=(chan_dev,), in_specs=specs + [pl.Bloc...  11.2 us
    cos x2, other arithmetic, cos_sin_of_phase(): return (jnp.cos(angle), jnp.sin(angle))  8.81 us
    convert_element_type x1, other arithmetic, theta_table(): return (jnp.cos(angle) * weight[None, :]).astype(jnp.bfloat16)  7.96 us
  transfers between devices with their start and end apart: 14, of which 7 were waited for; matrix products, arithmetic and copies ran while one was open for 12% of the time, Pallas kernels for 10%

profile of v8, /device:TPU:0, one launch (start us, length us, event | category | flops | bytes accessed | tf_op | source)
XLA Modules:
  0.0 177.2 jit_solution(6004934190312170672)
XLA Ops:
  0.8 3.0 %convolution_convert_fusion = bf16[8192,16]{0,1:T(8,128)(2,1)S(1)} fusion(bf16[256,16]{0,1:T(8,128)(2,1)} %param.6, bf16[256,8192]{1,0:T(8,128)(2,1)} %sky_ref.1, pred[8192]{0:T(1024)(128)(4,1)S(1)} %bitcast.34), kind=kOutput, calls=%fused_computation | convolution fusion | flops 69337088 | bytes 4472832 | tf_op jit(solution)/shard_map/dot_general | solution.py:222
  6.3 7.0 %fusion.34 = (f32[4,16,1024]{2,1,0:T(8,128)S(1)}, f32[4,16,1024]{2,1,0:T(8,128)S(1)}, f32[4,16,1024]{2,1,0:T(8,128)S(1)}, f32[4,16,1024]{2,1,0:T(8,128)S(1)}) fusion(f32[4]{0:T(128)S(1)} %get-tuple-element.16, pred[4]{0:T(512)(128)(4,1)S(1)} %broadcast_compare_fusion, s32[4]{0:T(128)S(1)} %get-tuple-element.15, s32[16,1024]{1,0:T(8,128)S(1)} %iota_multiply_fusion, ...), kind=kLoop, calls=%fused_computation.53 | loop fusion | flops 1376256 | bytes 1114404 | tf_op jit(solution)/shard_map/cos | solution.py:16
  13.5 1.7 collective-permute-start.1
  15.2 2.7 %collective-permute-start.2 = (f32[16,272]{0,1:T(8,128)S(1)}, f32[16,272]{0,1:T(8,128)S(1)}, u32[]{:S(2)}, u32[]{:S(2)}) collective-permute-start(f32[16,272]{0,1:T(8,128)S(1)} %add.184), channel_id=1, source_target_pairs={{0,16},{4,20},{8,24},{12,28},{16,0},{20,4},{24,8},{28,12},{32,48},... | collective-permute-start | bytes 52232 | tf_op jit(solution)/shard_map/ppermute | solution.py:204
  17.9 1.4 collective-permute-start.3
  19.3 1.8 %fusion.38 = (f32[4,8,1024]{2,1,0:T(8,128)S(1)}, f32[4,8,1024]{2,1,0:T(8,128)S(1)}) fusion(f32[4]{0:T(128)S(1)} %get-tuple-element.16, pred[4]{0:T(512)(128)(4,1)S(1)} %broadcast_compare_fusion, s32[4]{0:T(128)S(1)} %get-tuple-element.15, s32[4,8]{1,0:T(4,128)S(1)} %remainder_select_fusion.1), kind=kLoop, calls=%fused_computation.58 | loop fusion | flops 360448 | bytes 262308 | tf_op jit(solution)/shard_map/cos | solution.py:16
  21.2 3.7 %collective-permute-done.2 = f32[16,272]{0,1:T(8,128)S(1)} collective-permute-done((f32[16,272]{0,1:T(8,128)S(1)}, f32[16,272]{0,1:T(8,128)S(1)}, u32[]{:S(2)}, u32[]{:S(2)}) %collective-permute-start.2) | collective-permute-done | bytes 17440 | tf_op jit(solution)/shard_map/ppermute | solution.py:204
  24.9 1.6 collective-permute-start.4
  26.6 2.9 %collective-permute-start.5 = (f32[16,272]{0,1:T(8,128)S(1)}, f32[16,272]{0,1:T(8,128)S(1)}, u32[]{:S(2)}, u32[]{:S(2)}) collective-permute-start(f32[16,272]{0,1:T(8,128)S(1)} %add_add_fusion.2), channel_id=1, source_target_pairs={{0,64},{4,68},{8,72},{12,76},{16,80},{20,84},{24,88},{28,92},{32,9... | collective-permute-start | bytes 52232 | tf_op jit(solution)/shard_map/ppermute | solution.py:204
  31.6 4.0 %collective-permute-done.5 = f32[16,272]{0,1:T(8,128)S(1)} collective-permute-done((f32[16,272]{0,1:T(8,128)S(1)}, f32[16,272]{0,1:T(8,128)S(1)}, u32[]{:S(2)}, u32[]{:S(2)}) %collective-permute-start.5) | collective-permute-done | bytes 17440 | tf_op jit(solution)/shard_map/ppermute | solution.py:204
  35.7 2.0 %collective-permute-start.7 = (f32[16,272]{0,1:T(8,128)S(1)}, f32[16,272]{0,1:T(8,128)S(1)}, u32[]{:S(2)}, u32[]{:S(2)}) collective-permute-start(f32[16,272]{0,1:T(8,128)S(1)} %add_add_fusion.1), channel_id=1, source_target_pairs={{0,1},{1,2},{2,3},{3,0},{4,5},{5,6},{6,7},{7,4},{8,9},{9,10},{10,1... | collective-permute-start | bytes 52232 | tf_op jit(solution)/shard_map/ppermute | solution.py:204
  37.7 3.6 %collective-permute-start.8 = (f32[16,272]{0,1:T(8,128)S(1)}, f32[16,272]{0,1:T(8,128)S(1)}, u32[]{:S(2)}, u32[]{:S(2)}) collective-permute-start(f32[16,272]{0,1:T(8,128)S(1)} %add_add_fusion.1), channel_id=1, source_target_pairs={{0,2},{1,3},{2,0},{3,1},{4,6},{5,7},{6,4},{7,5},{8,10},{9,11},{10,... | collective-permute-start | bytes 52232 | tf_op jit(solution)/shard_map/ppermute | solution.py:204
  42.4 18.5 %shard_map.55.tab_ref = bf16[4,2048,2048]{2,1,0:T(8,128)(2,1)} custom-call(f32[4,16,1024]{2,1,0:T(8,128)S(1)} %get-tuple-element.13.ca_ref, f32[4,16,1024]{2,1,0:T(8,128)S(1)} %get-tuple-element.14.sa_ref, f32[4,128,1024]{2,1,0:T(8,128)S(1)} %bitcast.31, f32[4,128,1024]{2,1,0:T(8,128)S(1)} %bitcast.30, f32[4,1,128]{2,1,0:T(1,128)S(1)} %broadcast_in_dim.26.inv_ref, ...), custom_call_target="tpu_custom_call" | custom-call | tf_op jit(solution)/shard_map/pallas_call | solution.py:70
  61.1 1.5 cholesky.16
  65.8 19.8 %shard_map.56 = bf16[128,4,8,512]{3,2,1,0:T(8,128)(2,1)S(1)} custom-call(s32[4,1,128]{2,1,0:T(1,128)S(1)} %broadcast_in_dim.23.len_ref, bf16[256,8192]{1,0:T(8,128)(2,1)} %sky_ref.1, f32[256,16]{1,0:T(8,128)S(1)} %fusion.27.proj_ref, f32[16,8192]{1,0:T(8,128)S(1)} %fusion.41.basis_ref, bf16[4,2048,2048]{2,1,0:T(8,128)(2,1)} %shard_map.55.tab_ref), custom_call_target="tpu_custom_call" | custom-call | tf_op jit(solution)/shard_map/pallas_call | solution.py:125
  85.6 2.0 %copy-done.2 = bf16[128,4,8,512]{3,2,1,0:T(8,128)(2,1)} copy-done((bf16[128,4,8,512]{3,2,1,0:T(8,128)(2,1)}, bf16[128,4,8,512]{3,2,1,0:T(8,128)(2,1)S(1)}, u32[]{:S(2)}) %copy-start.2) | copy-done | bytes 4194328
  87.6 7.5 %all-to-all-start = ((bf16[128,4,8,512]{3,2,1,0:T(8,128)(2,1)}), bf16[128,4,8,512]{3,2,1,0:T(8,128)(2,1)}, u32[]{:S(2)}, u32[]{:S(2)}) async-start(bf16[128,4,8,512]{3,2,1,0:T(8,128)(2,1)} %copy-done.2), calls=%async_computation | async-start | bytes 8388608 | tf_op jit(solution)/shard_map/all_to_all | solution.py:239
  95.4 2.7 %copy.21.prof_ref = f32[8,1024,1]{2,1,0:T(8,128)} copy(f32[8,1024,1]{1,0,2:T(8,128)S(1)} %convolution_bitcast_fusion) | data formatting | bytes 65536 | tf_op jit(solution)/shard_map/broadcast_in_dim | solution.py:249
  98.2 8.0 %fusion.6.theta_ref = bf16[1024,512]{1,0:T(8,128)(2,1)S(1)} fusion(f32[512]{0:T(512)S(1)} %sine_multiply_fusion, s32[512]{0:T(512)S(1)} %multiply_add_fusion.1), kind=kLoop, calls=%fused_computation.11 | loop fusion | flops 8388608 | bytes 1052672 | tf_op jit(solution)/shard_map/convert_element_type | solution.py:182
  106.1 40.2 %all-to-all-done = bf16[128,4,8,512]{3,2,1,0:T(8,128)(2,1)} async-done(((bf16[128,4,8,512]{3,2,1,0:T(8,128)(2,1)}), bf16[128,4,8,512]{3,2,1,0:T(8,128)(2,1)}, u32[]{:S(2)}, u32[]{:S(2)}) %all-to-all-start) | async-done | bytes 4194336 | tf_op jit(solution)/shard_map/all_to_all | solution.py:239
  146.4 4.6 %copy.24 = bf16[64,8,8,512]{3,1,2,0:T(8,128)(2,1)S(1)} copy(bf16[64,8,8,512]{3,2,1,0:T(8,128)(2,1)} %bitcast.10) | data formatting | bytes 8388608
  151.0 7.8 %shard_map.57 = f32[8,1,128]{2,1,0:T(1,128)S(1)} custom-call(bf16[1024,512]{1,0:T(8,128)(2,1)S(1)} %fusion.6.theta_ref, bf16[512,4096]{1,0:T(8,128)(2,1)S(1)} %bitcast.28, f32[8,1024,1]{2,1,0:T(8,128)S(1)} %copy-done.1, f32[1,512]{1,0:T(1,128)S(1)} %bitcast.32), custom_call_target="tpu_custom_call" | custom-call | tf_op jit(solution)/shard_map/pallas_call | solution.py:253
  159.8 2.5 %collective-permute-start.11 = (f32[8]{0:T(128)S(1)}, f32[8]{0:T(128)S(1)}, u32[]{:S(2)}, u32[]{:S(2)}) collective-permute-start(f32[8]{0:T(128)S(1)} %slice_reduce_fusion), channel_id=1, source_target_pairs={{0,2},{1,3},{2,0},{3,1},{4,6},{5,7},{6,4},{7,5},{8,10},{9,11},{10,... | collective-permute-start | bytes 104 | tf_op jit(solution)/shard_map/ppermute | solution.py:204
  166.0 11.2 %shard_map.58 = f32[1024,8,2,256]{3,2,1,0:T(2,128)} custom-call(bf16[1024,512]{1,0:T(8,128)(2,1)S(1)} %fusion.6.theta_ref, bf16[512,4096]{1,0:T(8,128)(2,1)S(1)} %bitcast.29, f32[8,1024,1]{2,1,0:T(8,128)S(1)} %copy-done.1, f32[1,512]{1,0:T(1,128)S(1)} %bitcast.33, f32[8,1,128]{2,1,0:T(1,128)S(1)} %broadcast_in_dim.30.scale_ref), custom_call_target="tpu_custom_call" | custom-call | tf_op jit(solution)/shard_map/pallas_call | solution.py:264
  (66 shorter events, 15.1 us)
Async XLA Ops:
  0.0 95.2 %copy-start = (f32[8,1024]{1,0:T(8,128)S(1)}, f32[8,1024]{1,0:T(8,128)}, u32[]{:S(2)}) copy-start(f32[8,1024]{1,0:T(8,128)} %param.8) | copy-start | bytes 98308
  0.8 3.5 %copy-start.3 = (bf16[256,8192]{1,0:T(8,128)(2,1)S(1)}, bf16[256,8192]{1,0:T(8,128)(2,1)}, u32[]{:S(2)}) copy-start(bf16[256,8192]{1,0:T(8,128)(2,1)} %sky_ref.1) | copy-start | bytes 12582916
  4.2 1.7 copy-start.4
  5.8 7.6 %collective-permute-start = (f32[16,272]{0,1:T(8,128)S(1)}, f32[16,272]{0,1:T(8,128)S(1)}, u32[]{:S(2)}, u32[]{:S(2)}) collective-permute-start(f32[16,272]{0,1:T(8,128)S(1)} %copy.17), channel_id=1, source_target_pairs={{0,4},{4,0},{8,12},{12,8},{16,20},{20,16},{24,28},{28,24},{32,36},... | collective-permute-start | bytes 52232 | tf_op jit(solution)/shard_map/ppermute | solution.py:204
  13.5 7.7 %collective-permute-start.1 = (f32[16,272]{0,1:T(8,128)S(1)}, f32[16,272]{0,1:T(8,128)S(1)}, u32[]{:S(2)}, u32[]{:S(2)}) collective-permute-start(f32[16,272]{0,1:T(8,128)S(1)} %add.184), channel_id=1, source_target_pairs={{0,8},{4,12},{8,16},{12,20},{16,24},{20,28},{24,0},{28,4},{32,40},... | collective-permute-start | bytes 52232 | tf_op jit(solution)/shard_map/ppermute | solution.py:204
  15.2 9.7 %collective-permute-start.2 = (f32[16,272]{0,1:T(8,128)S(1)}, f32[16,272]{0,1:T(8,128)S(1)}, u32[]{:S(2)}, u32[]{:S(2)}) collective-permute-start(f32[16,272]{0,1:T(8,128)S(1)} %add.184), channel_id=1, source_target_pairs={{0,16},{4,20},{8,24},{12,28},{16,0},{20,4},{24,8},{28,12},{32,48},... | collective-permute-start | bytes 52232 | tf_op jit(solution)/shard_map/ppermute | solution.py:204
  17.9 7.0 %collective-permute-start.3 = (f32[16,272]{0,1:T(8,128)S(1)}, f32[16,272]{0,1:T(8,128)S(1)}, u32[]{:S(2)}, u32[]{:S(2)}) collective-permute-start(f32[16,272]{0,1:T(8,128)S(1)} %add.184), channel_id=1, source_target_pairs={{0,24},{4,28},{8,0},{12,4},{16,8},{20,12},{24,16},{28,20},{32,56},... | collective-permute-start | bytes 52232 | tf_op jit(solution)/shard_map/ppermute | solution.py:204
  24.9 6.7 %collective-permute-start.4 = (f32[16,272]{0,1:T(8,128)S(1)}, f32[16,272]{0,1:T(8,128)S(1)}, u32[]{:S(2)}, u32[]{:S(2)}) collective-permute-start(f32[16,272]{0,1:T(8,128)S(1)} %add_add_fusion.2), channel_id=1, source_target_pairs={{0,32},{4,36},{8,40},{12,44},{16,48},{20,52},{24,56},{28,60},{32,6... | collective-permute-start | bytes 52232 | tf_op jit(solution)/shard_map/ppermute | solution.py:204
  26.6 9.1 %collective-permute-start.5 = (f32[16,272]{0,1:T(8,128)S(1)}, f32[16,272]{0,1:T(8,128)S(1)}, u32[]{:S(2)}, u32[]{:S(2)}) collective-permute-start(f32[16,272]{0,1:T(8,128)S(1)} %add_add_fusion.2), channel_id=1, source_target_pairs={{0,64},{4,68},{8,72},{12,76},{16,80},{20,84},{24,88},{28,92},{32,9... | collective-permute-start | bytes 52232 | tf_op jit(solution)/shard_map/ppermute | solution.py:204
  29.5 6.2 %collective-permute-start.6 = (f32[16,272]{0,1:T(8,128)S(1)}, f32[16,272]{0,1:T(8,128)S(1)}, u32[]{:S(2)}, u32[]{:S(2)}) collective-permute-start(f32[16,272]{0,1:T(8,128)S(1)} %add_add_fusion.2), channel_id=1, source_target_pairs={{0,96},{4,100},{8,104},{12,108},{16,112},{20,116},{24,120},{28,124... | collective-permute-start | bytes 52232 | tf_op jit(solution)/shard_map/ppermute | solution.py:204
  35.7 25.3 %collective-permute-start.7 = (f32[16,272]{0,1:T(8,128)S(1)}, f32[16,272]{0,1:T(8,128)S(1)}, u32[]{:S(2)}, u32[]{:S(2)}) collective-permute-start(f32[16,272]{0,1:T(8,128)S(1)} %add_add_fusion.1), channel_id=1, source_target_pairs={{0,1},{1,2},{2,3},{3,0},{4,5},{5,6},{6,7},{7,4},{8,9},{9,10},{10,1... | collective-permute-start | bytes 52232 | tf_op jit(solution)/shard_map/ppermute | solution.py:204
  37.7 23.3 %collective-permute-start.8 = (f32[16,272]{0,1:T(8,128)S(1)}, f32[16,272]{0,1:T(8,128)S(1)}, u32[]{:S(2)}, u32[]{:S(2)}) collective-permute-start(f32[16,272]{0,1:T(8,128)S(1)} %add_add_fusion.1), channel_id=1, source_target_pairs={{0,2},{1,3},{2,0},{3,1},{4,6},{5,7},{6,4},{7,5},{8,10},{9,11},{10,... | collective-permute-start | bytes 52232 | tf_op jit(solution)/shard_map/ppermute | solution.py:204
  41.2 19.7 %collective-permute-start.9 = (f32[16,272]{0,1:T(8,128)S(1)}, f32[16,272]{0,1:T(8,128)S(1)}, u32[]{:S(2)}, u32[]{:S(2)}) collective-permute-start(f32[16,272]{0,1:T(8,128)S(1)} %add_add_fusion.1), channel_id=1, source_target_pairs={{0,3},{1,0},{2,1},{3,2},{4,7},{5,4},{6,5},{7,6},{8,11},{9,8},{10,9... | collective-permute-start | bytes 52232 | tf_op jit(solution)/shard_map/ppermute | solution.py:204
  85.6 2.0 %copy-start.2 = (bf16[128,4,8,512]{3,2,1,0:T(8,128)(2,1)}, bf16[128,4,8,512]{3,2,1,0:T(8,128)(2,1)S(1)}, u32[]{:S(2)}) copy-start(bf16[128,4,8,512]{3,2,1,0:T(8,128)(2,1)S(1)} %shard_map.56) | copy-start | bytes 12582916
  87.6 7.6 %copy-start.5 = (s32[8]{0:T(128)S(1)}, s32[8]{0:T(128)}, u32[]{:S(2)}) copy-start(s32[8]{0:T(128)} %param.9) | copy-start | bytes 100
  87.6 58.7 %all-to-all-start = ((bf16[128,4,8,512]{3,2,1,0:T(8,128)(2,1)}), bf16[128,4,8,512]{3,2,1,0:T(8,128)(2,1)}, u32[]{:S(2)}, u32[]{:S(2)}) async-start(bf16[128,4,8,512]{3,2,1,0:T(8,128)(2,1)} %copy-done.2), calls=%async_computation | async-start | bytes 8388608 | tf_op jit(solution)/shard_map/all_to_all | solution.py:239
  146.4 4.6 %copy-start.1 = (f32[8,1024,1]{2,1,0:T(8,128)S(1)}, f32[8,1024,1]{2,1,0:T(8,128)}, u32[]{:S(2)}) copy-start(f32[8,1024,1]{2,1,0:T(8,128)} %copy.21.prof_ref) | copy-start | bytes 98308
  159.0 4.8 %collective-permute-start.10 = (f32[8]{0:T(128)S(1)}, f32[8]{0:T(128)S(1)}, u32[]{:S(2)}, u32[]{:S(2)}) collective-permute-start(f32[8]{0:T(128)S(1)} %slice_reduce_fusion), channel_id=1, source_target_pairs={{0,1},{1,2},{2,3},{3,0},{4,5},{5,6},{6,7},{7,4},{8,9},{9,10},{10,1... | collective-permute-start | bytes 104 | tf_op jit(solution)/shard_map/ppermute | solution.py:204
  159.8 5.1 %collective-permute-start.11 = (f32[8]{0:T(128)S(1)}, f32[8]{0:T(128)S(1)}, u32[]{:S(2)}, u32[]{:S(2)}) collective-permute-start(f32[8]{0:T(128)S(1)} %slice_reduce_fusion), channel_id=1, source_target_pairs={{0,2},{1,3},{2,0},{3,1},{4,6},{5,7},{6,4},{7,5},{8,10},{9,11},{10,... | collective-permute-start | bytes 104 | tf_op jit(solution)/shard_map/ppermute | solution.py:204
  162.4 3.6 %collective-permute-start.12 = (f32[8]{0:T(128)S(1)}, f32[8]{0:T(128)S(1)}, u32[]{:S(2)}, u32[]{:S(2)}) collective-permute-start(f32[8]{0:T(128)S(1)} %slice_reduce_fusion), channel_id=1, source_target_pairs={{0,3},{1,0},{2,1},{3,2},{4,7},{5,4},{6,5},{7,6},{8,11},{9,8},{10,9... | collective-permute-start | bytes 104 | tf_op jit(solution)/shard_map/ppermute | solution.py:204

commit v9 on v4

--- a/solution.py
+++ b/solution.py
@@ -52,7 +52,7 @@
         cos_t, sin_t = add_angles(ca, sa, cb, sb)
         r0 = pl.multiple_of(t * J_LO, J_LO)
         tab_ref[0, pl.ds(r0, J_LO), 0:m_width] = (cos_t * weight).astype(jnp.bfloat16)
-        tab_ref[0, pl.ds(r0, J_LO), m_width : 2 * m_width] = (-sin_t * weight).astype(jnp.bfloat16)
+        tab_ref[0, pl.ds(r0, J_LO), m_width : 2 * m_width] = (sin_t * -weight).astype(jnp.bfloat16)
         return carry
 
     lax.fori_loop(0, RPIX // J_LO, build, 0)
@@ -136,34 +136,42 @@
     )(lens, sky_map, projected_t, basis, tables)
 
 
-def harmonic_tile(theta_ref, mv_ref, prof_ref, mw_ref, lc):
+CH_STEP = 2
+
+
+def harmonic_tile(theta_ref, mv_ref, prof_ref, mw_ref, lc, ci):
     rows = pl.ds(lc * 256, 256)
-    h = jnp.dot(theta_ref[rows, :], mv_ref[...], preferred_element_type=jnp.float32)
-    return h * prof_ref[0, rows, :] * mw_ref[...]
+    width = mw_ref.shape[1]
+    h = jnp.dot(
+        theta_ref[rows, :], mv_ref[:, ci * width : (ci + 1) * width], preferred_element_type=jnp.float32
+    )
+    return h * prof_ref[ci, rows, :] * mw_ref[...]
 
 
 def power_kernel(theta_ref, mv_ref, prof_ref, mw_ref, o_ref):
-    total = jnp.zeros((1, 1), jnp.float32)
-    for lc in range(theta_ref.shape[0] // 256):
-        w = harmonic_tile(theta_ref, mv_ref, prof_ref, mw_ref, lc)
-        total = total + jnp.sum(w * w, keepdims=True)
-    o_ref[0] = jnp.broadcast_to(total, (1, 128))
+    for ci in range(prof_ref.shape[0]):
+        total = jnp.zeros((1, 1), jnp.float32)
+        for lc in range(theta_ref.shape[0] // 256):
+            w = harmonic_tile(theta_ref, mv_ref, prof_ref, mw_ref, lc, ci)
+            total = total + jnp.sum(w * w, keepdims=True)
+        o_ref[ci] = jnp.broadcast_to(total, (1, 128))
 
 
 def output_kernel(theta_ref, mv_ref, prof_ref, mw_ref, scale_ref, o_ref):
-    scale = scale_ref[0][:, 0:1]
-    half = mv_ref.shape[1] // 2
-    for lc in range(theta_ref.shape[0] // 256):
-        w = harmonic_tile(theta_ref, mv_ref, prof_ref, mw_ref, lc) * scale
-        for p in range(2):
-            o_ref[pl.ds(lc * 256, 256), 0, p, :] = w[:, p * half : (p + 1) * half]
+    half = mw_ref.shape[1] // 2
+    for ci in range(prof_ref.shape[0]):
+        scale = scale_ref[ci][:, 0:1]
+        for lc in range(theta_ref.shape[0] // 256):
+            w = harmonic_tile(theta_ref, mv_ref, prof_ref, mw_ref, lc, ci) * scale
+            for p in range(2):
+                o_ref[pl.ds(lc * 256, 256), ci, p, :] = w[:, p * half : (p + 1) * half]
 
 
 def harmonic_specs(n_l, n_cycle, width):
     return [
         pl.BlockSpec((n_l, n_cycle), lambda c: (0, 0)),
-        pl.BlockSpec((n_cycle, width), lambda c: (0, c)),
-        pl.BlockSpec((1, n_l, 1), lambda c: (c, 0, 0)),
+        pl.BlockSpec((n_cycle, CH_STEP * width), lambda c: (0, c)),
+        pl.BlockSpec((CH_STEP, n_l, 1), lambda c: (c, 0, 0)),
         pl.BlockSpec((1, width), lambda c: (0, 0)),
     ]
 
@@ -249,9 +257,9 @@
     vmem = pltpu.CompilerParams(vmem_limit_bytes=32 * 1024 * 1024)
     power_part = pl.pallas_call(
         power_kernel,
-        grid=(chan_dev,),
+        grid=(chan_dev // CH_STEP,),
         in_specs=specs,
-        out_specs=pl.BlockSpec((1, 1, 128), lambda c: (c, 0, 0)),
+        out_specs=pl.BlockSpec((CH_STEP, 1, 128), lambda c: (c, 0, 0)),
         out_shape=jax.ShapeDtypeStruct((chan_dev, 1, 128), jnp.float32),
         compiler_params=vmem,
     )(theta_tab, moved, prof_col, mw_row)[:, 0, 0]
@@ -260,9 +268,9 @@
     scale = jnp.broadcast_to(scale[:, None, None], (chan_dev, 1, 128))
     return pl.pallas_call(
         output_kernel,
-        grid=(chan_dev,),
-        in_specs=specs + [pl.BlockSpec((1, 1, 128), lambda c: (c, 0, 0))],
-        out_specs=pl.BlockSpec((L, 1, 2, M_DEV), lambda c: (0, c, 0, 0)),
+        grid=(chan_dev // CH_STEP,),
+        in_specs=specs + [pl.BlockSpec((CH_STEP, 1, 128), lambda c: (c, 0, 0))],
+        out_specs=pl.BlockSpec((L, CH_STEP, 2, M_DEV), lambda c: (0, c, 0, 0)),
         out_shape=jax.ShapeDtypeStruct((L, chan_dev, 2, M_DEV), jnp.float32),
         compiler_params=vmem,
     )(theta_tab, moved, prof_col, mw_row, scale)

time: 175 us -> 174 us (level)
  no operation moved by 1% of the time
where the time goes in v9:
time: 174 us
  Pallas kernels  54 us (31%)
  waiting for transfers between devices  51.4 us (30%)
  starting transfers between devices  29.6 us (17%)
  other arithmetic  22.9 us (13%)
  local copies, waits for them, and re-layouts  10.3 us (6%)
  matrix products  5.3 us (3%)
    all_to_all x1, waiting for transfers between devices, body(): moved = lax.all_to_all(sendbuf, ('blk', 'grp'), 0, 0, tiled=True)  40.2 us
    ppermute x13, starting transfers between devices, ring_sum(): lax.ppermute(v, axis, shift_perm(size, stride, total, k))  22.1 us
    pallas_call x1, Pallas kernels, cycle_fourier(): pl.pallas_call(fourier_kernel, grid=(n_cyc,), in_specs=[pl.BlockSpec((1,...  19.8 us
    pallas_call x1, Pallas kernels, cycle_tables(): pl.pallas_call(table_kernel, grid=(n_cyc,), in_specs=[pl.BlockSpec((1, n_...  16.2 us
    pallas_call x1, Pallas kernels, body(): pl.pallas_call(output_kernel, grid=(chan_dev // CH_STEP,), in_specs=specs...  11.5 us
    ppermute x13, waiting for transfers between devices, ring_sum(): lax.ppermute(v, axis, shift_perm(size, stride, total, k))  11.2 us
    cos x2, other arithmetic, cos_sin_of_phase(): return (jnp.cos(angle), jnp.sin(angle))  8.81 us
    convert_element_type x1, other arithmetic, theta_table(): return (jnp.cos(angle) * weight[None, :]).astype(jnp.bfloat16)  7.96 us
  transfers between devices with their start and end apart: 14, of which 7 were waited for; matrix products, arithmetic and copies ran while one was open for 12% of the time, Pallas kernels for 9%

profile of v9, /device:TPU:0, one launch (start us, length us, event | category | flops | bytes accessed | tf_op | source)
XLA Modules:
  0.0 173.8 jit_solution(14635807697306615588)
XLA Ops:
  0.8 3.0 %convolution_convert_fusion = bf16[8192,16]{0,1:T(8,128)(2,1)S(1)} fusion(bf16[256,16]{0,1:T(8,128)(2,1)} %param.6, bf16[256,8192]{1,0:T(8,128)(2,1)} %sky_ref.1, pred[8192]{0:T(1024)(128)(4,1)S(1)} %bitcast.34), kind=kOutput, calls=%fused_computation | convolution fusion | flops 69337088 | bytes 4472832 | tf_op jit(solution)/shard_map/dot_general | solution.py:227
  6.3 7.0 %fusion.34 = (f32[4,16,1024]{2,1,0:T(8,128)S(1)}, f32[4,16,1024]{2,1,0:T(8,128)S(1)}, f32[4,16,1024]{2,1,0:T(8,128)S(1)}, f32[4,16,1024]{2,1,0:T(8,128)S(1)}) fusion(f32[4]{0:T(128)S(1)} %get-tuple-element.16, pred[4]{0:T(512)(128)(4,1)S(1)} %broadcast_compare_fusion, s32[4]{0:T(128)S(1)} %get-tuple-element.15, s32[16,1024]{1,0:T(8,128)S(1)} %iota_multiply_fusion, ...), kind=kLoop, calls=%fused_computation.53 | loop fusion | flops 1376256 | bytes 1114404 | tf_op jit(solution)/shard_map/cos | solution.py:16
  13.5 1.7 collective-permute-start.1
  15.2 2.7 %collective-permute-start.2 = (f32[16,272]{0,1:T(8,128)S(1)}, f32[16,272]{0,1:T(8,128)S(1)}, u32[]{:S(2)}, u32[]{:S(2)}) collective-permute-start(f32[16,272]{0,1:T(8,128)S(1)} %add.184), channel_id=1, source_target_pairs={{0,16},{4,20},{8,24},{12,28},{16,0},{20,4},{24,8},{28,12},{32,48},... | collective-permute-start | bytes 52232 | tf_op jit(solution)/shard_map/ppermute | solution.py:209
  17.9 1.4 collective-permute-start.3
  19.3 1.8 %fusion.38 = (f32[4,8,1024]{2,1,0:T(8,128)S(1)}, f32[4,8,1024]{2,1,0:T(8,128)S(1)}) fusion(f32[4]{0:T(128)S(1)} %get-tuple-element.16, pred[4]{0:T(512)(128)(4,1)S(1)} %broadcast_compare_fusion, s32[4]{0:T(128)S(1)} %get-tuple-element.15, s32[4,8]{1,0:T(4,128)S(1)} %remainder_select_fusion.1), kind=kLoop, calls=%fused_computation.58 | loop fusion | flops 360448 | bytes 262308 | tf_op jit(solution)/shard_map/cos | solution.py:16
  21.2 3.7 %collective-permute-done.2 = f32[16,272]{0,1:T(8,128)S(1)} collective-permute-done((f32[16,272]{0,1:T(8,128)S(1)}, f32[16,272]{0,1:T(8,128)S(1)}, u32[]{:S(2)}, u32[]{:S(2)}) %collective-permute-start.2) | collective-permute-done | bytes 17440 | tf_op jit(solution)/shard_map/ppermute | solution.py:209
  24.9 1.6 collective-permute-start.4
  26.6 2.9 %collective-permute-start.5 = (f32[16,272]{0,1:T(8,128)S(1)}, f32[16,272]{0,1:T(8,128)S(1)}, u32[]{:S(2)}, u32[]{:S(2)}) collective-permute-start(f32[16,272]{0,1:T(8,128)S(1)} %add_add_fusion.2), channel_id=1, source_target_pairs={{0,64},{4,68},{8,72},{12,76},{16,80},{20,84},{24,88},{28,92},{32,9... | collective-permute-start | bytes 52232 | tf_op jit(solution)/shard_map/ppermute | solution.py:209
  31.6 4.0 %collective-permute-done.5 = f32[16,272]{0,1:T(8,128)S(1)} collective-permute-done((f32[16,272]{0,1:T(8,128)S(1)}, f32[16,272]{0,1:T(8,128)S(1)}, u32[]{:S(2)}, u32[]{:S(2)}) %collective-permute-start.5) | collective-permute-done | bytes 17440 | tf_op jit(solution)/shard_map/ppermute | solution.py:209
  35.7 2.0 %collective-permute-start.7 = (f32[16,272]{0,1:T(8,128)S(1)}, f32[16,272]{0,1:T(8,128)S(1)}, u32[]{:S(2)}, u32[]{:S(2)}) collective-permute-start(f32[16,272]{0,1:T(8,128)S(1)} %add_add_fusion.1), channel_id=1, source_target_pairs={{0,1},{1,2},{2,3},{3,0},{4,5},{5,6},{6,7},{7,4},{8,9},{9,10},{10,1... | collective-permute-start | bytes 52232 | tf_op jit(solution)/shard_map/ppermute | solution.py:209
  37.7 3.6 %collective-permute-start.8 = (f32[16,272]{0,1:T(8,128)S(1)}, f32[16,272]{0,1:T(8,128)S(1)}, u32[]{:S(2)}, u32[]{:S(2)}) collective-permute-start(f32[16,272]{0,1:T(8,128)S(1)} %add_add_fusion.1), channel_id=1, source_target_pairs={{0,2},{1,3},{2,0},{3,1},{4,6},{5,7},{6,4},{7,5},{8,10},{9,11},{10,... | collective-permute-start | bytes 52232 | tf_op jit(solution)/shard_map/ppermute | solution.py:209
  42.4 16.2 %shard_map.55.tab_ref = bf16[4,2048,2048]{2,1,0:T(8,128)(2,1)} custom-call(f32[4,16,1024]{2,1,0:T(8,128)S(1)} %get-tuple-element.13.ca_ref, f32[4,16,1024]{2,1,0:T(8,128)S(1)} %get-tuple-element.14.sa_ref, f32[4,128,1024]{2,1,0:T(8,128)S(1)} %bitcast.31, f32[4,128,1024]{2,1,0:T(8,128)S(1)} %bitcast.30, f32[4,1,128]{2,1,0:T(1,128)S(1)} %broadcast_in_dim.26.inv_ref, ...), custom_call_target="tpu_custom_call" | custom-call | tf_op jit(solution)/shard_map/pallas_call | solution.py:67
  58.7 1.5 cholesky.16
  63.4 19.8 %shard_map.56 = bf16[128,4,8,512]{3,2,1,0:T(8,128)(2,1)S(1)} custom-call(s32[4,1,128]{2,1,0:T(1,128)S(1)} %broadcast_in_dim.23.len_ref, bf16[256,8192]{1,0:T(8,128)(2,1)} %sky_ref.1, f32[256,16]{1,0:T(8,128)S(1)} %fusion.27.proj_ref, f32[16,8192]{1,0:T(8,128)S(1)} %fusion.41.basis_ref, bf16[4,2048,2048]{2,1,0:T(8,128)(2,1)} %shard_map.55.tab_ref), custom_call_target="tpu_custom_call" | custom-call | tf_op jit(solution)/shard_map/pallas_call | solution.py:122
  83.3 2.0 %copy-done.2 = bf16[128,4,8,512]{3,2,1,0:T(8,128)(2,1)} copy-done((bf16[128,4,8,512]{3,2,1,0:T(8,128)(2,1)}, bf16[128,4,8,512]{3,2,1,0:T(8,128)(2,1)S(1)}, u32[]{:S(2)}) %copy-start.2) | copy-done | bytes 4194328
  85.3 7.5 %all-to-all-start = ((bf16[128,4,8,512]{3,2,1,0:T(8,128)(2,1)}), bf16[128,4,8,512]{3,2,1,0:T(8,128)(2,1)}, u32[]{:S(2)}, u32[]{:S(2)}) async-start(bf16[128,4,8,512]{3,2,1,0:T(8,128)(2,1)} %copy-done.2), calls=%async_computation | async-start | bytes 8388608 | tf_op jit(solution)/shard_map/all_to_all | solution.py:244
  93.1 2.7 %copy.21.prof_ref = f32[8,1024,1]{2,1,0:T(8,128)} copy(f32[8,1024,1]{1,0,2:T(8,128)S(1)} %convolution_bitcast_fusion) | data formatting | bytes 65536 | tf_op jit(solution)/shard_map/broadcast_in_dim | solution.py:254
  95.8 8.0 %fusion.6.theta_ref = bf16[1024,512]{1,0:T(8,128)(2,1)S(1)} fusion(f32[512]{0:T(512)S(1)} %sine_multiply_fusion, s32[512]{0:T(512)S(1)} %multiply_add_fusion.1), kind=kLoop, calls=%fused_computation.11 | loop fusion | flops 8388608 | bytes 1052672 | tf_op jit(solution)/shard_map/convert_element_type | solution.py:187
  103.8 40.2 %all-to-all-done = bf16[128,4,8,512]{3,2,1,0:T(8,128)(2,1)} async-done(((bf16[128,4,8,512]{3,2,1,0:T(8,128)(2,1)}), bf16[128,4,8,512]{3,2,1,0:T(8,128)(2,1)}, u32[]{:S(2)}, u32[]{:S(2)}) %all-to-all-start) | async-done | bytes 4194336 | tf_op jit(solution)/shard_map/all_to_all | solution.py:244
  144.0 4.6 %copy.24 = bf16[64,8,8,512]{3,1,2,0:T(8,128)(2,1)S(1)} copy(bf16[64,8,8,512]{3,2,1,0:T(8,128)(2,1)} %bitcast.10) | data formatting | bytes 8388608
  148.6 6.5 %shard_map.57 = f32[8,1,128]{2,1,0:T(1,128)S(1)} custom-call(bf16[1024,512]{1,0:T(8,128)(2,1)S(1)} %fusion.6.theta_ref, bf16[512,4096]{1,0:T(8,128)(2,1)S(1)} %bitcast.28, f32[8,1024,1]{2,1,0:T(8,128)S(1)} %copy-done.1, f32[1,512]{1,0:T(1,128)S(1)} %bitcast.32), custom_call_target="tpu_custom_call" | custom-call | tf_op jit(solution)/shard_map/pallas_call | solution.py:258
  156.2 2.5 %collective-permute-start.11 = (f32[8]{0:T(128)S(1)}, f32[8]{0:T(128)S(1)}, u32[]{:S(2)}, u32[]{:S(2)}) collective-permute-start(f32[8]{0:T(128)S(1)} %slice_reduce_fusion), channel_id=1, source_target_pairs={{0,2},{1,3},{2,0},{3,1},{4,6},{5,7},{6,4},{7,5},{8,10},{9,11},{10,... | collective-permute-start | bytes 104 | tf_op jit(solution)/shard_map/ppermute | solution.py:209
  162.3 11.5 %shard_map.58 = f32[1024,8,2,256]{3,2,1,0:T(2,128)} custom-call(bf16[1024,512]{1,0:T(8,128)(2,1)S(1)} %fusion.6.theta_ref, bf16[512,4096]{1,0:T(8,128)(2,1)S(1)} %bitcast.29, f32[8,1024,1]{2,1,0:T(8,128)S(1)} %copy-done.1, f32[1,512]{1,0:T(1,128)S(1)} %bitcast.33, f32[8,1,128]{2,1,0:T(1,128)S(1)} %broadcast_in_dim.30.scale_ref), custom_call_target="tpu_custom_call" | custom-call | tf_op jit(solution)/shard_map/pallas_call | solution.py:269
  (66 shorter events, 15.1 us)
Async XLA Ops:
  0.0 92.8 %copy-start = (f32[8,1024]{1,0:T(8,128)S(1)}, f32[8,1024]{1,0:T(8,128)}, u32[]{:S(2)}) copy-start(f32[8,1024]{1,0:T(8,128)} %param.8) | copy-start | bytes 98308
  0.8 3.5 %copy-start.3 = (bf16[256,8192]{1,0:T(8,128)(2,1)S(1)}, bf16[256,8192]{1,0:T(8,128)(2,1)}, u32[]{:S(2)}) copy-start(bf16[256,8192]{1,0:T(8,128)(2,1)} %sky_ref.1) | copy-start | bytes 12582916
  4.2 1.7 copy-start.4
  5.8 7.6 %collective-permute-start = (f32[16,272]{0,1:T(8,128)S(1)}, f32[16,272]{0,1:T(8,128)S(1)}, u32[]{:S(2)}, u32[]{:S(2)}) collective-permute-start(f32[16,272]{0,1:T(8,128)S(1)} %copy.17), channel_id=1, source_target_pairs={{0,4},{4,0},{8,12},{12,8},{16,20},{20,16},{24,28},{28,24},{32,36},... | collective-permute-start | bytes 52232 | tf_op jit(solution)/shard_map/ppermute | solution.py:209
  13.5 7.7 %collective-permute-start.1 = (f32[16,272]{0,1:T(8,128)S(1)}, f32[16,272]{0,1:T(8,128)S(1)}, u32[]{:S(2)}, u32[]{:S(2)}) collective-permute-start(f32[16,272]{0,1:T(8,128)S(1)} %add.184), channel_id=1, source_target_pairs={{0,8},{4,12},{8,16},{12,20},{16,24},{20,28},{24,0},{28,4},{32,40},... | collective-permute-start | bytes 52232 | tf_op jit(solution)/shard_map/ppermute | solution.py:209
  15.2 9.7 %collective-permute-start.2 = (f32[16,272]{0,1:T(8,128)S(1)}, f32[16,272]{0,1:T(8,128)S(1)}, u32[]{:S(2)}, u32[]{:S(2)}) collective-permute-start(f32[16,272]{0,1:T(8,128)S(1)} %add.184), channel_id=1, source_target_pairs={{0,16},{4,20},{8,24},{12,28},{16,0},{20,4},{24,8},{28,12},{32,48},... | collective-permute-start | bytes 52232 | tf_op jit(solution)/shard_map/ppermute | solution.py:209
  17.9 7.0 %collective-permute-start.3 = (f32[16,272]{0,1:T(8,128)S(1)}, f32[16,272]{0,1:T(8,128)S(1)}, u32[]{:S(2)}, u32[]{:S(2)}) collective-permute-start(f32[16,272]{0,1:T(8,128)S(1)} %add.184), channel_id=1, source_target_pairs={{0,24},{4,28},{8,0},{12,4},{16,8},{20,12},{24,16},{28,20},{32,56},... | collective-permute-start | bytes 52232 | tf_op jit(solution)/shard_map/ppermute | solution.py:209
  24.9 6.7 %collective-permute-start.4 = (f32[16,272]{0,1:T(8,128)S(1)}, f32[16,272]{0,1:T(8,128)S(1)}, u32[]{:S(2)}, u32[]{:S(2)}) collective-permute-start(f32[16,272]{0,1:T(8,128)S(1)} %add_add_fusion.2), channel_id=1, source_target_pairs={{0,32},{4,36},{8,40},{12,44},{16,48},{20,52},{24,56},{28,60},{32,6... | collective-permute-start | bytes 52232 | tf_op jit(solution)/shard_map/ppermute | solution.py:209
  26.6 9.1 %collective-permute-start.5 = (f32[16,272]{0,1:T(8,128)S(1)}, f32[16,272]{0,1:T(8,128)S(1)}, u32[]{:S(2)}, u32[]{:S(2)}) collective-permute-start(f32[16,272]{0,1:T(8,128)S(1)} %add_add_fusion.2), channel_id=1, source_target_pairs={{0,64},{4,68},{8,72},{12,76},{16,80},{20,84},{24,88},{28,92},{32,9... | collective-permute-start | bytes 52232 | tf_op jit(solution)/shard_map/ppermute | solution.py:209
  29.5 6.2 %collective-permute-start.6 = (f32[16,272]{0,1:T(8,128)S(1)}, f32[16,272]{0,1:T(8,128)S(1)}, u32[]{:S(2)}, u32[]{:S(2)}) collective-permute-start(f32[16,272]{0,1:T(8,128)S(1)} %add_add_fusion.2), channel_id=1, source_target_pairs={{0,96},{4,100},{8,104},{12,108},{16,112},{20,116},{24,120},{28,124... | collective-permute-start | bytes 52232 | tf_op jit(solution)/shard_map/ppermute | solution.py:209
  35.7 22.9 %collective-permute-start.7 = (f32[16,272]{0,1:T(8,128)S(1)}, f32[16,272]{0,1:T(8,128)S(1)}, u32[]{:S(2)}, u32[]{:S(2)}) collective-permute-start(f32[16,272]{0,1:T(8,128)S(1)} %add_add_fusion.1), channel_id=1, source_target_pairs={{0,1},{1,2},{2,3},{3,0},{4,5},{5,6},{6,7},{7,4},{8,9},{9,10},{10,1... | collective-permute-start | bytes 52232 | tf_op jit(solution)/shard_map/ppermute | solution.py:209
  37.7 20.9 %collective-permute-start.8 = (f32[16,272]{0,1:T(8,128)S(1)}, f32[16,272]{0,1:T(8,128)S(1)}, u32[]{:S(2)}, u32[]{:S(2)}) collective-permute-start(f32[16,272]{0,1:T(8,128)S(1)} %add_add_fusion.1), channel_id=1, source_target_pairs={{0,2},{1,3},{2,0},{3,1},{4,6},{5,7},{6,4},{7,5},{8,10},{9,11},{10,... | collective-permute-start | bytes 52232 | tf_op jit(solution)/shard_map/ppermute | solution.py:209
  41.2 17.3 %collective-permute-start.9 = (f32[16,272]{0,1:T(8,128)S(1)}, f32[16,272]{0,1:T(8,128)S(1)}, u32[]{:S(2)}, u32[]{:S(2)}) collective-permute-start(f32[16,272]{0,1:T(8,128)S(1)} %add_add_fusion.1), channel_id=1, source_target_pairs={{0,3},{1,0},{2,1},{3,2},{4,7},{5,4},{6,5},{7,6},{8,11},{9,8},{10,9... | collective-permute-start | bytes 52232 | tf_op jit(solution)/shard_map/ppermute | solution.py:209
  83.3 2.0 %copy-start.2 = (bf16[128,4,8,512]{3,2,1,0:T(8,128)(2,1)}, bf16[128,4,8,512]{3,2,1,0:T(8,128)(2,1)S(1)}, u32[]{:S(2)}) copy-start(bf16[128,4,8,512]{3,2,1,0:T(8,128)(2,1)S(1)} %shard_map.56) | copy-start | bytes 12582916
  85.3 7.6 %copy-start.5 = (s32[8]{0:T(128)S(1)}, s32[8]{0:T(128)}, u32[]{:S(2)}) copy-start(s32[8]{0:T(128)} %param.9) | copy-start | bytes 100
  85.3 58.7 %all-to-all-start = ((bf16[128,4,8,512]{3,2,1,0:T(8,128)(2,1)}), bf16[128,4,8,512]{3,2,1,0:T(8,128)(2,1)}, u32[]{:S(2)}, u32[]{:S(2)}) async-start(bf16[128,4,8,512]{3,2,1,0:T(8,128)(2,1)} %copy-done.2), calls=%async_computation | async-start | bytes 8388608 | tf_op jit(solution)/shard_map/all_to_all | solution.py:244
  144.0 4.6 %copy-start.1 = (f32[8,1024,1]{2,1,0:T(8,128)S(1)}, f32[8,1024,1]{2,1,0:T(8,128)}, u32[]{:S(2)}) copy-start(f32[8,1024,1]{2,1,0:T(8,128)} %copy.21.prof_ref) | copy-start | bytes 98308
  155.3 4.8 %collective-permute-start.10 = (f32[8]{0:T(128)S(1)}, f32[8]{0:T(128)S(1)}, u32[]{:S(2)}, u32[]{:S(2)}) collective-permute-start(f32[8]{0:T(128)S(1)} %slice_reduce_fusion), channel_id=1, source_target_pairs={{0,1},{1,2},{2,3},{3,0},{4,5},{5,6},{6,7},{7,4},{8,9},{9,10},{10,1... | collective-permute-start | bytes 104 | tf_op jit(solution)/shard_map/ppermute | solution.py:209
  156.2 5.1 %collective-permute-start.11 = (f32[8]{0:T(128)S(1)}, f32[8]{0:T(128)S(1)}, u32[]{:S(2)}, u32[]{:S(2)}) collective-permute-start(f32[8]{0:T(128)S(1)} %slice_reduce_fusion), channel_id=1, source_target_pairs={{0,2},{1,3},{2,0},{3,1},{4,6},{5,7},{6,4},{7,5},{8,10},{9,11},{10,... | collective-permute-start | bytes 104 | tf_op jit(solution)/shard_map/ppermute | solution.py:209
  158.7 3.6 %collective-permute-start.12 = (f32[8]{0:T(128)S(1)}, f32[8]{0:T(128)S(1)}, u32[]{:S(2)}, u32[]{:S(2)}) collective-permute-start(f32[8]{0:T(128)S(1)} %slice_reduce_fusion), channel_id=1, source_target_pairs={{0,3},{1,0},{2,1},{3,2},{4,7},{5,4},{6,5},{7,6},{8,11},{9,8},{10,9... | collective-permute-start | bytes 104 | tf_op jit(solution)/shard_map/ppermute | solution.py:209

commit v10 on v9

--- a/solution.py
+++ b/solution.py
@@ -136,7 +136,8 @@
     )(lens, sky_map, projected_t, basis, tables)
 
 
-CH_STEP = 2
+POWER_STEP = 4
+OUT_STEP = 1
 
 
 def harmonic_tile(theta_ref, mv_ref, prof_ref, mw_ref, lc, ci):
@@ -167,11 +168,11 @@
                 o_ref[pl.ds(lc * 256, 256), ci, p, :] = w[:, p * half : (p + 1) * half]
 
 
-def harmonic_specs(n_l, n_cycle, width):
+def harmonic_specs(n_l, n_cycle, width, step):
     return [
         pl.BlockSpec((n_l, n_cycle), lambda c: (0, 0)),
-        pl.BlockSpec((n_cycle, CH_STEP * width), lambda c: (0, c)),
-        pl.BlockSpec((CH_STEP, n_l, 1), lambda c: (c, 0, 0)),
+        pl.BlockSpec((n_cycle, step * width), lambda c: (0, c)),
+        pl.BlockSpec((step, n_l, 1), lambda c: (c, 0, 0)),
         pl.BlockSpec((1, width), lambda c: (0, 0)),
     ]
 
@@ -253,13 +254,12 @@
     mw_row = jnp.concatenate([mweight, mweight])[None, :]
     prof_col = profiles[:, :, None]
     width = 2 * M_DEV
-    specs = harmonic_specs(L, n_cycle, width)
     vmem = pltpu.CompilerParams(vmem_limit_bytes=32 * 1024 * 1024)
     power_part = pl.pallas_call(
         power_kernel,
-        grid=(chan_dev // CH_STEP,),
-        in_specs=specs,
-        out_specs=pl.BlockSpec((CH_STEP, 1, 128), lambda c: (c, 0, 0)),
+        grid=(chan_dev // POWER_STEP,),
+        in_specs=harmonic_specs(L, n_cycle, width, POWER_STEP),
+        out_specs=pl.BlockSpec((POWER_STEP, 1, 128), lambda c: (c, 0, 0)),
         out_shape=jax.ShapeDtypeStruct((chan_dev, 1, 128), jnp.float32),
         compiler_params=vmem,
     )(theta_tab, moved, prof_col, mw_row)[:, 0, 0]
@@ -268,9 +268,10 @@
     scale = jnp.broadcast_to(scale[:, None, None], (chan_dev, 1, 128))
     return pl.pallas_call(
         output_kernel,
-        grid=(chan_dev // CH_STEP,),
-        in_specs=specs + [pl.BlockSpec((CH_STEP, 1, 128), lambda c: (c, 0, 0))],
-        out_specs=pl.BlockSpec((L, CH_STEP, 2, M_DEV), lambda c: (0, c, 0, 0)),
+        grid=(chan_dev // OUT_STEP,),
+        in_specs=harmonic_specs(L, n_cycle, width, OUT_STEP)
+        + [pl.BlockSpec((OUT_STEP, 1, 128), lambda c: (c, 0, 0))],
+        out_specs=pl.BlockSpec((L, OUT_STEP, 2, M_DEV), lambda c: (0, c, 0, 0)),
         out_shape=jax.ShapeDtypeStruct((L, chan_dev, 2, M_DEV), jnp.float32),
         compiler_params=vmem,
     )(theta_tab, moved, prof_col, mw_row, scale)

time: 174 us -> 173 us (level)
  no operation moved by 1% of the time
where the time goes in v10:
time: 173 us
  Pallas kernels  53 us (31%)
  waiting for transfers between devices  51.4 us (30%)
  starting transfers between devices  29.6 us (17%)
  other arithmetic  22.9 us (13%)
  local copies, waits for them, and re-layouts  10.3 us (6%)
  matrix products  5.3 us (3%)
    all_to_all x1, waiting for transfers between devices, body(): moved = lax.all_to_all(sendbuf, ('blk', 'grp'), 0, 0, tiled=True)  40.2 us
    ppermute x13, starting transfers between devices, ring_sum(): lax.ppermute(v, axis, shift_perm(size, stride, total, k))  22.1 us
    pallas_call x1, Pallas kernels, cycle_fourier(): pl.pallas_call(fourier_kernel, grid=(n_cyc,), in_specs=[pl.BlockSpec((1,...  19.8 us
    pallas_call x1, Pallas kernels, cycle_tables(): pl.pallas_call(table_kernel, grid=(n_cyc,), in_specs=[pl.BlockSpec((1, n_...  16.2 us
    pallas_call x1, Pallas kernels, body(): pl.pallas_call(output_kernel, grid=(chan_dev // OUT_STEP,), in_specs=harm...  11.2 us
    ppermute x13, waiting for transfers between devices, ring_sum(): lax.ppermute(v, axis, shift_perm(size, stride, total, k))  11.2 us
    cos x2, other arithmetic, cos_sin_of_phase(): return (jnp.cos(angle), jnp.sin(angle))  8.81 us
    convert_element_type x1, other arithmetic, theta_table(): return (jnp.cos(angle) * weight[None, :]).astype(jnp.bfloat16)  7.96 us
  transfers between devices with their start and end apart: 14, of which 7 were waited for; matrix products, arithmetic and copies ran while one was open for 12% of the time, Pallas kernels for 9%

profile of v10, /device:TPU:0, one launch (start us, length us, event | category | flops | bytes accessed | tf_op | source)
XLA Modules:
  0.0 172.8 jit_solution(1765467668034981661)
XLA Ops:
  0.8 3.0 %convolution_convert_fusion = bf16[8192,16]{0,1:T(8,128)(2,1)S(1)} fusion(bf16[256,16]{0,1:T(8,128)(2,1)} %param.6, bf16[256,8192]{1,0:T(8,128)(2,1)} %sky_ref.1, pred[8192]{0:T(1024)(128)(4,1)S(1)} %bitcast.34), kind=kOutput, calls=%fused_computation | convolution fusion | flops 69337088 | bytes 4472832 | tf_op jit(solution)/shard_map/dot_general | solution.py:228
  6.3 7.0 %fusion.34 = (f32[4,16,1024]{2,1,0:T(8,128)S(1)}, f32[4,16,1024]{2,1,0:T(8,128)S(1)}, f32[4,16,1024]{2,1,0:T(8,128)S(1)}, f32[4,16,1024]{2,1,0:T(8,128)S(1)}) fusion(f32[4]{0:T(128)S(1)} %get-tuple-element.16, pred[4]{0:T(512)(128)(4,1)S(1)} %broadcast_compare_fusion, s32[4]{0:T(128)S(1)} %get-tuple-element.15, s32[16,1024]{1,0:T(8,128)S(1)} %iota_multiply_fusion, ...), kind=kLoop, calls=%fused_computation.53 | loop fusion | flops 1376256 | bytes 1114404 | tf_op jit(solution)/shard_map/cos | solution.py:16
  13.5 1.7 collective-permute-start.1
  15.2 2.7 %collective-permute-start.2 = (f32[16,272]{0,1:T(8,128)S(1)}, f32[16,272]{0,1:T(8,128)S(1)}, u32[]{:S(2)}, u32[]{:S(2)}) collective-permute-start(f32[16,272]{0,1:T(8,128)S(1)} %add.184), channel_id=1, source_target_pairs={{0,16},{4,20},{8,24},{12,28},{16,0},{20,4},{24,8},{28,12},{32,48},... | collective-permute-start | bytes 52232 | tf_op jit(solution)/shard_map/ppermute | solution.py:210
  17.9 1.4 collective-permute-start.3
  19.3 1.8 %fusion.38 = (f32[4,8,1024]{2,1,0:T(8,128)S(1)}, f32[4,8,1024]{2,1,0:T(8,128)S(1)}) fusion(f32[4]{0:T(128)S(1)} %get-tuple-element.16, pred[4]{0:T(512)(128)(4,1)S(1)} %broadcast_compare_fusion, s32[4]{0:T(128)S(1)} %get-tuple-element.15, s32[4,8]{1,0:T(4,128)S(1)} %remainder_select_fusion.1), kind=kLoop, calls=%fused_computation.58 | loop fusion | flops 360448 | bytes 262308 | tf_op jit(solution)/shard_map/cos | solution.py:16
  21.2 3.7 %collective-permute-done.2 = f32[16,272]{0,1:T(8,128)S(1)} collective-permute-done((f32[16,272]{0,1:T(8,128)S(1)}, f32[16,272]{0,1:T(8,128)S(1)}, u32[]{:S(2)}, u32[]{:S(2)}) %collective-permute-start.2) | collective-permute-done | bytes 17440 | tf_op jit(solution)/shard_map/ppermute | solution.py:210
  24.9 1.6 collective-permute-start.4
  26.6 2.9 %collective-permute-start.5 = (f32[16,272]{0,1:T(8,128)S(1)}, f32[16,272]{0,1:T(8,128)S(1)}, u32[]{:S(2)}, u32[]{:S(2)}) collective-permute-start(f32[16,272]{0,1:T(8,128)S(1)} %add_add_fusion.2), channel_id=1, source_target_pairs={{0,64},{4,68},{8,72},{12,76},{16,80},{20,84},{24,88},{28,92},{32,9... | collective-permute-start | bytes 52232 | tf_op jit(solution)/shard_map/ppermute | solution.py:210
  31.6 4.0 %collective-permute-done.5 = f32[16,272]{0,1:T(8,128)S(1)} collective-permute-done((f32[16,272]{0,1:T(8,128)S(1)}, f32[16,272]{0,1:T(8,128)S(1)}, u32[]{:S(2)}, u32[]{:S(2)}) %collective-permute-start.5) | collective-permute-done | bytes 17440 | tf_op jit(solution)/shard_map/ppermute | solution.py:210
  35.7 2.0 %collective-permute-start.7 = (f32[16,272]{0,1:T(8,128)S(1)}, f32[16,272]{0,1:T(8,128)S(1)}, u32[]{:S(2)}, u32[]{:S(2)}) collective-permute-start(f32[16,272]{0,1:T(8,128)S(1)} %add_add_fusion.1), channel_id=1, source_target_pairs={{0,1},{1,2},{2,3},{3,0},{4,5},{5,6},{6,7},{7,4},{8,9},{9,10},{10,1... | collective-permute-start | bytes 52232 | tf_op jit(solution)/shard_map/ppermute | solution.py:210
  37.7 3.6 %collective-permute-start.8 = (f32[16,272]{0,1:T(8,128)S(1)}, f32[16,272]{0,1:T(8,128)S(1)}, u32[]{:S(2)}, u32[]{:S(2)}) collective-permute-start(f32[16,272]{0,1:T(8,128)S(1)} %add_add_fusion.1), channel_id=1, source_target_pairs={{0,2},{1,3},{2,0},{3,1},{4,6},{5,7},{6,4},{7,5},{8,10},{9,11},{10,... | collective-permute-start | bytes 52232 | tf_op jit(solution)/shard_map/ppermute | solution.py:210
  42.4 16.2 %shard_map.55.tab_ref = bf16[4,2048,2048]{2,1,0:T(8,128)(2,1)} custom-call(f32[4,16,1024]{2,1,0:T(8,128)S(1)} %get-tuple-element.13.ca_ref, f32[4,16,1024]{2,1,0:T(8,128)S(1)} %get-tuple-element.14.sa_ref, f32[4,128,1024]{2,1,0:T(8,128)S(1)} %bitcast.31, f32[4,128,1024]{2,1,0:T(8,128)S(1)} %bitcast.30, f32[4,1,128]{2,1,0:T(1,128)S(1)} %broadcast_in_dim.26.inv_ref, ...), custom_call_target="tpu_custom_call" | custom-call | tf_op jit(solution)/shard_map/pallas_call | solution.py:67
  58.7 1.5 cholesky.16
  63.4 19.8 %shard_map.56 = bf16[128,4,8,512]{3,2,1,0:T(8,128)(2,1)S(1)} custom-call(s32[4,1,128]{2,1,0:T(1,128)S(1)} %broadcast_in_dim.23.len_ref, bf16[256,8192]{1,0:T(8,128)(2,1)} %sky_ref.1, f32[256,16]{1,0:T(8,128)S(1)} %fusion.27.proj_ref, f32[16,8192]{1,0:T(8,128)S(1)} %fusion.41.basis_ref, bf16[4,2048,2048]{2,1,0:T(8,128)(2,1)} %shard_map.55.tab_ref), custom_call_target="tpu_custom_call" | custom-call | tf_op jit(solution)/shard_map/pallas_call | solution.py:122
  83.3 2.0 %copy-done.2 = bf16[128,4,8,512]{3,2,1,0:T(8,128)(2,1)} copy-done((bf16[128,4,8,512]{3,2,1,0:T(8,128)(2,1)}, bf16[128,4,8,512]{3,2,1,0:T(8,128)(2,1)S(1)}, u32[]{:S(2)}) %copy-start.2) | copy-done | bytes 4194328
  85.3 7.5 %all-to-all-start = ((bf16[128,4,8,512]{3,2,1,0:T(8,128)(2,1)}), bf16[128,4,8,512]{3,2,1,0:T(8,128)(2,1)}, u32[]{:S(2)}, u32[]{:S(2)}) async-start(bf16[128,4,8,512]{3,2,1,0:T(8,128)(2,1)} %copy-done.2), calls=%async_computation | async-start | bytes 8388608 | tf_op jit(solution)/shard_map/all_to_all | solution.py:245
  93.1 2.7 %copy.21.prof_ref = f32[8,1024,1]{2,1,0:T(8,128)} copy(f32[8,1024,1]{1,0,2:T(8,128)S(1)} %convolution_bitcast_fusion) | data formatting | bytes 65536 | tf_op jit(solution)/shard_map/broadcast_in_dim | solution.py:255
  95.8 8.0 %fusion.6.theta_ref = bf16[1024,512]{1,0:T(8,128)(2,1)S(1)} fusion(f32[512]{0:T(512)S(1)} %sine_multiply_fusion, s32[512]{0:T(512)S(1)} %multiply_add_fusion.1), kind=kLoop, calls=%fused_computation.11 | loop fusion | flops 8388608 | bytes 1052672 | tf_op jit(solution)/shard_map/convert_element_type | solution.py:188
  103.8 40.2 %all-to-all-done = bf16[128,4,8,512]{3,2,1,0:T(8,128)(2,1)} async-done(((bf16[128,4,8,512]{3,2,1,0:T(8,128)(2,1)}), bf16[128,4,8,512]{3,2,1,0:T(8,128)(2,1)}, u32[]{:S(2)}, u32[]{:S(2)}) %all-to-all-start) | async-done | bytes 4194336 | tf_op jit(solution)/shard_map/all_to_all | solution.py:245
  144.0 4.6 %copy.24 = bf16[64,8,8,512]{3,1,2,0:T(8,128)(2,1)S(1)} copy(bf16[64,8,8,512]{3,2,1,0:T(8,128)(2,1)} %bitcast.10) | data formatting | bytes 8388608
  148.6 5.8 %shard_map.57 = f32[8,1,128]{2,1,0:T(1,128)S(1)} custom-call(bf16[1024,512]{1,0:T(8,128)(2,1)S(1)} %fusion.6.theta_ref, bf16[512,4096]{1,0:T(8,128)(2,1)S(1)} %bitcast.28, f32[8,1024,1]{2,1,0:T(8,128)S(1)} %copy-done.1, f32[1,512]{1,0:T(1,128)S(1)} %bitcast.32), custom_call_target="tpu_custom_call" | custom-call | tf_op jit(solution)/shard_map/pallas_call | solution.py:258
  155.5 2.5 %collective-permute-start.11 = (f32[8]{0:T(128)S(1)}, f32[8]{0:T(128)S(1)}, u32[]{:S(2)}, u32[]{:S(2)}) collective-permute-start(f32[8]{0:T(128)S(1)} %slice_reduce_fusion), channel_id=1, source_target_pairs={{0,2},{1,3},{2,0},{3,1},{4,6},{5,7},{6,4},{7,5},{8,10},{9,11},{10,... | collective-permute-start | bytes 104 | tf_op jit(solution)/shard_map/ppermute | solution.py:210
  161.6 11.2 %shard_map.58 = f32[1024,8,2,256]{3,2,1,0:T(2,128)} custom-call(bf16[1024,512]{1,0:T(8,128)(2,1)S(1)} %fusion.6.theta_ref, bf16[512,4096]{1,0:T(8,128)(2,1)S(1)} %bitcast.29, f32[8,1024,1]{2,1,0:T(8,128)S(1)} %copy-done.1, f32[1,512]{1,0:T(1,128)S(1)} %bitcast.33, f32[8,1,128]{2,1,0:T(1,128)S(1)} %broadcast_in_dim.30.scale_ref), custom_call_target="tpu_custom_call" | custom-call | tf_op jit(solution)/shard_map/pallas_call | solution.py:269
  (66 shorter events, 15.1 us)
Async XLA Ops:
  0.0 92.8 %copy-start = (f32[8,1024]{1,0:T(8,128)S(1)}, f32[8,1024]{1,0:T(8,128)}, u32[]{:S(2)}) copy-start(f32[8,1024]{1,0:T(8,128)} %param.8) | copy-start | bytes 98308
  0.8 3.5 %copy-start.3 = (bf16[256,8192]{1,0:T(8,128)(2,1)S(1)}, bf16[256,8192]{1,0:T(8,128)(2,1)}, u32[]{:S(2)}) copy-start(bf16[256,8192]{1,0:T(8,128)(2,1)} %sky_ref.1) | copy-start | bytes 12582916
  4.2 1.7 copy-start.4
  5.8 7.6 %collective-permute-start = (f32[16,272]{0,1:T(8,128)S(1)}, f32[16,272]{0,1:T(8,128)S(1)}, u32[]{:S(2)}, u32[]{:S(2)}) collective-permute-start(f32[16,272]{0,1:T(8,128)S(1)} %copy.17), channel_id=1, source_target_pairs={{0,4},{4,0},{8,12},{12,8},{16,20},{20,16},{24,28},{28,24},{32,36},... | collective-permute-start | bytes 52232 | tf_op jit(solution)/shard_map/ppermute | solution.py:210
  13.5 7.7 %collective-permute-start.1 = (f32[16,272]{0,1:T(8,128)S(1)}, f32[16,272]{0,1:T(8,128)S(1)}, u32[]{:S(2)}, u32[]{:S(2)}) collective-permute-start(f32[16,272]{0,1:T(8,128)S(1)} %add.184), channel_id=1, source_target_pairs={{0,8},{4,12},{8,16},{12,20},{16,24},{20,28},{24,0},{28,4},{32,40},... | collective-permute-start | bytes 52232 | tf_op jit(solution)/shard_map/ppermute | solution.py:210
  15.2 9.7 %collective-permute-start.2 = (f32[16,272]{0,1:T(8,128)S(1)}, f32[16,272]{0,1:T(8,128)S(1)}, u32[]{:S(2)}, u32[]{:S(2)}) collective-permute-start(f32[16,272]{0,1:T(8,128)S(1)} %add.184), channel_id=1, source_target_pairs={{0,16},{4,20},{8,24},{12,28},{16,0},{20,4},{24,8},{28,12},{32,48},... | collective-permute-start | bytes 52232 | tf_op jit(solution)/shard_map/ppermute | solution.py:210
  17.9 7.0 %collective-permute-start.3 = (f32[16,272]{0,1:T(8,128)S(1)}, f32[16,272]{0,1:T(8,128)S(1)}, u32[]{:S(2)}, u32[]{:S(2)}) collective-permute-start(f32[16,272]{0,1:T(8,128)S(1)} %add.184), channel_id=1, source_target_pairs={{0,24},{4,28},{8,0},{12,4},{16,8},{20,12},{24,16},{28,20},{32,56},... | collective-permute-start | bytes 52232 | tf_op jit(solution)/shard_map/ppermute | solution.py:210
  24.9 6.7 %collective-permute-start.4 = (f32[16,272]{0,1:T(8,128)S(1)}, f32[16,272]{0,1:T(8,128)S(1)}, u32[]{:S(2)}, u32[]{:S(2)}) collective-permute-start(f32[16,272]{0,1:T(8,128)S(1)} %add_add_fusion.2), channel_id=1, source_target_pairs={{0,32},{4,36},{8,40},{12,44},{16,48},{20,52},{24,56},{28,60},{32,6... | collective-permute-start | bytes 52232 | tf_op jit(solution)/shard_map/ppermute | solution.py:210
  26.6 9.1 %collective-permute-start.5 = (f32[16,272]{0,1:T(8,128)S(1)}, f32[16,272]{0,1:T(8,128)S(1)}, u32[]{:S(2)}, u32[]{:S(2)}) collective-permute-start(f32[16,272]{0,1:T(8,128)S(1)} %add_add_fusion.2), channel_id=1, source_target_pairs={{0,64},{4,68},{8,72},{12,76},{16,80},{20,84},{24,88},{28,92},{32,9... | collective-permute-start | bytes 52232 | tf_op jit(solution)/shard_map/ppermute | solution.py:210
  29.5 6.2 %collective-permute-start.6 = (f32[16,272]{0,1:T(8,128)S(1)}, f32[16,272]{0,1:T(8,128)S(1)}, u32[]{:S(2)}, u32[]{:S(2)}) collective-permute-start(f32[16,272]{0,1:T(8,128)S(1)} %add_add_fusion.2), channel_id=1, source_target_pairs={{0,96},{4,100},{8,104},{12,108},{16,112},{20,116},{24,120},{28,124... | collective-permute-start | bytes 52232 | tf_op jit(solution)/shard_map/ppermute | solution.py:210
  35.7 22.9 %collective-permute-start.7 = (f32[16,272]{0,1:T(8,128)S(1)}, f32[16,272]{0,1:T(8,128)S(1)}, u32[]{:S(2)}, u32[]{:S(2)}) collective-permute-start(f32[16,272]{0,1:T(8,128)S(1)} %add_add_fusion.1), channel_id=1, source_target_pairs={{0,1},{1,2},{2,3},{3,0},{4,5},{5,6},{6,7},{7,4},{8,9},{9,10},{10,1... | collective-permute-start | bytes 52232 | tf_op jit(solution)/shard_map/ppermute | solution.py:210
  37.7 20.9 %collective-permute-start.8 = (f32[16,272]{0,1:T(8,128)S(1)}, f32[16,272]{0,1:T(8,128)S(1)}, u32[]{:S(2)}, u32[]{:S(2)}) collective-permute-start(f32[16,272]{0,1:T(8,128)S(1)} %add_add_fusion.1), channel_id=1, source_target_pairs={{0,2},{1,3},{2,0},{3,1},{4,6},{5,7},{6,4},{7,5},{8,10},{9,11},{10,... | collective-permute-start | bytes 52232 | tf_op jit(solution)/shard_map/ppermute | solution.py:210
  41.2 17.3 %collective-permute-start.9 = (f32[16,272]{0,1:T(8,128)S(1)}, f32[16,272]{0,1:T(8,128)S(1)}, u32[]{:S(2)}, u32[]{:S(2)}) collective-permute-start(f32[16,272]{0,1:T(8,128)S(1)} %add_add_fusion.1), channel_id=1, source_target_pairs={{0,3},{1,0},{2,1},{3,2},{4,7},{5,4},{6,5},{7,6},{8,11},{9,8},{10,9... | collective-permute-start | bytes 52232 | tf_op jit(solution)/shard_map/ppermute | solution.py:210
  83.3 2.0 %copy-start.2 = (bf16[128,4,8,512]{3,2,1,0:T(8,128)(2,1)}, bf16[128,4,8,512]{3,2,1,0:T(8,128)(2,1)S(1)}, u32[]{:S(2)}) copy-start(bf16[128,4,8,512]{3,2,1,0:T(8,128)(2,1)S(1)} %shard_map.56) | copy-start | bytes 12582916
  85.3 7.6 %copy-start.5 = (s32[8]{0:T(128)S(1)}, s32[8]{0:T(128)}, u32[]{:S(2)}) copy-start(s32[8]{0:T(128)} %param.9) | copy-start | bytes 100
  85.3 58.7 %all-to-all-start = ((bf16[128,4,8,512]{3,2,1,0:T(8,128)(2,1)}), bf16[128,4,8,512]{3,2,1,0:T(8,128)(2,1)}, u32[]{:S(2)}, u32[]{:S(2)}) async-start(bf16[128,4,8,512]{3,2,1,0:T(8,128)(2,1)} %copy-done.2), calls=%async_computation | async-start | bytes 8388608 | tf_op jit(solution)/shard_map/all_to_all | solution.py:245
  144.0 4.6 %copy-start.1 = (f32[8,1024,1]{2,1,0:T(8,128)S(1)}, f32[8,1024,1]{2,1,0:T(8,128)}, u32[]{:S(2)}) copy-start(f32[8,1024,1]{2,1,0:T(8,128)} %copy.21.prof_ref) | copy-start | bytes 98308
  154.6 4.8 %collective-permute-start.10 = (f32[8]{0:T(128)S(1)}, f32[8]{0:T(128)S(1)}, u32[]{:S(2)}, u32[]{:S(2)}) collective-permute-start(f32[8]{0:T(128)S(1)} %slice_reduce_fusion), channel_id=1, source_target_pairs={{0,1},{1,2},{2,3},{3,0},{4,5},{5,6},{6,7},{7,4},{8,9},{9,10},{10,1... | collective-permute-start | bytes 104 | tf_op jit(solution)/shard_map/ppermute | solution.py:210
  155.5 5.1 %collective-permute-start.11 = (f32[8]{0:T(128)S(1)}, f32[8]{0:T(128)S(1)}, u32[]{:S(2)}, u32[]{:S(2)}) collective-permute-start(f32[8]{0:T(128)S(1)} %slice_reduce_fusion), channel_id=1, source_target_pairs={{0,2},{1,3},{2,0},{3,1},{4,6},{5,7},{6,4},{7,5},{8,10},{9,11},{10,... | collective-permute-start | bytes 104 | tf_op jit(solution)/shard_map/ppermute | solution.py:210
  158.0 3.6 %collective-permute-start.12 = (f32[8]{0:T(128)S(1)}, f32[8]{0:T(128)S(1)}, u32[]{:S(2)}, u32[]{:S(2)}) collective-permute-start(f32[8]{0:T(128)S(1)} %slice_reduce_fusion), channel_id=1, source_target_pairs={{0,3},{1,0},{2,1},{3,2},{4,7},{5,4},{6,5},{7,6},{8,11},{9,8},{10,9... | collective-permute-start | bytes 104 | tf_op jit(solution)/shard_map/ppermute | solution.py:210

commit v11 on v10

--- a/solution.py
+++ b/solution.py
@@ -55,7 +55,7 @@
         tab_ref[0, pl.ds(r0, J_LO), m_width : 2 * m_width] = (sin_t * -weight).astype(jnp.bfloat16)
         return carry
 
-    lax.fori_loop(0, RPIX // J_LO, build, 0)
+    lax.fori_loop(0, RPIX // J_LO, build, 0, unroll=2)
 
 
 def cycle_tables(cycle_len, m_width):
@@ -136,7 +136,7 @@
     )(lens, sky_map, projected_t, basis, tables)
 
 
-POWER_STEP = 4
+POWER_STEP = 8
 OUT_STEP = 1
 
 

time: 173 us -> 172 us (level)
  no operation moved by 1% of the time
where the time goes in v11:
time: 172 us; the launch traced here: 171 us
  waiting for transfers between devices  51.4 us (30%)
  Pallas kernels  51.4 us (30%)
  starting transfers between devices  29.7 us (17%)
  other arithmetic  22.9 us (13%)
  local copies, waits for them, and re-layouts  10.3 us (6%)
  matrix products  5.29 us (3%)
    all_to_all x1, waiting for transfers between devices, body(): moved = lax.all_to_all(sendbuf, ('blk', 'grp'), 0, 0, tiled=True)  40.2 us
    ppermute x13, starting transfers between devices, ring_sum(): lax.ppermute(v, axis, shift_perm(size, stride, total, k))  22.1 us
    pallas_call x1, Pallas kernels, cycle_fourier(): pl.pallas_call(fourier_kernel, grid=(n_cyc,), in_specs=[pl.BlockSpec((1,...  19.8 us
    pallas_call x1, Pallas kernels, cycle_tables(): pl.pallas_call(table_kernel, grid=(n_cyc,), in_specs=[pl.BlockSpec((1, n_...  15.4 us
    pallas_call x1, Pallas kernels, body(): pl.pallas_call(output_kernel, grid=(chan_dev // OUT_STEP,), in_specs=harm...  11.2 us
    ppermute x13, waiting for transfers between devices, ring_sum(): lax.ppermute(v, axis, shift_perm(size, stride, total, k))  11.2 us
    cos x2, other arithmetic, cos_sin_of_phase(): return (jnp.cos(angle), jnp.sin(angle))  8.81 us
    convert_element_type x1, other arithmetic, theta_table(): return (jnp.cos(angle) * weight[None, :]).astype(jnp.bfloat16)  7.96 us
  transfers between devices with their start and end apart: 14, of which 7 were waited for; matrix products, arithmetic and copies ran while one was open for 12% of the time, Pallas kernels for 9%

profile of v11, /device:TPU:0, one launch (start us, length us, event | category | flops | bytes accessed | tf_op | source)
XLA Modules:
  0.0 171.3 jit_solution(11771678752174395674)
XLA Ops:
  0.8 3.0 %convolution_convert_fusion = bf16[8192,16]{0,1:T(8,128)(2,1)S(1)} fusion(bf16[256,16]{0,1:T(8,128)(2,1)} %param.6, bf16[256,8192]{1,0:T(8,128)(2,1)} %sky_ref.1, pred[8192]{0:T(1024)(128)(4,1)S(1)} %bitcast.34), kind=kOutput, calls=%fused_computation | convolution fusion | flops 69337088 | bytes 4472832 | tf_op jit(solution)/shard_map/dot_general | solution.py:228
  6.3 7.0 %fusion.34 = (f32[4,16,1024]{2,1,0:T(8,128)S(1)}, f32[4,16,1024]{2,1,0:T(8,128)S(1)}, f32[4,16,1024]{2,1,0:T(8,128)S(1)}, f32[4,16,1024]{2,1,0:T(8,128)S(1)}) fusion(f32[4]{0:T(128)S(1)} %get-tuple-element.16, pred[4]{0:T(512)(128)(4,1)S(1)} %broadcast_compare_fusion, s32[4]{0:T(128)S(1)} %get-tuple-element.15, s32[16,1024]{1,0:T(8,128)S(1)} %iota_multiply_fusion, ...), kind=kLoop, calls=%fused_computation.53 | loop fusion | flops 1376256 | bytes 1114404 | tf_op jit(solution)/shard_map/cos | solution.py:16
  13.5 1.7 collective-permute-start.1
  15.2 2.7 %collective-permute-start.2 = (f32[16,272]{0,1:T(8,128)S(1)}, f32[16,272]{0,1:T(8,128)S(1)}, u32[]{:S(2)}, u32[]{:S(2)}) collective-permute-start(f32[16,272]{0,1:T(8,128)S(1)} %add.184), channel_id=1, source_target_pairs={{0,16},{4,20},{8,24},{12,28},{16,0},{20,4},{24,8},{28,12},{32,48},... | collective-permute-start | bytes 52232 | tf_op jit(solution)/shard_map/ppermute | solution.py:210
  17.9 1.4 collective-permute-start.3
  19.3 1.8 %fusion.38 = (f32[4,8,1024]{2,1,0:T(8,128)S(1)}, f32[4,8,1024]{2,1,0:T(8,128)S(1)}) fusion(f32[4]{0:T(128)S(1)} %get-tuple-element.16, pred[4]{0:T(512)(128)(4,1)S(1)} %broadcast_compare_fusion, s32[4]{0:T(128)S(1)} %get-tuple-element.15, s32[4,8]{1,0:T(4,128)S(1)} %remainder_select_fusion.1), kind=kLoop, calls=%fused_computation.58 | loop fusion | flops 360448 | bytes 262308 | tf_op jit(solution)/shard_map/cos | solution.py:16
  21.2 3.7 %collective-permute-done.2 = f32[16,272]{0,1:T(8,128)S(1)} collective-permute-done((f32[16,272]{0,1:T(8,128)S(1)}, f32[16,272]{0,1:T(8,128)S(1)}, u32[]{:S(2)}, u32[]{:S(2)}) %collective-permute-start.2) | collective-permute-done | bytes 17440 | tf_op jit(solution)/shard_map/ppermute | solution.py:210
  24.9 1.6 collective-permute-start.4
  26.6 2.9 %collective-permute-start.5 = (f32[16,272]{0,1:T(8,128)S(1)}, f32[16,272]{0,1:T(8,128)S(1)}, u32[]{:S(2)}, u32[]{:S(2)}) collective-permute-start(f32[16,272]{0,1:T(8,128)S(1)} %add_add_fusion.2), channel_id=1, source_target_pairs={{0,64},{4,68},{8,72},{12,76},{16,80},{20,84},{24,88},{28,92},{32,9... | collective-permute-start | bytes 52232 | tf_op jit(solution)/shard_map/ppermute | solution.py:210
  31.6 4.0 %collective-permute-done.5 = f32[16,272]{0,1:T(8,128)S(1)} collective-permute-done((f32[16,272]{0,1:T(8,128)S(1)}, f32[16,272]{0,1:T(8,128)S(1)}, u32[]{:S(2)}, u32[]{:S(2)}) %collective-permute-start.5) | collective-permute-done | bytes 17440 | tf_op jit(solution)/shard_map/ppermute | solution.py:210
  35.7 2.0 %collective-permute-start.7 = (f32[16,272]{0,1:T(8,128)S(1)}, f32[16,272]{0,1:T(8,128)S(1)}, u32[]{:S(2)}, u32[]{:S(2)}) collective-permute-start(f32[16,272]{0,1:T(8,128)S(1)} %add_add_fusion.1), channel_id=1, source_target_pairs={{0,1},{1,2},{2,3},{3,0},{4,5},{5,6},{6,7},{7,4},{8,9},{9,10},{10,1... | collective-permute-start | bytes 52232 | tf_op jit(solution)/shard_map/ppermute | solution.py:210
  37.7 3.6 %collective-permute-start.8 = (f32[16,272]{0,1:T(8,128)S(1)}, f32[16,272]{0,1:T(8,128)S(1)}, u32[]{:S(2)}, u32[]{:S(2)}) collective-permute-start(f32[16,272]{0,1:T(8,128)S(1)} %add_add_fusion.1), channel_id=1, source_target_pairs={{0,2},{1,3},{2,0},{3,1},{4,6},{5,7},{6,4},{7,5},{8,10},{9,11},{10,... | collective-permute-start | bytes 52232 | tf_op jit(solution)/shard_map/ppermute | solution.py:210
  42.4 15.4 %shard_map.55.tab_ref = bf16[4,2048,2048]{2,1,0:T(8,128)(2,1)} custom-call(f32[4,16,1024]{2,1,0:T(8,128)S(1)} %get-tuple-element.13.ca_ref, f32[4,16,1024]{2,1,0:T(8,128)S(1)} %get-tuple-element.14.sa_ref, f32[4,128,1024]{2,1,0:T(8,128)S(1)} %bitcast.31, f32[4,128,1024]{2,1,0:T(8,128)S(1)} %bitcast.30, f32[4,1,128]{2,1,0:T(1,128)S(1)} %broadcast_in_dim.26.inv_ref, ...), custom_call_target="tpu_custom_call" | custom-call | tf_op jit(solution)/shard_map/pallas_call | solution.py:67
  57.9 1.5 cholesky.16
  62.6 19.8 %shard_map.56 = bf16[128,4,8,512]{3,2,1,0:T(8,128)(2,1)S(1)} custom-call(s32[4,1,128]{2,1,0:T(1,128)S(1)} %broadcast_in_dim.23.len_ref, bf16[256,8192]{1,0:T(8,128)(2,1)} %sky_ref.1, f32[256,16]{1,0:T(8,128)S(1)} %fusion.27.proj_ref, f32[16,8192]{1,0:T(8,128)S(1)} %fusion.41.basis_ref, bf16[4,2048,2048]{2,1,0:T(8,128)(2,1)} %shard_map.55.tab_ref), custom_call_target="tpu_custom_call" | custom-call | tf_op jit(solution)/shard_map/pallas_call | solution.py:122
  82.4 2.0 %copy-done.2 = bf16[128,4,8,512]{3,2,1,0:T(8,128)(2,1)} copy-done((bf16[128,4,8,512]{3,2,1,0:T(8,128)(2,1)}, bf16[128,4,8,512]{3,2,1,0:T(8,128)(2,1)S(1)}, u32[]{:S(2)}) %copy-start.2) | copy-done | bytes 4194328
  84.5 7.6 %all-to-all-start = ((bf16[128,4,8,512]{3,2,1,0:T(8,128)(2,1)}), bf16[128,4,8,512]{3,2,1,0:T(8,128)(2,1)}, u32[]{:S(2)}, u32[]{:S(2)}) async-start(bf16[128,4,8,512]{3,2,1,0:T(8,128)(2,1)} %copy-done.2), calls=%async_computation | async-start | bytes 8388608 | tf_op jit(solution)/shard_map/all_to_all | solution.py:245
  92.2 2.7 %copy.21.prof_ref = f32[8,1024,1]{2,1,0:T(8,128)} copy(f32[8,1024,1]{1,0,2:T(8,128)S(1)} %convolution_bitcast_fusion) | data formatting | bytes 65536 | tf_op jit(solution)/shard_map/broadcast_in_dim | solution.py:255
  95.0 8.0 %fusion.6.theta_ref = bf16[1024,512]{1,0:T(8,128)(2,1)S(1)} fusion(f32[512]{0:T(512)S(1)} %sine_multiply_fusion, s32[512]{0:T(512)S(1)} %multiply_add_fusion.1), kind=kLoop, calls=%fused_computation.11 | loop fusion | flops 8388608 | bytes 1052672 | tf_op jit(solution)/shard_map/convert_element_type | solution.py:188
  103.0 40.2 %all-to-all-done = bf16[128,4,8,512]{3,2,1,0:T(8,128)(2,1)} async-done(((bf16[128,4,8,512]{3,2,1,0:T(8,128)(2,1)}), bf16[128,4,8,512]{3,2,1,0:T(8,128)(2,1)}, u32[]{:S(2)}, u32[]{:S(2)}) %all-to-all-start) | async-done | bytes 4194336 | tf_op jit(solution)/shard_map/all_to_all | solution.py:245
  143.2 4.6 %copy.24 = bf16[64,8,8,512]{3,1,2,0:T(8,128)(2,1)S(1)} copy(bf16[64,8,8,512]{3,2,1,0:T(8,128)(2,1)} %bitcast.10) | data formatting | bytes 8388608
  147.8 5.1 %shard_map.57 = f32[8,1,128]{2,1,0:T(1,128)S(1)} custom-call(bf16[1024,512]{1,0:T(8,128)(2,1)S(1)} %fusion.6.theta_ref, bf16[512,4096]{1,0:T(8,128)(2,1)S(1)} %bitcast.28, f32[8,1024,1]{2,1,0:T(8,128)S(1)} %copy-done.1, f32[1,512]{1,0:T(1,128)S(1)} %bitcast.32), custom_call_target="tpu_custom_call" | custom-call | tf_op jit(solution)/shard_map/pallas_call | solution.py:258
  153.9 2.5 %collective-permute-start.11 = (f32[8]{0:T(128)S(1)}, f32[8]{0:T(128)S(1)}, u32[]{:S(2)}, u32[]{:S(2)}) collective-permute-start(f32[8]{0:T(128)S(1)} %slice_reduce_fusion), channel_id=1, source_target_pairs={{0,2},{1,3},{2,0},{3,1},{4,6},{5,7},{6,4},{7,5},{8,10},{9,11},{10,... | collective-permute-start | bytes 104 | tf_op jit(solution)/shard_map/ppermute | solution.py:210
  160.1 11.2 %shard_map.58 = f32[1024,8,2,256]{3,2,1,0:T(2,128)} custom-call(bf16[1024,512]{1,0:T(8,128)(2,1)S(1)} %fusion.6.theta_ref, bf16[512,4096]{1,0:T(8,128)(2,1)S(1)} %bitcast.29, f32[8,1024,1]{2,1,0:T(8,128)S(1)} %copy-done.1, f32[1,512]{1,0:T(1,128)S(1)} %bitcast.33, f32[8,1,128]{2,1,0:T(1,128)S(1)} %broadcast_in_dim.30.scale_ref), custom_call_target="tpu_custom_call" | custom-call | tf_op jit(solution)/shard_map/pallas_call | solution.py:269
  (66 shorter events, 15.1 us)
Async XLA Ops:
  0.0 92.0 %copy-start = (f32[8,1024]{1,0:T(8,128)S(1)}, f32[8,1024]{1,0:T(8,128)}, u32[]{:S(2)}) copy-start(f32[8,1024]{1,0:T(8,128)} %param.8) | copy-start | bytes 98308
  0.8 3.5 %copy-start.3 = (bf16[256,8192]{1,0:T(8,128)(2,1)S(1)}, bf16[256,8192]{1,0:T(8,128)(2,1)}, u32[]{:S(2)}) copy-start(bf16[256,8192]{1,0:T(8,128)(2,1)} %sky_ref.1) | copy-start | bytes 12582916
  4.2 1.7 %copy-start.4 = (s32[4]{0:T(128)S(1)}, s32[4]{0:T(128)}, u32[]{:S(2)}) copy-start(s32[4]{0:T(128)} %param.7) | copy-start | bytes 52
  5.8 7.6 %collective-permute-start = (f32[16,272]{0,1:T(8,128)S(1)}, f32[16,272]{0,1:T(8,128)S(1)}, u32[]{:S(2)}, u32[]{:S(2)}) collective-permute-start(f32[16,272]{0,1:T(8,128)S(1)} %copy.17), channel_id=1, source_target_pairs={{0,4},{4,0},{8,12},{12,8},{16,20},{20,16},{24,28},{28,24},{32,36},... | collective-permute-start | bytes 52232 | tf_op jit(solution)/shard_map/ppermute | solution.py:210
  13.5 7.7 %collective-permute-start.1 = (f32[16,272]{0,1:T(8,128)S(1)}, f32[16,272]{0,1:T(8,128)S(1)}, u32[]{:S(2)}, u32[]{:S(2)}) collective-permute-start(f32[16,272]{0,1:T(8,128)S(1)} %add.184), channel_id=1, source_target_pairs={{0,8},{4,12},{8,16},{12,20},{16,24},{20,28},{24,0},{28,4},{32,40},... | collective-permute-start | bytes 52232 | tf_op jit(solution)/shard_map/ppermute | solution.py:210
  15.2 9.7 %collective-permute-start.2 = (f32[16,272]{0,1:T(8,128)S(1)}, f32[16,272]{0,1:T(8,128)S(1)}, u32[]{:S(2)}, u32[]{:S(2)}) collective-permute-start(f32[16,272]{0,1:T(8,128)S(1)} %add.184), channel_id=1, source_target_pairs={{0,16},{4,20},{8,24},{12,28},{16,0},{20,4},{24,8},{28,12},{32,48},... | collective-permute-start | bytes 52232 | tf_op jit(solution)/shard_map/ppermute | solution.py:210
  17.9 7.0 %collective-permute-start.3 = (f32[16,272]{0,1:T(8,128)S(1)}, f32[16,272]{0,1:T(8,128)S(1)}, u32[]{:S(2)}, u32[]{:S(2)}) collective-permute-start(f32[16,272]{0,1:T(8,128)S(1)} %add.184), channel_id=1, source_target_pairs={{0,24},{4,28},{8,0},{12,4},{16,8},{20,12},{24,16},{28,20},{32,56},... | collective-permute-start | bytes 52232 | tf_op jit(solution)/shard_map/ppermute | solution.py:210
  24.9 6.7 %collective-permute-start.4 = (f32[16,272]{0,1:T(8,128)S(1)}, f32[16,272]{0,1:T(8,128)S(1)}, u32[]{:S(2)}, u32[]{:S(2)}) collective-permute-start(f32[16,272]{0,1:T(8,128)S(1)} %add_add_fusion.2), channel_id=1, source_target_pairs={{0,32},{4,36},{8,40},{12,44},{16,48},{20,52},{24,56},{28,60},{32,6... | collective-permute-start | bytes 52232 | tf_op jit(solution)/shard_map/ppermute | solution.py:210
  26.6 9.1 %collective-permute-start.5 = (f32[16,272]{0,1:T(8,128)S(1)}, f32[16,272]{0,1:T(8,128)S(1)}, u32[]{:S(2)}, u32[]{:S(2)}) collective-permute-start(f32[16,272]{0,1:T(8,128)S(1)} %add_add_fusion.2), channel_id=1, source_target_pairs={{0,64},{4,68},{8,72},{12,76},{16,80},{20,84},{24,88},{28,92},{32,9... | collective-permute-start | bytes 52232 | tf_op jit(solution)/shard_map/ppermute | solution.py:210
  29.5 6.2 %collective-permute-start.6 = (f32[16,272]{0,1:T(8,128)S(1)}, f32[16,272]{0,1:T(8,128)S(1)}, u32[]{:S(2)}, u32[]{:S(2)}) collective-permute-start(f32[16,272]{0,1:T(8,128)S(1)} %add_add_fusion.2), channel_id=1, source_target_pairs={{0,96},{4,100},{8,104},{12,108},{16,112},{20,116},{24,120},{28,124... | collective-permute-start | bytes 52232 | tf_op jit(solution)/shard_map/ppermute | solution.py:210
  35.7 22.1 %collective-permute-start.7 = (f32[16,272]{0,1:T(8,128)S(1)}, f32[16,272]{0,1:T(8,128)S(1)}, u32[]{:S(2)}, u32[]{:S(2)}) collective-permute-start(f32[16,272]{0,1:T(8,128)S(1)} %add_add_fusion.1), channel_id=1, source_target_pairs={{0,1},{1,2},{2,3},{3,0},{4,5},{5,6},{6,7},{7,4},{8,9},{9,10},{10,1... | collective-permute-start | bytes 52232 | tf_op jit(solution)/shard_map/ppermute | solution.py:210
  37.7 20.1 %collective-permute-start.8 = (f32[16,272]{0,1:T(8,128)S(1)}, f32[16,272]{0,1:T(8,128)S(1)}, u32[]{:S(2)}, u32[]{:S(2)}) collective-permute-start(f32[16,272]{0,1:T(8,128)S(1)} %add_add_fusion.1), channel_id=1, source_target_pairs={{0,2},{1,3},{2,0},{3,1},{4,6},{5,7},{6,4},{7,5},{8,10},{9,11},{10,... | collective-permute-start | bytes 52232 | tf_op jit(solution)/shard_map/ppermute | solution.py:210
  41.2 16.5 %collective-permute-start.9 = (f32[16,272]{0,1:T(8,128)S(1)}, f32[16,272]{0,1:T(8,128)S(1)}, u32[]{:S(2)}, u32[]{:S(2)}) collective-permute-start(f32[16,272]{0,1:T(8,128)S(1)} %add_add_fusion.1), channel_id=1, source_target_pairs={{0,3},{1,0},{2,1},{3,2},{4,7},{5,4},{6,5},{7,6},{8,11},{9,8},{10,9... | collective-permute-start | bytes 52232 | tf_op jit(solution)/shard_map/ppermute | solution.py:210
  82.4 2.0 %copy-start.2 = (bf16[128,4,8,512]{3,2,1,0:T(8,128)(2,1)}, bf16[128,4,8,512]{3,2,1,0:T(8,128)(2,1)S(1)}, u32[]{:S(2)}) copy-start(bf16[128,4,8,512]{3,2,1,0:T(8,128)(2,1)S(1)} %shard_map.56) | copy-start | bytes 12582916
  84.5 7.6 %copy-start.5 = (s32[8]{0:T(128)S(1)}, s32[8]{0:T(128)}, u32[]{:S(2)}) copy-start(s32[8]{0:T(128)} %param.9) | copy-start | bytes 100
  84.5 58.7 %all-to-all-start = ((bf16[128,4,8,512]{3,2,1,0:T(8,128)(2,1)}), bf16[128,4,8,512]{3,2,1,0:T(8,128)(2,1)}, u32[]{:S(2)}, u32[]{:S(2)}) async-start(bf16[128,4,8,512]{3,2,1,0:T(8,128)(2,1)} %copy-done.2), calls=%async_computation | async-start | bytes 8388608 | tf_op jit(solution)/shard_map/all_to_all | solution.py:245
  143.2 4.6 %copy-start.1 = (f32[8,1024,1]{2,1,0:T(8,128)S(1)}, f32[8,1024,1]{2,1,0:T(8,128)}, u32[]{:S(2)}) copy-start(f32[8,1024,1]{2,1,0:T(8,128)} %copy.21.prof_ref) | copy-start | bytes 98308
  153.1 4.8 %collective-permute-start.10 = (f32[8]{0:T(128)S(1)}, f32[8]{0:T(128)S(1)}, u32[]{:S(2)}, u32[]{:S(2)}) collective-permute-start(f32[8]{0:T(128)S(1)} %slice_reduce_fusion), channel_id=1, source_target_pairs={{0,1},{1,2},{2,3},{3,0},{4,5},{5,6},{6,7},{7,4},{8,9},{9,10},{10,1... | collective-permute-start | bytes 104 | tf_op jit(solution)/shard_map/ppermute | solution.py:210
  153.9 5.1 %collective-permute-start.11 = (f32[8]{0:T(128)S(1)}, f32[8]{0:T(128)S(1)}, u32[]{:S(2)}, u32[]{:S(2)}) collective-permute-start(f32[8]{0:T(128)S(1)} %slice_reduce_fusion), channel_id=1, source_target_pairs={{0,2},{1,3},{2,0},{3,1},{4,6},{5,7},{6,4},{7,5},{8,10},{9,11},{10,... | collective-permute-start | bytes 104 | tf_op jit(solution)/shard_map/ppermute | solution.py:210
  156.5 3.6 %collective-permute-start.12 = (f32[8]{0:T(128)S(1)}, f32[8]{0:T(128)S(1)}, u32[]{:S(2)}, u32[]{:S(2)}) collective-permute-start(f32[8]{0:T(128)S(1)} %slice_reduce_fusion), channel_id=1, source_target_pairs={{0,3},{1,0},{2,1},{3,2},{4,7},{5,4},{6,5},{7,6},{8,11},{9,8},{10,9... | collective-permute-start | bytes 104 | tf_op jit(solution)/shard_map/ppermute | solution.py:210

commit v12 on v11

--- a/solution.py
+++ b/solution.py
@@ -55,7 +55,7 @@
         tab_ref[0, pl.ds(r0, J_LO), m_width : 2 * m_width] = (sin_t * -weight).astype(jnp.bfloat16)
         return carry
 
-    lax.fori_loop(0, RPIX // J_LO, build, 0, unroll=2)
+    lax.fori_loop(0, RPIX // J_LO, build, 0, unroll=4)
 
 
 def cycle_tables(cycle_len, m_width):

time: 172 us -> 171 us (level)
  no operation moved by 1% of the time
where the time goes in v12:
time: 171 us
  waiting for transfers between devices  51.4 us (30%)
  Pallas kernels  51 us (30%)
  starting transfers between devices  29.6 us (17%)
  other arithmetic  22.9 us (13%)
  local copies, waits for them, and re-layouts  10.3 us (6%)
  matrix products  5.3 us (3%)
    all_to_all x1, waiting for transfers between devices, body(): moved = lax.all_to_all(sendbuf, ('blk', 'grp'), 0, 0, tiled=True)  40.2 us
    ppermute x13, starting transfers between devices, ring_sum(): lax.ppermute(v, axis, shift_perm(size, stride, total, k))  22.1 us
    pallas_call x1, Pallas kernels, cycle_fourier(): pl.pallas_call(fourier_kernel, grid=(n_cyc,), in_specs=[pl.BlockSpec((1,...  19.8 us
    pallas_call x1, Pallas kernels, cycle_tables(): pl.pallas_call(table_kernel, grid=(n_cyc,), in_specs=[pl.BlockSpec((1, n_...  14.9 us
    ppermute x13, waiting for transfers between devices, ring_sum(): lax.ppermute(v, axis, shift_perm(size, stride, total, k))  11.2 us
    pallas_call x1, Pallas kernels, body(): pl.pallas_call(output_kernel, grid=(chan_dev // OUT_STEP,), in_specs=harm...  11.2 us
    cos x2, other arithmetic, cos_sin_of_phase(): return (jnp.cos(angle), jnp.sin(angle))  8.81 us
    convert_element_type x1, other arithmetic, theta_table(): return (jnp.cos(angle) * weight[None, :]).astype(jnp.bfloat16)  7.96 us
  transfers between devices with their start and end apart: 14, of which 7 were waited for; matrix products, arithmetic and copies ran while one was open for 12% of the time, Pallas kernels for 9%

profile of v12, /device:TPU:0, one launch (start us, length us, event | category | flops | bytes accessed | tf_op | source)
XLA Modules:
  0.0 170.8 jit_solution(14157422873829986411)
XLA Ops:
  0.8 3.0 %convolution_convert_fusion = bf16[8192,16]{0,1:T(8,128)(2,1)S(1)} fusion(bf16[256,16]{0,1:T(8,128)(2,1)} %param.6, bf16[256,8192]{1,0:T(8,128)(2,1)} %sky_ref.1, pred[8192]{0:T(1024)(128)(4,1)S(1)} %bitcast.34), kind=kOutput, calls=%fused_computation | convolution fusion | flops 69337088 | bytes 4472832 | tf_op jit(solution)/shard_map/dot_general | solution.py:228
  6.3 7.0 %fusion.34 = (f32[4,16,1024]{2,1,0:T(8,128)S(1)}, f32[4,16,1024]{2,1,0:T(8,128)S(1)}, f32[4,16,1024]{2,1,0:T(8,128)S(1)}, f32[4,16,1024]{2,1,0:T(8,128)S(1)}) fusion(f32[4]{0:T(128)S(1)} %get-tuple-element.16, pred[4]{0:T(512)(128)(4,1)S(1)} %broadcast_compare_fusion, s32[4]{0:T(128)S(1)} %get-tuple-element.15, s32[16,1024]{1,0:T(8,128)S(1)} %iota_multiply_fusion, ...), kind=kLoop, calls=%fused_computation.53 | loop fusion | flops 1376256 | bytes 1114404 | tf_op jit(solution)/shard_map/cos | solution.py:16
  13.5 1.7 collective-permute-start.1
  15.2 2.7 %collective-permute-start.2 = (f32[16,272]{0,1:T(8,128)S(1)}, f32[16,272]{0,1:T(8,128)S(1)}, u32[]{:S(2)}, u32[]{:S(2)}) collective-permute-start(f32[16,272]{0,1:T(8,128)S(1)} %add.184), channel_id=1, source_target_pairs={{0,16},{4,20},{8,24},{12,28},{16,0},{20,4},{24,8},{28,12},{32,48},... | collective-permute-start | bytes 52232 | tf_op jit(solution)/shard_map/ppermute | solution.py:210
  17.9 1.4 collective-permute-start.3
  19.3 1.8 %fusion.38 = (f32[4,8,1024]{2,1,0:T(8,128)S(1)}, f32[4,8,1024]{2,1,0:T(8,128)S(1)}) fusion(f32[4]{0:T(128)S(1)} %get-tuple-element.16, pred[4]{0:T(512)(128)(4,1)S(1)} %broadcast_compare_fusion, s32[4]{0:T(128)S(1)} %get-tuple-element.15, s32[4,8]{1,0:T(4,128)S(1)} %remainder_select_fusion.1), kind=kLoop, calls=%fused_computation.58 | loop fusion | flops 360448 | bytes 262308 | tf_op jit(solution)/shard_map/cos | solution.py:16
  21.2 3.7 %collective-permute-done.2 = f32[16,272]{0,1:T(8,128)S(1)} collective-permute-done((f32[16,272]{0,1:T(8,128)S(1)}, f32[16,272]{0,1:T(8,128)S(1)}, u32[]{:S(2)}, u32[]{:S(2)}) %collective-permute-start.2) | collective-permute-done | bytes 17440 | tf_op jit(solution)/shard_map/ppermute | solution.py:210
  24.9 1.6 collective-permute-start.4
  26.6 2.9 %collective-permute-start.5 = (f32[16,272]{0,1:T(8,128)S(1)}, f32[16,272]{0,1:T(8,128)S(1)}, u32[]{:S(2)}, u32[]{:S(2)}) collective-permute-start(f32[16,272]{0,1:T(8,128)S(1)} %add_add_fusion.2), channel_id=1, source_target_pairs={{0,64},{4,68},{8,72},{12,76},{16,80},{20,84},{24,88},{28,92},{32,9... | collective-permute-start | bytes 52232 | tf_op jit(solution)/shard_map/ppermute | solution.py:210
  31.6 4.0 %collective-permute-done.5 = f32[16,272]{0,1:T(8,128)S(1)} collective-permute-done((f32[16,272]{0,1:T(8,128)S(1)}, f32[16,272]{0,1:T(8,128)S(1)}, u32[]{:S(2)}, u32[]{:S(2)}) %collective-permute-start.5) | collective-permute-done | bytes 17440 | tf_op jit(solution)/shard_map/ppermute | solution.py:210
  35.7 2.0 %collective-permute-start.7 = (f32[16,272]{0,1:T(8,128)S(1)}, f32[16,272]{0,1:T(8,128)S(1)}, u32[]{:S(2)}, u32[]{:S(2)}) collective-permute-start(f32[16,272]{0,1:T(8,128)S(1)} %add_add_fusion.1), channel_id=1, source_target_pairs={{0,1},{1,2},{2,3},{3,0},{4,5},{5,6},{6,7},{7,4},{8,9},{9,10},{10,1... | collective-permute-start | bytes 52232 | tf_op jit(solution)/shard_map/ppermute | solution.py:210
  37.7 3.6 %collective-permute-start.8 = (f32[16,272]{0,1:T(8,128)S(1)}, f32[16,272]{0,1:T(8,128)S(1)}, u32[]{:S(2)}, u32[]{:S(2)}) collective-permute-start(f32[16,272]{0,1:T(8,128)S(1)} %add_add_fusion.1), channel_id=1, source_target_pairs={{0,2},{1,3},{2,0},{3,1},{4,6},{5,7},{6,4},{7,5},{8,10},{9,11},{10,... | collective-permute-start | bytes 52232 | tf_op jit(solution)/shard_map/ppermute | solution.py:210
  42.4 14.9 %shard_map.55.tab_ref = bf16[4,2048,2048]{2,1,0:T(8,128)(2,1)} custom-call(f32[4,16,1024]{2,1,0:T(8,128)S(1)} %get-tuple-element.13.ca_ref, f32[4,16,1024]{2,1,0:T(8,128)S(1)} %get-tuple-element.14.sa_ref, f32[4,128,1024]{2,1,0:T(8,128)S(1)} %bitcast.31, f32[4,128,1024]{2,1,0:T(8,128)S(1)} %bitcast.30, f32[4,1,128]{2,1,0:T(1,128)S(1)} %broadcast_in_dim.26.inv_ref, ...), custom_call_target="tpu_custom_call" | custom-call | tf_op jit(solution)/shard_map/pallas_call | solution.py:67
  57.4 1.5 cholesky.16
  62.1 19.8 %shard_map.56 = bf16[128,4,8,512]{3,2,1,0:T(8,128)(2,1)S(1)} custom-call(s32[4,1,128]{2,1,0:T(1,128)S(1)} %broadcast_in_dim.23.len_ref, bf16[256,8192]{1,0:T(8,128)(2,1)} %sky_ref.1, f32[256,16]{1,0:T(8,128)S(1)} %fusion.27.proj_ref, f32[16,8192]{1,0:T(8,128)S(1)} %fusion.41.basis_ref, bf16[4,2048,2048]{2,1,0:T(8,128)(2,1)} %shard_map.55.tab_ref), custom_call_target="tpu_custom_call" | custom-call | tf_op jit(solution)/shard_map/pallas_call | solution.py:122
  82.0 2.0 %copy-done.2 = bf16[128,4,8,512]{3,2,1,0:T(8,128)(2,1)} copy-done((bf16[128,4,8,512]{3,2,1,0:T(8,128)(2,1)}, bf16[128,4,8,512]{3,2,1,0:T(8,128)(2,1)S(1)}, u32[]{:S(2)}) %copy-start.2) | copy-done | bytes 4194328
  84.0 7.5 %all-to-all-start = ((bf16[128,4,8,512]{3,2,1,0:T(8,128)(2,1)}), bf16[128,4,8,512]{3,2,1,0:T(8,128)(2,1)}, u32[]{:S(2)}, u32[]{:S(2)}) async-start(bf16[128,4,8,512]{3,2,1,0:T(8,128)(2,1)} %copy-done.2), calls=%async_computation | async-start | bytes 8388608 | tf_op jit(solution)/shard_map/all_to_all | solution.py:245
  91.8 2.7 %copy.21.prof_ref = f32[8,1024,1]{2,1,0:T(8,128)} copy(f32[8,1024,1]{1,0,2:T(8,128)S(1)} %convolution_bitcast_fusion) | data formatting | bytes 65536 | tf_op jit(solution)/shard_map/broadcast_in_dim | solution.py:255
  94.5 8.0 %fusion.6.theta_ref = bf16[1024,512]{1,0:T(8,128)(2,1)S(1)} fusion(f32[512]{0:T(512)S(1)} %sine_multiply_fusion, s32[512]{0:T(512)S(1)} %multiply_add_fusion.1), kind=kLoop, calls=%fused_computation.11 | loop fusion | flops 8388608 | bytes 1052672 | tf_op jit(solution)/shard_map/convert_element_type | solution.py:188
  102.5 40.2 %all-to-all-done = bf16[128,4,8,512]{3,2,1,0:T(8,128)(2,1)} async-done(((bf16[128,4,8,512]{3,2,1,0:T(8,128)(2,1)}), bf16[128,4,8,512]{3,2,1,0:T(8,128)(2,1)}, u32[]{:S(2)}, u32[]{:S(2)}) %all-to-all-start) | async-done | bytes 4194336 | tf_op jit(solution)/shard_map/all_to_all | solution.py:245
  142.7 4.6 %copy.24 = bf16[64,8,8,512]{3,1,2,0:T(8,128)(2,1)S(1)} copy(bf16[64,8,8,512]{3,2,1,0:T(8,128)(2,1)} %bitcast.10) | data formatting | bytes 8388608
  147.3 5.1 %shard_map.57 = f32[8,1,128]{2,1,0:T(1,128)S(1)} custom-call(bf16[1024,512]{1,0:T(8,128)(2,1)S(1)} %fusion.6.theta_ref, bf16[512,4096]{1,0:T(8,128)(2,1)S(1)} %bitcast.28, f32[8,1024,1]{2,1,0:T(8,128)S(1)} %copy-done.1, f32[1,512]{1,0:T(1,128)S(1)} %bitcast.32), custom_call_target="tpu_custom_call" | custom-call | tf_op jit(solution)/shard_map/pallas_call | solution.py:258
  153.5 2.5 %collective-permute-start.11 = (f32[8]{0:T(128)S(1)}, f32[8]{0:T(128)S(1)}, u32[]{:S(2)}, u32[]{:S(2)}) collective-permute-start(f32[8]{0:T(128)S(1)} %slice_reduce_fusion), channel_id=1, source_target_pairs={{0,2},{1,3},{2,0},{3,1},{4,6},{5,7},{6,4},{7,5},{8,10},{9,11},{10,... | collective-permute-start | bytes 104 | tf_op jit(solution)/shard_map/ppermute | solution.py:210
  159.7 11.2 %shard_map.58 = f32[1024,8,2,256]{3,2,1,0:T(2,128)} custom-call(bf16[1024,512]{1,0:T(8,128)(2,1)S(1)} %fusion.6.theta_ref, bf16[512,4096]{1,0:T(8,128)(2,1)S(1)} %bitcast.29, f32[8,1024,1]{2,1,0:T(8,128)S(1)} %copy-done.1, f32[1,512]{1,0:T(1,128)S(1)} %bitcast.33, f32[8,1,128]{2,1,0:T(1,128)S(1)} %broadcast_in_dim.30.scale_ref), custom_call_target="tpu_custom_call" | custom-call | tf_op jit(solution)/shard_map/pallas_call | solution.py:269
  (66 shorter events, 15.1 us)
Async XLA Ops:
  0.0 91.6 %copy-start = (f32[8,1024]{1,0:T(8,128)S(1)}, f32[8,1024]{1,0:T(8,128)}, u32[]{:S(2)}) copy-start(f32[8,1024]{1,0:T(8,128)} %param.8) | copy-start | bytes 98308
  0.8 3.5 %copy-start.3 = (bf16[256,8192]{1,0:T(8,128)(2,1)S(1)}, bf16[256,8192]{1,0:T(8,128)(2,1)}, u32[]{:S(2)}) copy-start(bf16[256,8192]{1,0:T(8,128)(2,1)} %sky_ref.1) | copy-start | bytes 12582916
  4.2 1.7 %copy-start.4 = (s32[4]{0:T(128)S(1)}, s32[4]{0:T(128)}, u32[]{:S(2)}) copy-start(s32[4]{0:T(128)} %param.7) | copy-start | bytes 52
  5.8 7.6 %collective-permute-start = (f32[16,272]{0,1:T(8,128)S(1)}, f32[16,272]{0,1:T(8,128)S(1)}, u32[]{:S(2)}, u32[]{:S(2)}) collective-permute-start(f32[16,272]{0,1:T(8,128)S(1)} %copy.17), channel_id=1, source_target_pairs={{0,4},{4,0},{8,12},{12,8},{16,20},{20,16},{24,28},{28,24},{32,36},... | collective-permute-start | bytes 52232 | tf_op jit(solution)/shard_map/ppermute | solution.py:210
  13.5 7.7 %collective-permute-start.1 = (f32[16,272]{0,1:T(8,128)S(1)}, f32[16,272]{0,1:T(8,128)S(1)}, u32[]{:S(2)}, u32[]{:S(2)}) collective-permute-start(f32[16,272]{0,1:T(8,128)S(1)} %add.184), channel_id=1, source_target_pairs={{0,8},{4,12},{8,16},{12,20},{16,24},{20,28},{24,0},{28,4},{32,40},... | collective-permute-start | bytes 52232 | tf_op jit(solution)/shard_map/ppermute | solution.py:210
  15.2 9.7 %collective-permute-start.2 = (f32[16,272]{0,1:T(8,128)S(1)}, f32[16,272]{0,1:T(8,128)S(1)}, u32[]{:S(2)}, u32[]{:S(2)}) collective-permute-start(f32[16,272]{0,1:T(8,128)S(1)} %add.184), channel_id=1, source_target_pairs={{0,16},{4,20},{8,24},{12,28},{16,0},{20,4},{24,8},{28,12},{32,48},... | collective-permute-start | bytes 52232 | tf_op jit(solution)/shard_map/ppermute | solution.py:210
  17.9 7.0 %collective-permute-start.3 = (f32[16,272]{0,1:T(8,128)S(1)}, f32[16,272]{0,1:T(8,128)S(1)}, u32[]{:S(2)}, u32[]{:S(2)}) collective-permute-start(f32[16,272]{0,1:T(8,128)S(1)} %add.184), channel_id=1, source_target_pairs={{0,24},{4,28},{8,0},{12,4},{16,8},{20,12},{24,16},{28,20},{32,56},... | collective-permute-start | bytes 52232 | tf_op jit(solution)/shard_map/ppermute | solution.py:210
  24.9 6.7 %collective-permute-start.4 = (f32[16,272]{0,1:T(8,128)S(1)}, f32[16,272]{0,1:T(8,128)S(1)}, u32[]{:S(2)}, u32[]{:S(2)}) collective-permute-start(f32[16,272]{0,1:T(8,128)S(1)} %add_add_fusion.2), channel_id=1, source_target_pairs={{0,32},{4,36},{8,40},{12,44},{16,48},{20,52},{24,56},{28,60},{32,6... | collective-permute-start | bytes 52232 | tf_op jit(solution)/shard_map/ppermute | solution.py:210
  26.6 9.1 %collective-permute-start.5 = (f32[16,272]{0,1:T(8,128)S(1)}, f32[16,272]{0,1:T(8,128)S(1)}, u32[]{:S(2)}, u32[]{:S(2)}) collective-permute-start(f32[16,272]{0,1:T(8,128)S(1)} %add_add_fusion.2), channel_id=1, source_target_pairs={{0,64},{4,68},{8,72},{12,76},{16,80},{20,84},{24,88},{28,92},{32,9... | collective-permute-start | bytes 52232 | tf_op jit(solution)/shard_map/ppermute | solution.py:210
  29.5 6.2 %collective-permute-start.6 = (f32[16,272]{0,1:T(8,128)S(1)}, f32[16,272]{0,1:T(8,128)S(1)}, u32[]{:S(2)}, u32[]{:S(2)}) collective-permute-start(f32[16,272]{0,1:T(8,128)S(1)} %add_add_fusion.2), channel_id=1, source_target_pairs={{0,96},{4,100},{8,104},{12,108},{16,112},{20,116},{24,120},{28,124... | collective-permute-start | bytes 52232 | tf_op jit(solution)/shard_map/ppermute | solution.py:210
  35.7 21.6 %collective-permute-start.7 = (f32[16,272]{0,1:T(8,128)S(1)}, f32[16,272]{0,1:T(8,128)S(1)}, u32[]{:S(2)}, u32[]{:S(2)}) collective-permute-start(f32[16,272]{0,1:T(8,128)S(1)} %add_add_fusion.1), channel_id=1, source_target_pairs={{0,1},{1,2},{2,3},{3,0},{4,5},{5,6},{6,7},{7,4},{8,9},{9,10},{10,1... | collective-permute-start | bytes 52232 | tf_op jit(solution)/shard_map/ppermute | solution.py:210
  37.7 19.7 %collective-permute-start.8 = (f32[16,272]{0,1:T(8,128)S(1)}, f32[16,272]{0,1:T(8,128)S(1)}, u32[]{:S(2)}, u32[]{:S(2)}) collective-permute-start(f32[16,272]{0,1:T(8,128)S(1)} %add_add_fusion.1), channel_id=1, source_target_pairs={{0,2},{1,3},{2,0},{3,1},{4,6},{5,7},{6,4},{7,5},{8,10},{9,11},{10,... | collective-permute-start | bytes 52232 | tf_op jit(solution)/shard_map/ppermute | solution.py:210
  41.2 16.1 %collective-permute-start.9 = (f32[16,272]{0,1:T(8,128)S(1)}, f32[16,272]{0,1:T(8,128)S(1)}, u32[]{:S(2)}, u32[]{:S(2)}) collective-permute-start(f32[16,272]{0,1:T(8,128)S(1)} %add_add_fusion.1), channel_id=1, source_target_pairs={{0,3},{1,0},{2,1},{3,2},{4,7},{5,4},{6,5},{7,6},{8,11},{9,8},{10,9... | collective-permute-start | bytes 52232 | tf_op jit(solution)/shard_map/ppermute | solution.py:210
  82.0 2.0 %copy-start.2 = (bf16[128,4,8,512]{3,2,1,0:T(8,128)(2,1)}, bf16[128,4,8,512]{3,2,1,0:T(8,128)(2,1)S(1)}, u32[]{:S(2)}) copy-start(bf16[128,4,8,512]{3,2,1,0:T(8,128)(2,1)S(1)} %shard_map.56) | copy-start | bytes 12582916
  84.0 7.6 %copy-start.5 = (s32[8]{0:T(128)S(1)}, s32[8]{0:T(128)}, u32[]{:S(2)}) copy-start(s32[8]{0:T(128)} %param.9) | copy-start | bytes 100
  84.0 58.7 %all-to-all-start = ((bf16[128,4,8,512]{3,2,1,0:T(8,128)(2,1)}), bf16[128,4,8,512]{3,2,1,0:T(8,128)(2,1)}, u32[]{:S(2)}, u32[]{:S(2)}) async-start(bf16[128,4,8,512]{3,2,1,0:T(8,128)(2,1)} %copy-done.2), calls=%async_computation | async-start | bytes 8388608 | tf_op jit(solution)/shard_map/all_to_all | solution.py:245
  142.7 4.6 %copy-start.1 = (f32[8,1024,1]{2,1,0:T(8,128)S(1)}, f32[8,1024,1]{2,1,0:T(8,128)}, u32[]{:S(2)}) copy-start(f32[8,1024,1]{2,1,0:T(8,128)} %copy.21.prof_ref) | copy-start | bytes 98308
  152.6 4.8 %collective-permute-start.10 = (f32[8]{0:T(128)S(1)}, f32[8]{0:T(128)S(1)}, u32[]{:S(2)}, u32[]{:S(2)}) collective-permute-start(f32[8]{0:T(128)S(1)} %slice_reduce_fusion), channel_id=1, source_target_pairs={{0,1},{1,2},{2,3},{3,0},{4,5},{5,6},{6,7},{7,4},{8,9},{9,10},{10,1... | collective-permute-start | bytes 104 | tf_op jit(solution)/shard_map/ppermute | solution.py:210
  153.5 5.1 %collective-permute-start.11 = (f32[8]{0:T(128)S(1)}, f32[8]{0:T(128)S(1)}, u32[]{:S(2)}, u32[]{:S(2)}) collective-permute-start(f32[8]{0:T(128)S(1)} %slice_reduce_fusion), channel_id=1, source_target_pairs={{0,2},{1,3},{2,0},{3,1},{4,6},{5,7},{6,4},{7,5},{8,10},{9,11},{10,... | collective-permute-start | bytes 104 | tf_op jit(solution)/shard_map/ppermute | solution.py:210
  156.0 3.6 %collective-permute-start.12 = (f32[8]{0:T(128)S(1)}, f32[8]{0:T(128)S(1)}, u32[]{:S(2)}, u32[]{:S(2)}) collective-permute-start(f32[8]{0:T(128)S(1)} %slice_reduce_fusion), channel_id=1, source_target_pairs={{0,3},{1,0},{2,1},{3,2},{4,7},{5,4},{6,5},{7,6},{8,11},{9,8},{10,9... | collective-permute-start | bytes 104 | tf_op jit(solution)/shard_map/ppermute | solution.py:210
